TPU v7x, 1024 devices: a whole 4x8x16 slice. The times are simulated.
1024 devices in a mesh: tile: 64 (over y_lo, z), kern: 16 (over x, y_hi, core).
Axes of the slice: x: 4, y: 8 (y_hi: 2, y_lo: 4; y = y_hi * 4 + y_lo), z: 16, core: 2. Of those that a mesh axis runs over, the one named last changes fastest.
Arguments:
- mask: bfloat16 [64, 128, 128], P('tile'), may hold values from 0 to 1
- kernels: bfloat16 [2, 16, 65, 65], P(None, 'kern'), may hold values from -0.09375 to 0.09375
- weights: float32 [16], P('kern'), may hold values from 0.03 to 0.1
- target: bfloat16 [64, 128, 128], P('tile'), may hold values from 0 to 1
- neighbours: int32 [64, 8], P('tile'), may hold values from -1 to 63, as said below
Outputs:
- gradient: float32 [64, 128, 128], P('tile', 'kern')
- resist: float32 [64, 128, 128], P('tile', 'kern')
Inputs may be any that keep to these rules, and one draw needn't show every extreme that they name: `neighbours`: tile t lies alone in row t of a grid of 2 cells a row, in its last cell; an entry names the tile in the cell at that direction (north is the row before), or is -1 where that cell is empty or off the grid.
All inputs are finite; a program needn't handle non-finite values.
Results may differ from a plain program's by a relative error of at most 0.0017.
Values may be sent and summed in bfloat16 or wider, within the bound.
No kernel may reach another device: no remote copies, remote signals or barrier semaphores. Data moves between devices by JAX's collectives and lax.ppermute only.
A program may use at most 128 MiB of HBM per device.

v0:
```python
import jax
import jax.numpy as jnp
from jax import lax
from jax.sharding import PartitionSpec as P

steepness = 8.0
threshold = 0.5


def padded_2(shard, sides, width):
    for axis, dim in sides:
        devices, length = (lax.axis_size(axis), shard.shape[dim])
        up = [(i, (i + 1) % devices) for i in range(devices - 1)]
        down = [(j, i) for i, j in up]
        last = lax.slice_in_dim(shard, length - width, length, axis=dim)
        first = lax.slice_in_dim(shard, 0, width, axis=dim)
        before = lax.ppermute(last, axis, up)
        after = lax.ppermute(first, axis, down)
        shard = jnp.concatenate([before, shard, after], axis=dim)
    return shard


def select_rows(source, chosen):
    tile_count = source.shape[0]
    picked = jnp.take(source, chosen % tile_count, axis=0)
    present = (chosen >= 0).astype(source.dtype)
    return picked * present[:, None, None, None]


def assemble(own_tiles, north_rows, south_rows, neighbours):
    half_width = north_rows.shape[2]
    tile_side = own_tiles.shape[3]
    cut_at = tile_side - half_width

    def beside_all(source, column):
        return select_rows(source, neighbours[:, column])

    upper_band = jnp.concatenate(
        [
            beside_all(north_rows, 0)[..., cut_at:],
            beside_all(north_rows, 1),
            beside_all(north_rows, 2)[..., :half_width],
        ],
        axis=3,
    )
    middle_band = jnp.concatenate(
        [
            beside_all(own_tiles, 3)[..., cut_at:],
            own_tiles,
            beside_all(own_tiles, 4)[..., :half_width],
        ],
        axis=3,
    )
    lower_band = jnp.concatenate(
        [
            beside_all(south_rows, 5)[..., cut_at:],
            beside_all(south_rows, 6),
            beside_all(south_rows, 7)[..., :half_width],
        ],
        axis=3,
    )
    return jnp.concatenate([upper_band, middle_band, lower_band], axis=2)


def group_size(tap_count):
    for candidate in range(min(tap_count, 16), 0, -1):
        if tap_count % candidate == 0:
            return candidate
    return 1


def banded(taps, width_in, width_out):
    channel_count = taps.shape[0]
    tap_count = taps.shape[1]
    row_len = taps.shape[2]
    padded = jnp.pad(taps, ((0, 0), (0, 0), (0, width_in + 1 - row_len)))
    repeated = jnp.broadcast_to(
        padded[:, :, None, :], (channel_count, tap_count, width_out, width_in + 1)
    )
    flat = repeated.reshape(channel_count, tap_count, width_out * (width_in + 1))[
        :, :, : width_out * width_in
    ]
    band = flat.reshape(channel_count, tap_count, width_out, width_in)
    return band.transpose(1, 0, 2, 3)


def correlate_forward(images, band, rows_out):
    tap_count = band.shape[0]
    group = group_size(tap_count)
    total = None
    for first in range(0, tap_count, group):
        stacked = jnp.stack(
            [images[:, first + step : first + step + rows_out, :] for step in range(group)], axis=1
        )
        term = lax.dot_general(
            stacked,
            band[first : first + group],
            (((1, 3), (0, 3)), ((), ())),
            preferred_element_type=jnp.float32,
        )
        total = term if total is None else total + term
    return total.transpose(0, 2, 1, 3)


def correlate_adjoint(images, band, rows_out):
    tap_count = band.shape[0]
    group = group_size(tap_count)
    total = None
    for first in range(0, tap_count, group):
        stacked = jnp.stack(
            [images[:, :, first + step : first + step + rows_out, :] for step in range(group)],
            axis=1,
        )
        term = lax.dot_general(
            stacked,
            band[first : first + group],
            (((1, 2, 4), (0, 1, 3)), ((), ())),
            preferred_element_type=jnp.float32,
        )
        total = term if total is None else total + term
    return total


def shards(mask, kernels, weights, target, neighbours):
    tile_side = mask.shape[1]
    local_kernels = kernels.shape[1]
    tap_count = kernels.shape[2]
    half_width = (tap_count - 1) // 2
    kern_count = lax.axis_size("kern")
    kern_place = lax.axis_index("kern")
    share_rows = tile_side // kern_count
    width_in = tile_side + 2 * half_width
    strips = jnp.stack([mask[:, :half_width, :], mask[:, tile_side - half_width :, :]])
    framed = padded_2(strips, (("tile", 0),), 1)
    north_rows = framed[0]
    south_rows = framed[3]
    extended = assemble(mask[:, None], north_rows[:, None], south_rows[:, None], neighbours)[:, 0]
    taps = kernels.reshape(2 * local_kernels, tap_count, tap_count)
    forward_band = banded(taps, width_in, tile_side)
    fields = correlate_forward(extended, forward_band, tile_side)
    doubled = jnp.concatenate([weights, weights])
    partial_sum = jnp.sum(doubled[None, :, None, None] * fields * fields, axis=1)
    intensity = lax.psum(partial_sum, "kern")
    resist_full = jax.nn.sigmoid(steepness * (intensity - threshold))
    sensitivity = (
        2.0
        * (resist_full - target.astype(jnp.float32))
        * steepness
        * resist_full
        * (1.0 - resist_full)
    )
    resist = lax.dynamic_slice_in_dim(resist_full, kern_place * share_rows, share_rows, 1)
    scaled = (2.0 * doubled)[None, :, None, None] * sensitivity[:, None] * fields
    adjoint_source = scaled.astype(jnp.bfloat16)
    source_strips = jnp.stack(
        [adjoint_source[:, :, :half_width, :], adjoint_source[:, :, tile_side - half_width :, :]]
    )
    source_framed = padded_2(source_strips, (("tile", 0),), 1)
    source_ext = assemble(adjoint_source, source_framed[0], source_framed[3], neighbours)
    adjoint_band = banded(taps[:, ::-1, ::-1], width_in, tile_side)
    gradient_term = correlate_adjoint(source_ext, adjoint_band, tile_side)
    gradient = lax.psum_scatter(gradient_term, "kern", scatter_dimension=1, tiled=True)
    return (gradient, resist)


def solution(mesh):
    in_specs = (
        P("tile", None, None),
        P(None, "kern", None, None),
        P("kern"),
        P("tile", None, None),
        P("tile", None),
    )
    out_specs = (P("tile", "kern", None), P("tile", "kern", None))
    return jax.shard_map(shards, mesh=mesh, in_specs=in_specs, out_specs=out_specs, check_vma=False)
```

profile of v0, /device:TPU:9, one launch (start us, length us, event | category | flops | bytes accessed | tf_op | source)
XLA Modules:
  0.0 548.2 jit_solution(17897235404437502032)
XLA Ops:
  7.9 17.8 %collective-permute-start.1 = (bf16[1,1,32,128]{3,2,1,0:T(8,128)(2,1)S(1)}, bf16[1,1,32,128]{3,2,1,0:T(8,128)(2,1)S(1)}, u32[]{:S(2)}, u32[]{:S(2)}) collective-permute-start(bf16[1,1,32,128]{3,2,1,0:T(8,128)(2,1)S(1)} %get-tuple-element.150), channel_id=1, source_target_pairs={{16,0},{32,16},{48,32},{64,48},{80,64},{96,80},{112,96},{128,112},... | collective-permute-start | bytes 24584 | tf_op jit(solution)/shard_map/ppermute | solution.py:18
  25.8 1.9 collective-permute-start
  29.2 1.6 fusion.111
  32.2 0.9 rev.3
  34.0 3.9 broadcast_in_dim.96
  37.9 25.2 %reshape.434 = bf16[2,65,24704]{2,0,1:T(2,128)(2,1)} reshape(bf16[2,65,128,193]{3,2,0,1:T(8,128)(2,1)} %broadcast_in_dim.96) | data formatting | bytes 12846080 | tf_op jit(solution)/shard_map/reshape | solution.py:80
  63.1 6.8 %slice.827 = bf16[2,65,24576]{2,0,1:T(2,128)(2,1)} slice(bf16[2,65,24704]{2,0,1:T(2,128)(2,1)} %reshape.434), slice={[0:2], [0:65], [0:24576]} | slice | bytes 12779520 | tf_op jit(solution)/shard_map/slice | solution.py:80
  70.0 14.2 %reshape.435 = bf16[2,65,128,192]{3,2,0,1:T(8,128)(2,1)} reshape(bf16[2,65,24576]{2,0,1:T(2,128)(2,1)} %slice.827) | data formatting | bytes 12779520 | tf_op jit(solution)/shard_map/reshape | solution.py:83
  84.2 10.2 %copy.39 = bf16[2,65,128,192]{2,3,0,1:T(8,128)(2,1)} copy(bf16[2,65,128,192]{3,2,0,1:T(8,128)(2,1)} %reshape.435) | data formatting | bytes 12779520 | tf_op jit(solution)/shard_map/reshape | solution.py:83
  94.3 3.9 broadcast_in_dim.95
  98.2 25.2 %reshape.427 = bf16[2,65,24704]{2,0,1:T(2,128)(2,1)} reshape(bf16[2,65,128,193]{3,2,0,1:T(8,128)(2,1)} %broadcast_in_dim.95) | data formatting | bytes 12846080 | tf_op jit(solution)/shard_map/reshape | solution.py:80
  123.4 6.8 %slice.751 = bf16[2,65,24576]{2,0,1:T(2,128)(2,1)} slice(bf16[2,65,24704]{2,0,1:T(2,128)(2,1)} %reshape.427), slice={[0:2], [0:65], [0:24576]} | slice | bytes 12779520 | tf_op jit(solution)/shard_map/slice | solution.py:80
  130.3 14.2 %reshape.428 = bf16[2,65,128,192]{3,2,0,1:T(8,128)(2,1)} reshape(bf16[2,65,24576]{2,0,1:T(2,128)(2,1)} %slice.751) | data formatting | bytes 12779520 | tf_op jit(solution)/shard_map/reshape | solution.py:83
  144.5 10.3 %copy.37 = bf16[2,65,128,192]{2,3,1,0:T(8,128)(2,1)} copy(bf16[2,65,128,192]{3,2,0,1:T(8,128)(2,1)} %reshape.428) | data formatting | bytes 12779520 | tf_op jit(solution)/shard_map/reshape | solution.py:83
  158.8 1.3 dynamic-slice
  166.5 1.2 fusion.110
  167.9 174.6 %all-reduce.6.cloned.1.call-done = f32[1,128,128]{1,2,0:T(8,128)} async-done(((f32[1,128,128]{1,2,0:T(8,128)}), f32[1,128,128]{1,2,0:T(8,128)}) %all-reduce.6.cloned.1.call-update) | async-done | bytes 65552 | tf_op jit(solution)/shard_map/psum | solution.py:143
  342.5 0.9 add_divide_fusion
  343.5 7.9 %collective-permute-start.3 = (bf16[1,1,2,32,128]{3,4,2,1,0:T(8,128)(2,1)S(1)}, bf16[1,1,2,32,128]{3,4,2,1,0:T(8,128)(2,1)S(1)}, u32[]{:S(2)}, u32[]{:S(2)}) collective-permute-start(bf16[1,1,2,32,128]{3,4,2,1,0:T(8,128)(2,1)S(1)} %get-tuple-element.142), channel_id=1, source_target_pairs={{16,0},{32,16},{48,32},{64,48},{80,64},{96,80},{112,96},{128,112},... | collective-permute-start | bytes 49160 | tf_op jit(solution)/shard_map/ppermute | solution.py:18
  351.5 2.1 collective-permute-start.2
  353.6 5.0 collective-permute-done.2
  365.2 1.1 fusion.85
  367.1 173.0 %all-reduce.8.cloned.1.call-done = f32[1,128,128]{2,1,0:T(8,128)} async-done(((f32[1,128,128]{2,1,0:T(8,128)}), f32[1,128,128]{2,1,0:T(8,128)}) %all-reduce.8.cloned.1.call-update) | async-done | bytes 65552
  540.1 1.3 constant_dynamic-slice_fusion
  (92 shorter events, 15.9 us)
Async XLA Ops:
  7.2 335.3 %all-reduce.6.cloned.1.call-start = ((), (), s32[]{:S(2)}) async-start(), calls=%async_computation | async-start | bytes 131072 | tf_op jit(solution)/shard_map/psum | solution.py:143
  7.9 152.7 %collective-permute-start.1 = (bf16[1,1,32,128]{3,2,1,0:T(8,128)(2,1)S(1)}, bf16[1,1,32,128]{3,2,1,0:T(8,128)(2,1)S(1)}, u32[]{:S(2)}, u32[]{:S(2)}) collective-permute-start(bf16[1,1,32,128]{3,2,1,0:T(8,128)(2,1)S(1)} %get-tuple-element.150), channel_id=1, source_target_pairs={{16,0},{32,16},{48,32},{64,48},{80,64},{96,80},{112,96},{128,112},... | collective-permute-start | bytes 24584 | tf_op jit(solution)/shard_map/ppermute | solution.py:18
  25.8 135.2 %collective-permute-start = (bf16[1,1,32,128]{3,2,1,0:T(8,128)(2,1)S(1)}, bf16[1,1,32,128]{3,2,1,0:T(8,128)(2,1)S(1)}, u32[]{:S(2)}, u32[]{:S(2)}) collective-permute-start(bf16[1,1,32,128]{3,2,1,0:T(8,128)(2,1)S(1)} %get-tuple-element.149), channel_id=1, source_target_pairs={{0,16},{16,32},{32,48},{48,64},{64,80},{80,96},{96,112},{112,128},... | collective-permute-start | bytes 24584 | tf_op jit(solution)/shard_map/ppermute | solution.py:17
  144.5 14.2 %copy-start.1 = (bf16[1,128,128]{2,1,0:T(8,128)(2,1)S(1)}, bf16[1,128,128]{2,1,0:T(8,128)(2,1)}, u32[]{:S(2)}) copy-start(bf16[1,128,128]{2,1,0:T(8,128)(2,1)} %param.8) | copy-start | bytes 98308
  161.3 2.8 copy-start
  165.9 196.0 %slice-start = ((s8[6389760]{0:T(1024)(128)(4,1)}), s8[2195456]{0:T(1024)(128)(4,1)S(1)}, s32[]{:S(2)}) async-start(s8[6389760]{0:T(1024)(128)(4,1)} %bitcast.690), calls=%async_computation.2 | async-start | bytes 4390912
  167.7 372.4 %all-reduce.8.cloned.1.call-start = ((), (), s32[]{:S(2)}) async-start(), calls=%async_computation.1 | async-start | bytes 131072
  343.5 10.0 %collective-permute-start.3 = (bf16[1,1,2,32,128]{3,4,2,1,0:T(8,128)(2,1)S(1)}, bf16[1,1,2,32,128]{3,4,2,1,0:T(8,128)(2,1)S(1)}, u32[]{:S(2)}, u32[]{:S(2)}) collective-permute-start(bf16[1,1,2,32,128]{3,4,2,1,0:T(8,128)(2,1)S(1)} %get-tuple-element.142), channel_id=1, source_target_pairs={{16,0},{32,16},{48,32},{64,48},{80,64},{96,80},{112,96},{128,112},... | collective-permute-start | bytes 49160 | tf_op jit(solution)/shard_map/ppermute | solution.py:18
  351.5 7.1 %collective-permute-start.2 = (bf16[1,1,2,32,128]{3,4,2,1,0:T(8,128)(2,1)S(1)}, bf16[1,1,2,32,128]{3,4,2,1,0:T(8,128)(2,1)S(1)}, u32[]{:S(2)}, u32[]{:S(2)}) collective-permute-start(bf16[1,1,2,32,128]{3,4,2,1,0:T(8,128)(2,1)S(1)} %get-tuple-element.143), channel_id=1, source_target_pairs={{0,16},{16,32},{32,48},{48,64},{64,80},{80,96},{96,112},{112,128},... | collective-permute-start | bytes 49160 | tf_op jit(solution)/shard_map/ppermute | solution.py:17
  358.9 3.1 slice-start.1
Sparse Core Ops, SparseCore 0:
  167.8 174.5 all-reduce.5
  366.5 173.5 all-reduce.7
where the time goes:
time: 553 us; the launch traced here: 548 us
  waiting for transfers between devices  353 us (64%)
  local copies, waits for them, and re-layouts  136 us (25%)
  starting transfers between devices  29.8 us (5%)
  between operations  21 us (4%)
  matrix products  6.78 us (1%)
    psum x1, waiting for transfers between devices, shards(): intensity = lax.psum(partial_sum, 'kern')  175 us
    unnamed x3, waiting for transfers between devices  173 us
    reshape x2, local copies, waits for them, and re-layouts, banded(): repeated.reshape(channel_count, tap_count, width_out * (width_in + 1))  50.5 us
    reshape x4, local copies, waits for them, and re-layouts, banded(): band = flat.reshape(channel_count, tap_count, width_out, width_in)  48.8 us
    ppermute x2, starting transfers between devices, padded_2(): after = lax.ppermute(first, axis, down)  25.7 us
    slice x2, local copies, waits for them, and re-layouts, banded(): repeated.reshape(channel_count, tap_count, width_out * (width_in + 1))  13.7 us
  transfers between devices with their start and end apart: 6, of which 3 were waited for; matrix products, arithmetic and copies ran while one was open for 23% of the time, Pallas kernels for 0%

commit v1 on v0

--- a/solution.py
+++ b/solution.py
@@ -70,18 +70,41 @@
 
 
 def banded(taps, width_in, width_out):
-    channel_count = taps.shape[0]
-    tap_count = taps.shape[1]
-    row_len = taps.shape[2]
-    padded = jnp.pad(taps, ((0, 0), (0, 0), (0, width_in + 1 - row_len)))
-    repeated = jnp.broadcast_to(
-        padded[:, :, None, :], (channel_count, tap_count, width_out, width_in + 1)
+    tap_count = taps.shape[2]
+    shape = (tap_count, width_out, width_in)
+    along = lax.broadcasted_iota(jnp.int32, shape, 0)
+    row = lax.broadcasted_iota(jnp.int32, shape, 1)
+    col = lax.broadcasted_iota(jnp.int32, shape, 2)
+    select = (col - row == along).astype(taps.dtype)
+    band = jnp.einsum(
+        "acb,bji->acji", taps.transpose(1, 0, 2), select, preferred_element_type=jnp.float32
     )
-    flat = repeated.reshape(channel_count, tap_count, width_out * (width_in + 1))[
-        :, :, : width_out * width_in
-    ]
-    band = flat.reshape(channel_count, tap_count, width_out, width_in)
-    return band.transpose(1, 0, 2, 3)
+    return band.astype(taps.dtype)
+
+
+def butterfly_sum(value, axis):
+    devices = lax.axis_size(axis)
+    bit = 1
+    while bit < devices:
+        pairs = [(i, i ^ bit) for i in range(devices)]
+        value = value + lax.ppermute(value, axis, pairs)
+        bit *= 2
+    return value
+
+
+def halving_scatter(value, axis, dim):
+    devices = lax.axis_size(axis)
+    place = lax.axis_index(axis)
+    bit = devices // 2
+    while bit >= 1:
+        half = value.shape[dim] // 2
+        upper = (place // bit) % 2
+        keep = lax.dynamic_slice_in_dim(value, upper * half, half, dim)
+        give = lax.dynamic_slice_in_dim(value, (1 - upper) * half, half, dim)
+        pairs = [(i, i ^ bit) for i in range(devices)]
+        value = keep + lax.ppermute(give, axis, pairs)
+        bit //= 2
+    return value
 
 
 def correlate_forward(images, band, rows_out):
@@ -140,7 +163,7 @@
     fields = correlate_forward(extended, forward_band, tile_side)
     doubled = jnp.concatenate([weights, weights])
     partial_sum = jnp.sum(doubled[None, :, None, None] * fields * fields, axis=1)
-    intensity = lax.psum(partial_sum, "kern")
+    intensity = butterfly_sum(partial_sum, "kern")
     resist_full = jax.nn.sigmoid(steepness * (intensity - threshold))
     sensitivity = (
         2.0
@@ -159,7 +182,7 @@
     source_ext = assemble(adjoint_source, source_framed[0], source_framed[3], neighbours)
     adjoint_band = banded(taps[:, ::-1, ::-1], width_in, tile_side)
     gradient_term = correlate_adjoint(source_ext, adjoint_band, tile_side)
-    gradient = lax.psum_scatter(gradient_term, "kern", scatter_dimension=1, tiled=True)
+    gradient = halving_scatter(gradient_term, "kern", 1)
     return (gradient, resist)
 
 

time: 553 us -> 123 us (0.22)
  the two profiles are of different devices: /device:TPU:9 before, /device:TPU:41 now
where the time goes in v1:
time: 123 us
  starting transfers between devices  60.4 us (49%)
  local copies, waits for them, and re-layouts  21.8 us (18%)
  waiting for transfers between devices  18.5 us (15%)
  matrix products  13.2 us (11%)
  between operations  7.21 us (6%)
  other arithmetic  1.57 us (1%)
    ppermute x2, starting transfers between devices, padded_2(): after = lax.ppermute(first, axis, down)  22.1 us
    ppermute x4, starting transfers between devices, halving_scatter(): value = keep + lax.ppermute(give, axis, pairs)  20 us
    ppermute x4, starting transfers between devices, butterfly_sum(): value = value + lax.ppermute(value, axis, pairs)  12.4 us
    unnamed x55, local copies, waits for them, and re-layouts  10.5 us
    ppermute x4, waiting for transfers between devices, halving_scatter(): value = keep + lax.ppermute(give, axis, pairs)  9.6 us
    ppermute x4, waiting for transfers between devices, butterfly_sum(): value = value + lax.ppermute(value, axis, pairs)  7.61 us
    ppermute x2, starting transfers between devices, padded_2(): before = lax.ppermute(last, axis, up)  5.91 us
    dot_general x2, matrix products, banded(): jnp.einsum('acb,bji->acji', taps.transpose(1, 0, 2), select, preferred_el...  4.76 us
  transfers between devices with their start and end apart: 12, of which 7 were waited for; matrix products, arithmetic and copies ran while one was open for 14% of the time, Pallas kernels for 0%

profile of v1, /device:TPU:41, one launch (start us, length us, event | category | flops | bytes accessed | tf_op | source)
XLA Modules:
  0.0 122.6 jit_solution(3634276809868066417)
XLA Ops:
  1.3 4.0 %collective-permute-start = (bf16[1,1,32,128]{3,2,1,0:T(8,128)(2,1)S(1)}, bf16[1,1,32,128]{3,2,1,0:T(8,128)(2,1)S(1)}, u32[]{:S(2)}, u32[]{:S(2)}) collective-permute-start(bf16[1,1,32,128]{3,2,1,0:T(8,128)(2,1)S(1)} %get-tuple-element.159), channel_id=1, source_target_pairs={{0,16},{16,32},{32,48},{48,64},{64,80},{80,96},{96,112},{112,128},... | collective-permute-start | bytes 24584 | tf_op jit(solution)/shard_map/ppermute | solution.py:17
  5.3 16.6 %collective-permute-start.1 = (bf16[1,1,32,128]{3,2,1,0:T(8,128)(2,1)S(1)}, bf16[1,1,32,128]{3,2,1,0:T(8,128)(2,1)S(1)}, u32[]{:S(2)}, u32[]{:S(2)}) collective-permute-start(bf16[1,1,32,128]{3,2,1,0:T(8,128)(2,1)S(1)} %get-tuple-element.160), channel_id=1, source_target_pairs={{16,0},{32,16},{48,32},{64,48},{80,64},{96,80},{112,96},{128,112},... | collective-permute-start | bytes 24584 | tf_op jit(solution)/shard_map/ppermute | solution.py:18
  22.0 0.9 copy.48
  22.9 1.6 %fusion.121 = (s32[1,1]{1,0:T(1,128)}, s32[1,1]{1,0:T(1,128)}, s32[1,1]{1,0:T(1,128)}, s32[1,1]{1,0:T(1,128)}, s32[1,1]{1,0:T(1,128)}, /*index=5*/s32[1,1]{1,0:T(1,128)}, s32[1,1]{1,0:T(1,128)}, s32[1,1]{1,0:T(1,128)}) fusion(s32[1,8]{1,0:T(1,128)} %param.9), kind=kLoop, calls=%fused_computation.363 | loop fusion | bytes 64 | tf_op jit(solution)/shard_map/slice | solution.py:36
  25.8 2.8 %convert_bitcast_fusion.1 = bf16[65,2,128,192]{2,0,1,3:T(8,128)(2,1)S(1)} fusion(bf16[65,2,65]{2,1,0:T(2,128)(2,1)} %bitcast.697), kind=kOutput, calls=%fused_computation.1 | convolution fusion | flops 421724160 | bytes 6406660 | tf_op jit(solution)/shard_map/acb,bji->acji/dot_general | solution.py:79
  28.5 4.0 %fusion.120 = (bf16[13,2,128,192]{2,0,1,3:T(8,128)(2,1)S(1)}, bf16[13,2,128,192]{2,0,1,3:T(8,128)(2,1)S(1)}, bf16[13,2,128,192]{2,0,1,3:T(8,128)(2,1)}, bf16[13,...) fusion(bf16[65,2,128,192]{2,0,1,3:T(8,128)(2,1)S(1)} %convert_bitcast_fusion.1), kind=kLoop, calls=%fused_computation.362 | loop fusion | bytes 12779520 | tf_op jit(solution)/shard_map/slice | solution.py:120
  45.6 2.9 %collective-permute-start.2 = (f32[1,128,128]{1,2,0:T(8,128)S(1)}, f32[1,128,128]{1,2,0:T(8,128)S(1)}, u32[]{:S(2)}, u32[]{:S(2)}) collective-permute-start(f32[1,128,128]{1,2,0:T(8,128)S(1)} %bitcast.700), channel_id=1, source_target_pairs={{0,1},{1,0},{2,3},{3,2},{4,5},{5,4},{6,7},{7,6},{8,9},{9,8},{10,11... | collective-permute-start | bytes 196616 | tf_op jit(solution)/shard_map/ppermute | solution.py:90
  49.3 2.1 %collective-permute-start.3 = (f32[1,128,128]{1,2,0:T(8,128)S(1)}, f32[1,128,128]{1,2,0:T(8,128)S(1)}, u32[]{:S(2)}, u32[]{:S(2)}) collective-permute-start(f32[1,128,128]{1,2,0:T(8,128)S(1)} %bitcast_add_fusion.1), channel_id=1, source_target_pairs={{0,2},{1,3},{2,0},{3,1},{4,6},{5,7},{6,4},{7,5},{8,10},{9,11},{10,... | collective-permute-start | bytes 196616 | tf_op jit(solution)/shard_map/ppermute | solution.py:90
  51.4 2.0 %convert_bitcast_fusion = bf16[65,2,128,192]{2,0,1,3:T(8,128)(2,1)S(1)} fusion(bf16[65,2,65]{2,1,0:T(2,128)(2,1)S(1)} %bitcast.699), kind=kOutput, calls=%fused_computation | convolution fusion | flops 421724160 | bytes 6406660 | tf_op jit(solution)/shard_map/acb,bji->acji/dot_general | solution.py:79
  53.4 4.9 %collective-permute-done.3 = f32[1,128,128]{1,2,0:T(8,128)S(1)} collective-permute-done((f32[1,128,128]{1,2,0:T(8,128)S(1)}, f32[1,128,128]{1,2,0:T(8,128)S(1)}, u32[]{:S(2)}, u32[]{:S(2)}) %collective-permute-start.3) | collective-permute-done | bytes 65568 | tf_op jit(solution)/shard_map/ppermute | solution.py:90
  58.3 3.1 %collective-permute-start.4 = (f32[1,128,128]{1,2,0:T(8,128)S(1)}, f32[1,128,128]{1,2,0:T(8,128)S(1)}, u32[]{:S(2)}, u32[]{:S(2)}) collective-permute-start(f32[1,128,128]{1,2,0:T(8,128)S(1)} %add.166), channel_id=1, source_target_pairs={{0,4},{1,5},{2,6},{3,7},{4,0},{5,1},{6,2},{7,3},{8,12},{9,13},{10,... | collective-permute-start | bytes 196616 | tf_op jit(solution)/shard_map/ppermute | solution.py:90
  61.4 4.0 %fusion.119 = (bf16[13,2,128,192]{2,0,1,3:T(8,128)(2,1)S(1)}, bf16[13,2,128,192]{2,0,1,3:T(8,128)(2,1)S(1)}, bf16[13,2,128,192]{2,0,1,3:T(8,128)(2,1)}, bf16[13,...) fusion(bf16[65,2,128,192]{2,0,1,3:T(8,128)(2,1)S(1)} %convert_bitcast_fusion), kind=kLoop, calls=%fused_computation.361 | loop fusion | bytes 12779520 | tf_op jit(solution)/shard_map/slice | solution.py:139
  65.6 4.4 %collective-permute-start.5 = (f32[1,128,128]{1,2,0:T(8,128)S(1)}, f32[1,128,128]{1,2,0:T(8,128)S(1)}, u32[]{:S(2)}, u32[]{:S(2)}) collective-permute-start(f32[1,128,128]{1,2,0:T(8,128)S(1)} %add.167), channel_id=1, source_target_pairs={{0,8},{1,9},{2,10},{3,11},{4,12},{5,13},{6,14},{7,15},{8,0},{9,1},... | collective-permute-start | bytes 196616 | tf_op jit(solution)/shard_map/ppermute | solution.py:90
  70.0 2.1 %collective-permute-done.5 = f32[1,128,128]{1,2,0:T(8,128)S(1)} collective-permute-done((f32[1,128,128]{1,2,0:T(8,128)S(1)}, f32[1,128,128]{1,2,0:T(8,128)S(1)}, u32[]{:S(2)}, u32[]{:S(2)}) %collective-permute-start.5) | collective-permute-done | bytes 65568 | tf_op jit(solution)/shard_map/ppermute | solution.py:90
  72.3 1.9 %collective-permute-start.6 = (bf16[1,1,2,32,128]{3,4,2,1,0:T(8,128)(2,1)S(1)}, bf16[1,1,2,32,128]{3,4,2,1,0:T(8,128)(2,1)S(1)}, u32[]{:S(2)}, u32[]{:S(2)}) collective-permute-start(bf16[1,1,2,32,128]{3,4,2,1,0:T(8,128)(2,1)S(1)} %get-tuple-element.153), channel_id=1, source_target_pairs={{0,16},{16,32},{32,48},{48,64},{64,80},{80,96},{96,112},{112,128},... | collective-permute-start | bytes 49160 | tf_op jit(solution)/shard_map/ppermute | solution.py:17
  74.3 5.5 %collective-permute-start.7 = (bf16[1,1,2,32,128]{3,4,2,1,0:T(8,128)(2,1)S(1)}, bf16[1,1,2,32,128]{3,4,2,1,0:T(8,128)(2,1)S(1)}, u32[]{:S(2)}, u32[]{:S(2)}) collective-permute-start(bf16[1,1,2,32,128]{3,4,2,1,0:T(8,128)(2,1)S(1)} %get-tuple-element.152), channel_id=1, source_target_pairs={{16,0},{32,16},{48,32},{64,48},{80,64},{96,80},{112,96},{128,112},... | collective-permute-start | bytes 49160 | tf_op jit(solution)/shard_map/ppermute | solution.py:18
  79.8 1.2 %collective-permute-done.7 = bf16[1,1,2,32,128]{3,4,2,1,0:T(8,128)(2,1)S(1)} collective-permute-done((bf16[1,1,2,32,128]{3,4,2,1,0:T(8,128)(2,1)S(1)}, bf16[1,1,2,32,128]{3,4,2,1,0:T(8,128)(2,1)S(1)}, u32[]{:S(2)}, u32[]{:S(2)}) %collective-permute-start.7) | collective-permute-done | bytes 16416 | tf_op jit(solution)/shard_map/ppermute | solution.py:18
  91.5 4.4 %collective-permute-start.8 = (f32[1,64,128]{2,1,0:T(8,128)S(1)}, f32[1,64,128]{2,1,0:T(8,128)S(1)}, u32[]{:S(2)}, u32[]{:S(2)}) collective-permute-start(f32[1,64,128]{2,1,0:T(8,128)S(1)} %dynamic-slice_bitcast_fusion), channel_id=1, source_target_pairs={{0,8},{1,9},{2,10},{3,11},{4,12},{5,13},{6,14},{7,15},{8,0},{9,1},... | collective-permute-start | bytes 98312 | tf_op jit(solution)/shard_map/ppermute | solution.py:105
  95.9 1.8 %collective-permute-done.8 = f32[1,64,128]{2,1,0:T(8,128)S(1)} collective-permute-done((f32[1,64,128]{2,1,0:T(8,128)S(1)}, f32[1,64,128]{2,1,0:T(8,128)S(1)}, u32[]{:S(2)}, u32[]{:S(2)}) %collective-permute-start.8) | collective-permute-done | bytes 32800 | tf_op jit(solution)/shard_map/ppermute | solution.py:105
  97.7 2.2 %collective-permute-start.9 = (f32[1,32,128]{2,1,0:T(8,128)S(1)}, f32[1,32,128]{2,1,0:T(8,128)S(1)}, u32[]{:S(2)}, u32[]{:S(2)}) collective-permute-start(f32[1,32,128]{2,1,0:T(8,128)S(1)} %constant_dynamic-slice_fusion.3), channel_id=1, source_target_pairs={{0,4},{1,5},{2,6},{3,7},{4,0},{5,1},{6,2},{7,3},{8,12},{9,13},{10,... | collective-permute-start | bytes 49160 | tf_op jit(solution)/shard_map/ppermute | solution.py:105
  99.9 2.3 %collective-permute-done.9 = f32[1,32,128]{2,1,0:T(8,128)S(1)} collective-permute-done((f32[1,32,128]{2,1,0:T(8,128)S(1)}, f32[1,32,128]{2,1,0:T(8,128)S(1)}, u32[]{:S(2)}, u32[]{:S(2)}) %collective-permute-start.9) | collective-permute-done | bytes 16416 | tf_op jit(solution)/shard_map/ppermute | solution.py:105
  102.2 2.7 %collective-permute-start.10 = (f32[1,16,128]{2,1,0:T(8,128)S(1)}, f32[1,16,128]{2,1,0:T(8,128)S(1)}, u32[]{:S(2)}, u32[]{:S(2)}) collective-permute-start(f32[1,16,128]{2,1,0:T(8,128)S(1)} %constant_dynamic-slice_fusion.2), channel_id=1, source_target_pairs={{0,2},{1,3},{2,0},{3,1},{4,6},{5,7},{6,4},{7,5},{8,10},{9,11},{10,... | collective-permute-start | bytes 24584 | tf_op jit(solution)/shard_map/ppermute | solution.py:105
  105.0 5.5 %collective-permute-done.10 = f32[1,16,128]{2,1,0:T(8,128)S(1)} collective-permute-done((f32[1,16,128]{2,1,0:T(8,128)S(1)}, f32[1,16,128]{2,1,0:T(8,128)S(1)}, u32[]{:S(2)}, u32[]{:S(2)}) %collective-permute-start.10) | collective-permute-done | bytes 8224 | tf_op jit(solution)/shard_map/ppermute | solution.py:105
  110.5 10.7 %collective-permute-start.11 = (f32[1,8,128]{2,1,0:T(8,128)S(1)}, f32[1,8,128]{2,1,0:T(8,128)S(1)}, u32[]{:S(2)}, u32[]{:S(2)}) collective-permute-start(f32[1,8,128]{2,1,0:T(8,128)S(1)} %constant_dynamic-slice_fusion.1), channel_id=1, source_target_pairs={{0,1},{1,0},{2,3},{3,2},{4,5},{5,4},{6,7},{7,6},{8,9},{9,8},{10,11... | collective-permute-start | bytes 12296 | tf_op jit(solution)/shard_map/ppermute | solution.py:105
  (110 shorter events, 22.1 us)
Async XLA Ops:
  1.3 35.7 %collective-permute-start = (bf16[1,1,32,128]{3,2,1,0:T(8,128)(2,1)S(1)}, bf16[1,1,32,128]{3,2,1,0:T(8,128)(2,1)S(1)}, u32[]{:S(2)}, u32[]{:S(2)}) collective-permute-start(bf16[1,1,32,128]{3,2,1,0:T(8,128)(2,1)S(1)} %get-tuple-element.159), channel_id=1, source_target_pairs={{0,16},{16,32},{32,48},{48,64},{64,80},{80,96},{96,112},{112,128},... | collective-permute-start | bytes 24584 | tf_op jit(solution)/shard_map/ppermute | solution.py:17
  5.3 32.0 %collective-permute-start.1 = (bf16[1,1,32,128]{3,2,1,0:T(8,128)(2,1)S(1)}, bf16[1,1,32,128]{3,2,1,0:T(8,128)(2,1)S(1)}, u32[]{:S(2)}, u32[]{:S(2)}) collective-permute-start(bf16[1,1,32,128]{3,2,1,0:T(8,128)(2,1)S(1)} %get-tuple-element.160), channel_id=1, source_target_pairs={{16,0},{32,16},{48,32},{64,48},{80,64},{96,80},{112,96},{128,112},... | collective-permute-start | bytes 24584 | tf_op jit(solution)/shard_map/ppermute | solution.py:18
  39.1 1.4 %copy-start.5 = (bf16[13,2,128,192]{2,0,1,3:T(8,128)(2,1)S(1)}, bf16[13,2,128,192]{2,0,1,3:T(8,128)(2,1)}, u32[]{:S(2)}) copy-start(bf16[13,2,128,192]{2,0,1,3:T(8,128)(2,1)} %get-tuple-element.17) | copy-start | bytes 3833860
  40.0 1.5 %copy-start.4 = (bf16[13,2,128,192]{2,0,1,3:T(8,128)(2,1)S(1)}, bf16[13,2,128,192]{2,0,1,3:T(8,128)(2,1)}, u32[]{:S(2)}) copy-start(bf16[13,2,128,192]{2,0,1,3:T(8,128)(2,1)} %get-tuple-element.16) | copy-start | bytes 3833860
  41.6 1.4 %copy-start.3 = (bf16[13,2,128,192]{2,0,1,3:T(8,128)(2,1)S(1)}, bf16[13,2,128,192]{2,0,1,3:T(8,128)(2,1)}, u32[]{:S(2)}) copy-start(bf16[13,2,128,192]{2,0,1,3:T(8,128)(2,1)} %get-tuple-element.15) | copy-start | bytes 3833860
  44.7 3.7 %copy-start.6 = (bf16[2,1,65,65]{3,0,2,1:T(2,128)(2,1)S(1)}, bf16[2,1,65,65]{3,0,2,1:T(2,128)(2,1)}, u32[]{:S(2)}) copy-start(bf16[2,1,65,65]{3,0,2,1:T(2,128)(2,1)} %param.6) | copy-start | bytes 50704
  45.6 3.8 %collective-permute-start.2 = (f32[1,128,128]{1,2,0:T(8,128)S(1)}, f32[1,128,128]{1,2,0:T(8,128)S(1)}, u32[]{:S(2)}, u32[]{:S(2)}) collective-permute-start(f32[1,128,128]{1,2,0:T(8,128)S(1)} %bitcast.700), channel_id=1, source_target_pairs={{0,1},{1,0},{2,3},{3,2},{4,5},{5,4},{6,7},{7,6},{8,9},{9,8},{10,11... | collective-permute-start | bytes 196616 | tf_op jit(solution)/shard_map/ppermute | solution.py:90
  49.3 9.0 %collective-permute-start.3 = (f32[1,128,128]{1,2,0:T(8,128)S(1)}, f32[1,128,128]{1,2,0:T(8,128)S(1)}, u32[]{:S(2)}, u32[]{:S(2)}) collective-permute-start(f32[1,128,128]{1,2,0:T(8,128)S(1)} %bitcast_add_fusion.1), channel_id=1, source_target_pairs={{0,2},{1,3},{2,0},{3,1},{4,6},{5,7},{6,4},{7,5},{8,10},{9,11},{10,... | collective-permute-start | bytes 196616 | tf_op jit(solution)/shard_map/ppermute | solution.py:90
  58.3 7.1 %copy-start.7 = (bf16[1,128,128]{2,1,0:T(8,128)(2,1)S(1)}, bf16[1,128,128]{2,1,0:T(8,128)(2,1)}, u32[]{:S(2)}) copy-start(bf16[1,128,128]{2,1,0:T(8,128)(2,1)} %param.8) | copy-start | bytes 98308
  58.3 7.2 %collective-permute-start.4 = (f32[1,128,128]{1,2,0:T(8,128)S(1)}, f32[1,128,128]{1,2,0:T(8,128)S(1)}, u32[]{:S(2)}, u32[]{:S(2)}) collective-permute-start(f32[1,128,128]{1,2,0:T(8,128)S(1)} %add.166), channel_id=1, source_target_pairs={{0,4},{1,5},{2,6},{3,7},{4,0},{5,1},{6,2},{7,3},{8,12},{9,13},{10,... | collective-permute-start | bytes 196616 | tf_op jit(solution)/shard_map/ppermute | solution.py:90
  65.6 6.5 %collective-permute-start.5 = (f32[1,128,128]{1,2,0:T(8,128)S(1)}, f32[1,128,128]{1,2,0:T(8,128)S(1)}, u32[]{:S(2)}, u32[]{:S(2)}) collective-permute-start(f32[1,128,128]{1,2,0:T(8,128)S(1)} %add.167), channel_id=1, source_target_pairs={{0,8},{1,9},{2,10},{3,11},{4,12},{5,13},{6,14},{7,15},{8,0},{9,1},... | collective-permute-start | bytes 196616 | tf_op jit(solution)/shard_map/ppermute | solution.py:90
  72.3 7.4 %collective-permute-start.6 = (bf16[1,1,2,32,128]{3,4,2,1,0:T(8,128)(2,1)S(1)}, bf16[1,1,2,32,128]{3,4,2,1,0:T(8,128)(2,1)S(1)}, u32[]{:S(2)}, u32[]{:S(2)}) collective-permute-start(bf16[1,1,2,32,128]{3,4,2,1,0:T(8,128)(2,1)S(1)} %get-tuple-element.153), channel_id=1, source_target_pairs={{0,16},{16,32},{32,48},{48,64},{64,80},{80,96},{96,112},{112,128},... | collective-permute-start | bytes 49160 | tf_op jit(solution)/shard_map/ppermute | solution.py:17
  74.3 6.8 %collective-permute-start.7 = (bf16[1,1,2,32,128]{3,4,2,1,0:T(8,128)(2,1)S(1)}, bf16[1,1,2,32,128]{3,4,2,1,0:T(8,128)(2,1)S(1)}, u32[]{:S(2)}, u32[]{:S(2)}) collective-permute-start(bf16[1,1,2,32,128]{3,4,2,1,0:T(8,128)(2,1)S(1)} %get-tuple-element.152), channel_id=1, source_target_pairs={{16,0},{32,16},{48,32},{64,48},{80,64},{96,80},{112,96},{128,112},... | collective-permute-start | bytes 49160 | tf_op jit(solution)/shard_map/ppermute | solution.py:18
  83.6 1.4 %copy-start.2 = (bf16[13,2,128,192]{2,0,1,3:T(8,128)(2,1)S(1)}, bf16[13,2,128,192]{2,0,1,3:T(8,128)(2,1)}, u32[]{:S(2)}) copy-start(bf16[13,2,128,192]{2,0,1,3:T(8,128)(2,1)} %get-tuple-element.12) | copy-start | bytes 3833860
  86.2 1.4 %copy-start.1 = (bf16[13,2,128,192]{2,0,1,3:T(8,128)(2,1)S(1)}, bf16[13,2,128,192]{2,0,1,3:T(8,128)(2,1)}, u32[]{:S(2)}) copy-start(bf16[13,2,128,192]{2,0,1,3:T(8,128)(2,1)} %get-tuple-element.11) | copy-start | bytes 3833860
  87.6 1.4 %copy-start = (bf16[13,2,128,192]{2,0,1,3:T(8,128)(2,1)S(1)}, bf16[13,2,128,192]{2,0,1,3:T(8,128)(2,1)}, u32[]{:S(2)}) copy-start(bf16[13,2,128,192]{2,0,1,3:T(8,128)(2,1)} %get-tuple-element.10) | copy-start | bytes 3833860
  91.5 6.2 %collective-permute-start.8 = (f32[1,64,128]{2,1,0:T(8,128)S(1)}, f32[1,64,128]{2,1,0:T(8,128)S(1)}, u32[]{:S(2)}, u32[]{:S(2)}) collective-permute-start(f32[1,64,128]{2,1,0:T(8,128)S(1)} %dynamic-slice_bitcast_fusion), channel_id=1, source_target_pairs={{0,8},{1,9},{2,10},{3,11},{4,12},{5,13},{6,14},{7,15},{8,0},{9,1},... | collective-permute-start | bytes 98312 | tf_op jit(solution)/shard_map/ppermute | solution.py:105
  97.7 4.5 %collective-permute-start.9 = (f32[1,32,128]{2,1,0:T(8,128)S(1)}, f32[1,32,128]{2,1,0:T(8,128)S(1)}, u32[]{:S(2)}, u32[]{:S(2)}) collective-permute-start(f32[1,32,128]{2,1,0:T(8,128)S(1)} %constant_dynamic-slice_fusion.3), channel_id=1, source_target_pairs={{0,4},{1,5},{2,6},{3,7},{4,0},{5,1},{6,2},{7,3},{8,12},{9,13},{10,... | collective-permute-start | bytes 49160 | tf_op jit(solution)/shard_map/ppermute | solution.py:105
  102.2 8.3 %collective-permute-start.10 = (f32[1,16,128]{2,1,0:T(8,128)S(1)}, f32[1,16,128]{2,1,0:T(8,128)S(1)}, u32[]{:S(2)}, u32[]{:S(2)}) collective-permute-start(f32[1,16,128]{2,1,0:T(8,128)S(1)} %constant_dynamic-slice_fusion.2), channel_id=1, source_target_pairs={{0,2},{1,3},{2,0},{3,1},{4,6},{5,7},{6,4},{7,5},{8,10},{9,11},{10,... | collective-permute-start | bytes 24584 | tf_op jit(solution)/shard_map/ppermute | solution.py:105
  110.5 11.5 %collective-permute-start.11 = (f32[1,8,128]{2,1,0:T(8,128)S(1)}, f32[1,8,128]{2,1,0:T(8,128)S(1)}, u32[]{:S(2)}, u32[]{:S(2)}) collective-permute-start(f32[1,8,128]{2,1,0:T(8,128)S(1)} %constant_dynamic-slice_fusion.1), channel_id=1, source_target_pairs={{0,1},{1,0},{2,3},{3,2},{4,5},{5,4},{6,7},{7,6},{8,9},{9,8},{10,11... | collective-permute-start | bytes 12296 | tf_op jit(solution)/shard_map/ppermute | solution.py:105

commit v2 on v1

--- a/solution.py
+++ b/solution.py
@@ -82,29 +82,16 @@
     return band.astype(taps.dtype)
 
 
-def butterfly_sum(value, axis):
-    devices = lax.axis_size(axis)
-    bit = 1
-    while bit < devices:
-        pairs = [(i, i ^ bit) for i in range(devices)]
-        value = value + lax.ppermute(value, axis, pairs)
-        bit *= 2
-    return value
+def scatter_sum(value, axis, dim):
+    pieces = lax.all_to_all(value, axis, dim, 0, tiled=True)
+    return jnp.sum(pieces, axis=0, keepdims=True)
 
 
-def halving_scatter(value, axis, dim):
+def gather_blocks(block, axis, dim):
     devices = lax.axis_size(axis)
-    place = lax.axis_index(axis)
-    bit = devices // 2
-    while bit >= 1:
-        half = value.shape[dim] // 2
-        upper = (place // bit) % 2
-        keep = lax.dynamic_slice_in_dim(value, upper * half, half, dim)
-        give = lax.dynamic_slice_in_dim(value, (1 - upper) * half, half, dim)
-        pairs = [(i, i ^ bit) for i in range(devices)]
-        value = keep + lax.ppermute(give, axis, pairs)
-        bit //= 2
-    return value
+    copies = jnp.broadcast_to(block, (devices,) + block.shape[1:])
+    pieces = lax.all_to_all(copies, axis, 0, 0, tiled=True)
+    return jnp.concatenate(jnp.split(pieces, devices, axis=0), axis=dim)
 
 
 def correlate_forward(images, band, rows_out):
@@ -163,16 +150,13 @@
     fields = correlate_forward(extended, forward_band, tile_side)
     doubled = jnp.concatenate([weights, weights])
     partial_sum = jnp.sum(doubled[None, :, None, None] * fields * fields, axis=1)
-    intensity = butterfly_sum(partial_sum, "kern")
-    resist_full = jax.nn.sigmoid(steepness * (intensity - threshold))
-    sensitivity = (
-        2.0
-        * (resist_full - target.astype(jnp.float32))
-        * steepness
-        * resist_full
-        * (1.0 - resist_full)
+    intensity = scatter_sum(partial_sum, "kern", 1)
+    resist = jax.nn.sigmoid(steepness * (intensity - threshold))
+    own_target = lax.dynamic_slice_in_dim(target, kern_place * share_rows, share_rows, 1)
+    own_sensitivity = (
+        2.0 * (resist - own_target.astype(jnp.float32)) * steepness * resist * (1.0 - resist)
     )
-    resist = lax.dynamic_slice_in_dim(resist_full, kern_place * share_rows, share_rows, 1)
+    sensitivity = gather_blocks(own_sensitivity, "kern", 1)
     scaled = (2.0 * doubled)[None, :, None, None] * sensitivity[:, None] * fields
     adjoint_source = scaled.astype(jnp.bfloat16)
     source_strips = jnp.stack(
@@ -182,7 +166,7 @@
     source_ext = assemble(adjoint_source, source_framed[0], source_framed[3], neighbours)
     adjoint_band = banded(taps[:, ::-1, ::-1], width_in, tile_side)
     gradient_term = correlate_adjoint(source_ext, adjoint_band, tile_side)
-    gradient = halving_scatter(gradient_term, "kern", 1)
+    gradient = scatter_sum(gradient_term, "kern", 1)
     return (gradient, resist)
 
 

time: 123 us -> 121 us (0.984)
  the two profiles are of different devices: /device:TPU:41 before, /device:TPU:9 now
where the time goes in v2:
time: 121 us; the launch traced here: 120 us
  starting transfers between devices  42 us (35%)
  local copies, waits for them, and re-layouts  25.4 us (21%)
  blocking collectives  17.6 us (15%)
  matrix products  16.1 us (13%)
  waiting for transfers between devices  9.62 us (8%)
  between operations  7.04 us (6%)
  other arithmetic  2.74 us (2%)
    ppermute x2, starting transfers between devices, padded_2(): after = lax.ppermute(first, axis, down)  21.2 us
    all_to_all x1, blocking collectives, scatter_sum(): pieces = lax.all_to_all(value, axis, dim, 0, tiled=True)  17.6 us
    all_to_all x1, starting transfers between devices, scatter_sum(): pieces = lax.all_to_all(value, axis, dim, 0, tiled=True)  10.5 us
    unnamed x67, local copies, waits for them, and re-layouts  9.68 us
    dot_general x2, matrix products, banded(): jnp.einsum('acb,bji->acji', taps.transpose(1, 0, 2), select, preferred_el...  7.59 us
    slice x1, local copies, waits for them, and re-layouts, correlate_adjoint(): band[first:first + group]  7.05 us
    ppermute x2, starting transfers between devices, padded_2(): before = lax.ppermute(last, axis, up)  5.91 us
    all_to_all x1, waiting for transfers between devices, scatter_sum(): pieces = lax.all_to_all(value, axis, dim, 0, tiled=True)  5.29 us
  transfers between devices with their start and end apart: 6, of which 3 were waited for; matrix products, arithmetic and copies ran while one was open for 18% of the time, Pallas kernels for 0%

profile of v2, /device:TPU:9, one launch (start us, length us, event | category | flops | bytes accessed | tf_op | source)
XLA Modules:
  0.0 120.5 jit_solution(6244590656166273713)
XLA Ops:
  1.3 4.0 %collective-permute-start = (bf16[1,1,32,128]{3,2,1,0:T(8,128)(2,1)S(1)}, bf16[1,1,32,128]{3,2,1,0:T(8,128)(2,1)S(1)}, u32[]{:S(2)}, u32[]{:S(2)}) collective-permute-start(bf16[1,1,32,128]{3,2,1,0:T(8,128)(2,1)S(1)} %get-tuple-element.155), channel_id=1, source_target_pairs={{0,16},{16,32},{32,48},{48,64},{64,80},{80,96},{96,112},{112,128},... | collective-permute-start | bytes 24584 | tf_op jit(solution)/shard_map/ppermute | solution.py:17
  5.3 15.8 %collective-permute-start.1 = (bf16[1,1,32,128]{3,2,1,0:T(8,128)(2,1)S(1)}, bf16[1,1,32,128]{3,2,1,0:T(8,128)(2,1)S(1)}, u32[]{:S(2)}, u32[]{:S(2)}) collective-permute-start(bf16[1,1,32,128]{3,2,1,0:T(8,128)(2,1)S(1)} %get-tuple-element.156), channel_id=1, source_target_pairs={{16,0},{32,16},{48,32},{64,48},{80,64},{96,80},{112,96},{128,112},... | collective-permute-start | bytes 24584 | tf_op jit(solution)/shard_map/ppermute | solution.py:18
  21.1 0.9 copy.49
  22.0 1.6 %fusion.121 = (s32[1,1]{1,0:T(1,128)}, s32[1,1]{1,0:T(1,128)}, s32[1,1]{1,0:T(1,128)}, s32[1,1]{1,0:T(1,128)}, s32[1,1]{1,0:T(1,128)}, /*index=5*/s32[1,1]{1,0:T(1,128)}, s32[1,1]{1,0:T(1,128)}, s32[1,1]{1,0:T(1,128)}) fusion(s32[1,8]{1,0:T(1,128)} %param.9), kind=kLoop, calls=%fused_computation.369 | loop fusion | bytes 64 | tf_op jit(solution)/shard_map/slice | solution.py:36
  24.7 2.8 %convert_bitcast_fusion.1 = bf16[65,2,128,192]{2,0,1,3:T(8,128)(2,1)S(1)} fusion(bf16[65,2,65]{2,1,0:T(2,128)(2,1)} %bitcast.704), kind=kOutput, calls=%fused_computation.1 | convolution fusion | flops 421724160 | bytes 6406660 | tf_op jit(solution)/shard_map/acb,bji->acji/dot_general | solution.py:79
  27.5 4.0 %fusion.120 = (bf16[13,2,128,192]{2,0,1,3:T(8,128)(2,1)S(1)}, bf16[13,2,128,192]{2,0,1,3:T(8,128)(2,1)S(1)}, bf16[13,2,128,192]{2,0,1,3:T(8,128)(2,1)}, bf16[13,...) fusion(bf16[65,2,128,192]{2,0,1,3:T(8,128)(2,1)S(1)} %convert_bitcast_fusion.1), kind=kLoop, calls=%fused_computation.368 | loop fusion | bytes 12779520 | tf_op jit(solution)/shard_map/slice | solution.py:107
  39.8 0.9 fusion.34
  40.8 0.9 fusion.61
  42.2 0.8 fusion.58
  43.1 0.9 fusion.55
  43.9 0.9 fusion.114
  45.6 10.5 %all-to-all-start = ((f32[1,128,128]{2,0,1:T(1,128)}), f32[1,128,128]{2,0,1:T(1,128)S(1)}, u32[]{:S(2)}, u32[]{:S(2)}) async-start(f32[1,128,128]{2,0,1:T(1,128)} %copy.58), calls=%async_computation | async-start | bytes 131072 | tf_op jit(solution)/shard_map/all_to_all | solution.py:86
  56.1 4.8 %convert_bitcast_fusion = bf16[65,2,128,192]{2,0,1,3:T(8,128)(2,1)} fusion(bf16[65,2,65]{2,1,0:T(2,128)(2,1)S(1)} %bitcast.706), kind=kOutput, calls=%fused_computation | convolution fusion | flops 421724160 | bytes 6406660 | tf_op jit(solution)/shard_map/acb,bji->acji/dot_general | solution.py:79
  60.9 5.3 %all-to-all-done = f32[1,128,128]{2,0,1:T(1,128)S(1)} async-done(((f32[1,128,128]{2,0,1:T(1,128)}), f32[1,128,128]{2,0,1:T(1,128)S(1)}, u32[]{:S(2)}, u32[]{:S(2)}) %all-to-all-start) | async-done | bytes 65568 | tf_op jit(solution)/shard_map/all_to_all | solution.py:86
  66.3 1.3 %multiply_bitcast_fusion.6 = (f32[8,128]{1,0:T(8,128)S(1)}, f32[1,8,128]{2,1,0:T(8,128)}) fusion(bf16[1,128,128]{2,1,0:T(8,128)(2,1)} %param.8, s32[]{:T(128)S(6)} %select_n.207, f32[8,128]{1,0:T(8,128)S(1)} %reduce_sum.31), kind=kLoop, calls=%fused_computation.362 | loop fusion | flops 11264 | bytes 14340 | tf_op jit(solution)/shard_map/broadcast_in_dim | solution.py:92
  68.2 4.3 %all-to-all-start.1 = ((f32[16,8,128]{2,1,0:T(8,128)}), f32[16,8,128]{2,1,0:T(8,128)S(1)}, u32[]{:S(2)}, u32[]{:S(2)}) async-start(f32[16,8,128]{2,1,0:T(8,128)} %broadcast_in_dim.95), calls=%async_computation.1 | async-start | bytes 131072 | tf_op jit(solution)/shard_map/all_to_all | solution.py:93
  72.5 7.1 %fusion.119 = (bf16[13,2,128,192]{2,0,1,3:T(8,128)(2,1)S(1)}, bf16[13,2,128,192]{2,0,1,3:T(8,128)(2,1)S(1)}, bf16[13,2,128,192]{2,0,1,3:T(8,128)(2,1)}, bf16[13,...) fusion(bf16[65,2,128,192]{2,0,1,3:T(8,128)(2,1)} %convert_bitcast_fusion), kind=kLoop, calls=%fused_computation.367 | loop fusion | bytes 12779520 | tf_op jit(solution)/shard_map/slice | solution.py:126
  79.6 3.1 %all-to-all-done.1 = f32[16,8,128]{2,1,0:T(8,128)S(1)} async-done(((f32[16,8,128]{2,1,0:T(8,128)}), f32[16,8,128]{2,1,0:T(8,128)S(1)}, u32[]{:S(2)}, u32[]{:S(2)}) %all-to-all-start.1) | async-done | bytes 65568 | tf_op jit(solution)/shard_map/all_to_all | solution.py:93
  83.1 1.9 %collective-permute-start.2 = (bf16[1,1,2,32,128]{3,4,2,1,0:T(8,128)(2,1)S(1)}, bf16[1,1,2,32,128]{3,4,2,1,0:T(8,128)(2,1)S(1)}, u32[]{:S(2)}, u32[]{:S(2)}) collective-permute-start(bf16[1,1,2,32,128]{3,4,2,1,0:T(8,128)(2,1)S(1)} %get-tuple-element.149), channel_id=1, source_target_pairs={{0,16},{16,32},{32,48},{48,64},{64,80},{80,96},{96,112},{112,128},... | collective-permute-start | bytes 49160 | tf_op jit(solution)/shard_map/ppermute | solution.py:17
  85.0 5.5 %collective-permute-start.3 = (bf16[1,1,2,32,128]{3,4,2,1,0:T(8,128)(2,1)S(1)}, bf16[1,1,2,32,128]{3,4,2,1,0:T(8,128)(2,1)S(1)}, u32[]{:S(2)}, u32[]{:S(2)}) collective-permute-start(bf16[1,1,2,32,128]{3,4,2,1,0:T(8,128)(2,1)S(1)} %get-tuple-element.148), channel_id=1, source_target_pairs={{16,0},{32,16},{48,32},{64,48},{80,64},{96,80},{112,96},{128,112},... | collective-permute-start | bytes 49160 | tf_op jit(solution)/shard_map/ppermute | solution.py:18
  90.6 1.2 %collective-permute-done.3 = bf16[1,1,2,32,128]{3,4,2,1,0:T(8,128)(2,1)S(1)} collective-permute-done((bf16[1,1,2,32,128]{3,4,2,1,0:T(8,128)(2,1)S(1)}, bf16[1,1,2,32,128]{3,4,2,1,0:T(8,128)(2,1)S(1)}, u32[]{:S(2)}, u32[]{:S(2)}) %collective-permute-start.3) | collective-permute-done | bytes 16416 | tf_op jit(solution)/shard_map/ppermute | solution.py:18
  98.3 0.8 fusion.104
  100.6 0.8 fusion.94
  102.2 17.6 %all_to_all.29 = f32[1,128,128]{2,0,1:T(1,128)S(1)} all-to-all(f32[1,128,128]{2,0,1:T(1,128)S(1)} %bitcast.709), channel_id=1, replica_groups=mesh['tile'=64,'kern'=16] {'kern'}, dimensions={1} | all-to-all | bytes 131072 | tf_op jit(solution)/shard_map/all_to_all | solution.py:86
  (104 shorter events, 15.8 us)
Async XLA Ops:
  1.3 35.0 %collective-permute-start = (bf16[1,1,32,128]{3,2,1,0:T(8,128)(2,1)S(1)}, bf16[1,1,32,128]{3,2,1,0:T(8,128)(2,1)S(1)}, u32[]{:S(2)}, u32[]{:S(2)}) collective-permute-start(bf16[1,1,32,128]{3,2,1,0:T(8,128)(2,1)S(1)} %get-tuple-element.155), channel_id=1, source_target_pairs={{0,16},{16,32},{32,48},{48,64},{64,80},{80,96},{96,112},{112,128},... | collective-permute-start | bytes 24584 | tf_op jit(solution)/shard_map/ppermute | solution.py:17
  5.3 31.3 %collective-permute-start.1 = (bf16[1,1,32,128]{3,2,1,0:T(8,128)(2,1)S(1)}, bf16[1,1,32,128]{3,2,1,0:T(8,128)(2,1)S(1)}, u32[]{:S(2)}, u32[]{:S(2)}) collective-permute-start(bf16[1,1,32,128]{3,2,1,0:T(8,128)(2,1)S(1)} %get-tuple-element.156), channel_id=1, source_target_pairs={{16,0},{32,16},{48,32},{64,48},{80,64},{96,80},{112,96},{128,112},... | collective-permute-start | bytes 24584 | tf_op jit(solution)/shard_map/ppermute | solution.py:18
  27.5 8.6 %copy-start.6 = (bf16[2,1,65,65]{3,0,2,1:T(2,128)(2,1)S(1)}, bf16[2,1,65,65]{3,0,2,1:T(2,128)(2,1)}, u32[]{:S(2)}) copy-start(bf16[2,1,65,65]{3,0,2,1:T(2,128)(2,1)} %param.6) | copy-start | bytes 50704
  38.4 1.4 %copy-start.5 = (bf16[13,2,128,192]{2,0,1,3:T(8,128)(2,1)S(1)}, bf16[13,2,128,192]{2,0,1,3:T(8,128)(2,1)}, u32[]{:S(2)}) copy-start(bf16[13,2,128,192]{2,0,1,3:T(8,128)(2,1)} %get-tuple-element.13) | copy-start | bytes 3833860
  39.3 1.5 %copy-start.4 = (bf16[13,2,128,192]{2,0,1,3:T(8,128)(2,1)S(1)}, bf16[13,2,128,192]{2,0,1,3:T(8,128)(2,1)}, u32[]{:S(2)}) copy-start(bf16[13,2,128,192]{2,0,1,3:T(8,128)(2,1)} %get-tuple-element.12) | copy-start | bytes 3833860
  40.8 1.4 %copy-start.3 = (bf16[13,2,128,192]{2,0,1,3:T(8,128)(2,1)S(1)}, bf16[13,2,128,192]{2,0,1,3:T(8,128)(2,1)}, u32[]{:S(2)}) copy-start(bf16[13,2,128,192]{2,0,1,3:T(8,128)(2,1)} %get-tuple-element.11) | copy-start | bytes 3833860
  45.6 20.7 %all-to-all-start = ((f32[1,128,128]{2,0,1:T(1,128)}), f32[1,128,128]{2,0,1:T(1,128)S(1)}, u32[]{:S(2)}, u32[]{:S(2)}) async-start(f32[1,128,128]{2,0,1:T(1,128)} %copy.58), calls=%async_computation | async-start | bytes 131072 | tf_op jit(solution)/shard_map/all_to_all | solution.py:86
  68.2 14.5 %all-to-all-start.1 = ((f32[16,8,128]{2,1,0:T(8,128)}), f32[16,8,128]{2,1,0:T(8,128)S(1)}, u32[]{:S(2)}, u32[]{:S(2)}) async-start(f32[16,8,128]{2,1,0:T(8,128)} %broadcast_in_dim.95), calls=%async_computation.1 | async-start | bytes 131072 | tf_op jit(solution)/shard_map/all_to_all | solution.py:93
  83.1 7.4 %collective-permute-start.2 = (bf16[1,1,2,32,128]{3,4,2,1,0:T(8,128)(2,1)S(1)}, bf16[1,1,2,32,128]{3,4,2,1,0:T(8,128)(2,1)S(1)}, u32[]{:S(2)}, u32[]{:S(2)}) collective-permute-start(bf16[1,1,2,32,128]{3,4,2,1,0:T(8,128)(2,1)S(1)} %get-tuple-element.149), channel_id=1, source_target_pairs={{0,16},{16,32},{32,48},{48,64},{64,80},{80,96},{96,112},{112,128},... | collective-permute-start | bytes 49160 | tf_op jit(solution)/shard_map/ppermute | solution.py:17
  85.0 6.8 %collective-permute-start.3 = (bf16[1,1,2,32,128]{3,4,2,1,0:T(8,128)(2,1)S(1)}, bf16[1,1,2,32,128]{3,4,2,1,0:T(8,128)(2,1)S(1)}, u32[]{:S(2)}, u32[]{:S(2)}) collective-permute-start(bf16[1,1,2,32,128]{3,4,2,1,0:T(8,128)(2,1)S(1)} %get-tuple-element.148), channel_id=1, source_target_pairs={{16,0},{32,16},{48,32},{64,48},{80,64},{96,80},{112,96},{128,112},... | collective-permute-start | bytes 49160 | tf_op jit(solution)/shard_map/ppermute | solution.py:18
  94.3 1.4 %copy-start.2 = (bf16[13,2,128,192]{2,0,1,3:T(8,128)(2,1)S(1)}, bf16[13,2,128,192]{2,0,1,3:T(8,128)(2,1)}, u32[]{:S(2)}) copy-start(bf16[13,2,128,192]{2,0,1,3:T(8,128)(2,1)} %get-tuple-element.8) | copy-start | bytes 3833860
  96.9 1.4 %copy-start.1 = (bf16[13,2,128,192]{2,0,1,3:T(8,128)(2,1)S(1)}, bf16[13,2,128,192]{2,0,1,3:T(8,128)(2,1)}, u32[]{:S(2)}) copy-start(bf16[13,2,128,192]{2,0,1,3:T(8,128)(2,1)} %get-tuple-element.7) | copy-start | bytes 3833860
  98.3 1.4 %copy-start = (bf16[13,2,128,192]{2,0,1,3:T(8,128)(2,1)S(1)}, bf16[13,2,128,192]{2,0,1,3:T(8,128)(2,1)}, u32[]{:S(2)}) copy-start(bf16[13,2,128,192]{2,0,1,3:T(8,128)(2,1)} %get-tuple-element.6) | copy-start | bytes 3833860

commit v3 on v2

--- a/solution.py
+++ b/solution.py
@@ -62,13 +62,6 @@
     return jnp.concatenate([upper_band, middle_band, lower_band], axis=2)
 
 
-def group_size(tap_count):
-    for candidate in range(min(tap_count, 16), 0, -1):
-        if tap_count % candidate == 0:
-            return candidate
-    return 1
-
-
 def banded(taps, width_in, width_out):
     tap_count = taps.shape[2]
     shape = (tap_count, width_out, width_in)
@@ -94,41 +87,30 @@
     return jnp.concatenate(jnp.split(pieces, devices, axis=0), axis=dim)
 
 
+def shifted_rows(images, tap_count, rows_out):
+    rows_in = images.shape[-2]
+    shape = (tap_count, rows_out, rows_in)
+    along = lax.broadcasted_iota(jnp.int32, shape, 0)
+    row = lax.broadcasted_iota(jnp.int32, shape, 1)
+    source = lax.broadcasted_iota(jnp.int32, shape, 2)
+    return (source - row == along).astype(images.dtype)
+
+
 def correlate_forward(images, band, rows_out):
-    tap_count = band.shape[0]
-    group = group_size(tap_count)
-    total = None
-    for first in range(0, tap_count, group):
-        stacked = jnp.stack(
-            [images[:, first + step : first + step + rows_out, :] for step in range(group)], axis=1
-        )
-        term = lax.dot_general(
-            stacked,
-            band[first : first + group],
-            (((1, 3), (0, 3)), ((), ())),
-            preferred_element_type=jnp.float32,
-        )
-        total = term if total is None else total + term
-    return total.transpose(0, 2, 1, 3)
+    select = shifted_rows(images, band.shape[0], rows_out)
+    stacked = jnp.einsum(
+        "apr,tri->tapi", select, images, preferred_element_type=jnp.float32
+    ).astype(images.dtype)
+    total = jnp.einsum("tapi,acqi->tcpq", stacked, band, preferred_element_type=jnp.float32)
+    return total
 
 
 def correlate_adjoint(images, band, rows_out):
-    tap_count = band.shape[0]
-    group = group_size(tap_count)
-    total = None
-    for first in range(0, tap_count, group):
-        stacked = jnp.stack(
-            [images[:, :, first + step : first + step + rows_out, :] for step in range(group)],
-            axis=1,
-        )
-        term = lax.dot_general(
-            stacked,
-            band[first : first + group],
-            (((1, 2, 4), (0, 1, 3)), ((), ())),
-            preferred_element_type=jnp.float32,
-        )
-        total = term if total is None else total + term
-    return total
+    select = shifted_rows(images, band.shape[0], rows_out)
+    stacked = jnp.einsum(
+        "apr,tcri->tacpi", select, images, preferred_element_type=jnp.float32
+    ).astype(images.dtype)
+    return jnp.einsum("tacpi,acqi->tpq", stacked, band, preferred_element_type=jnp.float32)
 
 
 def shards(mask, kernels, weights, target, neighbours):

time: 121 us -> 111 us (0.917)
  local copies, waits for them, and re-layouts: 25.4 us -> 6.31 us
  waiting for transfers between devices: 9.62 us -> 16 us
  matrix products: 16.1 us -> 21.2 us
  blocking collectives: 17.6 us -> 15.5 us
    slice x2 -> x0, local copies, waits for them, and re-layouts: 11 us -> none  [the longest x1 7.05 us: correlate_adjoint(): band[first:first + group]]
    unnamed x67 -> x22, local copies, waits for them, and re-layouts: 9.68 us -> 2.01 us
    all_to_all x1, waiting for transfers between devices: 5.29 us -> 9.93 us  [scatter_sum(): pieces = lax.all_to_all(value, axis, dim, 0, tiled=True)]
    dot_general x2, matrix products: 7.59 us -> 10.5 us  [banded(): jnp.einsum('acb,bji->acji', taps.transpose(1, 0, 2), select, preferred_el...]
    all_to_all x1, blocking collectives: 17.6 us -> 15.5 us  [scatter_sum(): pieces = lax.all_to_all(value, axis, dim, 0, tiled=True)]
    dot_general x10 -> x3, matrix products: 8.47 us -> 10.6 us  [the longest x1 6.61 us: correlate_forward(): jnp.einsum('tapi,acqi->tcpq', stacked, band, preferred_element_type=jnp.f...]
    all_to_all x1, waiting for transfers between devices: 3.07 us -> 5.01 us  [gather_blocks(): pieces = lax.all_to_all(copies, axis, 0, 0, tiled=True)]
  transfers between devices with their start and end apart: 6 -> 6, of which waited for: 3 -> 3; matrix products, arithmetic and copies ran while one was open for 18% -> 13% of each run, Pallas kernels for 0% -> 0%
where the time goes in v3:
time: 111 us
  starting transfers between devices  41.6 us (37%)
  matrix products  21.2 us (19%)
  waiting for transfers between devices  16 us (14%)
  blocking collectives  15.5 us (14%)
  between operations  6.62 us (6%)
  local copies, waits for them, and re-layouts  6.31 us (6%)
  other arithmetic  3.49 us (3%)
    ppermute x2, starting transfers between devices, padded_2(): after = lax.ppermute(first, axis, down)  21.4 us
    all_to_all x1, blocking collectives, scatter_sum(): pieces = lax.all_to_all(value, axis, dim, 0, tiled=True)  15.5 us
    dot_general x2, matrix products, banded(): jnp.einsum('acb,bji->acji', taps.transpose(1, 0, 2), select, preferred_el...  10.5 us
    all_to_all x1, starting transfers between devices, scatter_sum(): pieces = lax.all_to_all(value, axis, dim, 0, tiled=True)  10.5 us
    all_to_all x1, waiting for transfers between devices, scatter_sum(): pieces = lax.all_to_all(value, axis, dim, 0, tiled=True)  9.93 us
    dot_general x1, matrix products, correlate_forward(): jnp.einsum('tapi,acqi->tcpq', stacked, band, preferred_element_type=jnp.f...  6.61 us
    ppermute x2, starting transfers between devices, padded_2(): before = lax.ppermute(last, axis, up)  5.91 us
    all_to_all x1, waiting for transfers between devices, gather_blocks(): pieces = lax.all_to_all(copies, axis, 0, 0, tiled=True)  5.01 us
  transfers between devices with their start and end apart: 6, of which 3 were waited for; matrix products, arithmetic and copies ran while one was open for 13% of the time, Pallas kernels for 0%

profile of v3, /device:TPU:9, one launch (start us, length us, event | category | flops | bytes accessed | tf_op | source)
XLA Modules:
  0.0 110.7 jit_solution(2329825697792162491)
XLA Ops:
  0.6 0.7 slice_bitcast_fusion.3
  1.3 4.0 %collective-permute-start = (bf16[1,1,32,128]{3,2,1,0:T(8,128)(2,1)S(1)}, bf16[1,1,32,128]{3,2,1,0:T(8,128)(2,1)S(1)}, u32[]{:S(2)}, u32[]{:S(2)}) collective-permute-start(bf16[1,1,32,128]{3,2,1,0:T(8,128)(2,1)S(1)} %get-tuple-element.14), channel_id=1, source_target_pairs={{0,16},{16,32},{32,48},{48,64},{64,80},{80,96},{96,112},{112,128},... | collective-permute-start | bytes 24584 | tf_op jit(solution)/shard_map/ppermute | solution.py:17
  5.3 15.8 %collective-permute-start.1 = (bf16[1,1,32,128]{3,2,1,0:T(8,128)(2,1)S(1)}, bf16[1,1,32,128]{3,2,1,0:T(8,128)(2,1)S(1)}, u32[]{:S(2)}, u32[]{:S(2)}) collective-permute-start(bf16[1,1,32,128]{3,2,1,0:T(8,128)(2,1)S(1)} %get-tuple-element.15), channel_id=1, source_target_pairs={{16,0},{32,16},{48,32},{64,48},{80,64},{96,80},{112,96},{128,112},... | collective-permute-start | bytes 24584 | tf_op jit(solution)/shard_map/ppermute | solution.py:18
  21.1 0.9 copy.28
  22.0 1.0 iota_compare_fusion
  23.0 1.6 %fusion.73 = (s32[1,1]{1,0:T(1,128)}, s32[1,1]{1,0:T(1,128)}, s32[1,1]{1,0:T(1,128)}, s32[1,1]{1,0:T(1,128)}, s32[1,1]{1,0:T(1,128)}, /*index=5*/s32[1,1]{1,0:T(1,128)}, s32[1,1]{1,0:T(1,128)}, s32[1,1]{1,0:T(1,128)}) fusion(s32[1,8]{1,0:T(1,128)} %param.9), kind=kLoop, calls=%fused_computation.98 | loop fusion | bytes 64 | tf_op jit(solution)/shard_map/slice | solution.py:36
  26.5 5.6 %convert_bitcast_fusion.1 = bf16[65,2,128,192]{2,0,1,3:T(8,128)(2,1)} fusion(bf16[65,2,65]{2,1,0:T(2,128)(2,1)} %bitcast.119), kind=kOutput, calls=%fused_computation.1 | convolution fusion | flops 421724160 | bytes 6406660 | tf_op jit(solution)/shard_map/acb,bji->acji/dot_general | solution.py:72
  36.6 6.6 %fusion.49 = (f32[128,128]{0,1:T(8,128)S(1)}, f32[1,2,128,128]{2,3,1,0:T(8,128)S(1)}) fusion(f32[2]{0:T(128)S(1)} %get-tuple-element.32, pred[65,128,192]{1,0,2:T(8,128)(4,1)S(1)} %iota_compare_fusion, bf16[1,1,32,192]{2,3,1,0:T(8,128)(2,1)S(1)} %copy.30, bf16[1,1,128,32]{2,3,1,0:T(8,128)(2,1)S(1)} %get-tuple-element.17, ...), kind=kOutput, calls=%fused_computation.39 | convolution fusion | flops 1433354240 | bytes 8257544 | tf_op jit(solution)/shard_map/tapi,acqi->tcpq/dot_general | solution.py:104
  43.3 0.7 copy.33
  44.0 10.5 %all-to-all-start = ((f32[1,128,128]{2,0,1:T(1,128)}), f32[1,128,128]{2,0,1:T(1,128)S(1)}, u32[]{:S(2)}, u32[]{:S(2)}) async-start(f32[1,128,128]{2,0,1:T(1,128)} %copy.33), calls=%async_computation | async-start | bytes 131072 | tf_op jit(solution)/shard_map/all_to_all | solution.py:79
  54.7 9.9 %all-to-all-done = f32[1,128,128]{2,0,1:T(1,128)S(1)} async-done(((f32[1,128,128]{2,0,1:T(1,128)}), f32[1,128,128]{2,0,1:T(1,128)S(1)}, u32[]{:S(2)}, u32[]{:S(2)}) %all-to-all-start) | async-done | bytes 65568 | tf_op jit(solution)/shard_map/all_to_all | solution.py:79
  64.6 1.3 %multiply_bitcast_fusion.6 = (f32[8,128]{1,0:T(8,128)S(1)}, f32[1,8,128]{2,1,0:T(8,128)}) fusion(bf16[1,128,128]{2,1,0:T(8,128)(2,1)} %param.8, s32[]{:T(128)S(6)} %select_n.207, f32[8,128]{1,0:T(8,128)S(1)} %reduce_sum.31), kind=kLoop, calls=%fused_computation.91 | loop fusion | flops 11264 | bytes 14340 | tf_op jit(solution)/shard_map/broadcast_in_dim | solution.py:85
  65.9 0.6 broadcast_in_dim.95
  66.6 3.8 %all-to-all-start.1 = ((f32[16,8,128]{2,1,0:T(8,128)}), f32[16,8,128]{2,1,0:T(8,128)S(1)}, u32[]{:S(2)}, u32[]{:S(2)}) async-start(f32[16,8,128]{2,1,0:T(8,128)} %broadcast_in_dim.95), calls=%async_computation.1 | async-start | bytes 131072 | tf_op jit(solution)/shard_map/all_to_all | solution.py:86
  70.4 4.9 %convert_bitcast_fusion = bf16[65,2,128,192]{2,0,1,3:T(8,128)(2,1)} fusion(bf16[65,2,65]{2,1,0:T(2,128)(2,1)S(1)} %bitcast.121), kind=kOutput, calls=%fused_computation | convolution fusion | flops 421724160 | bytes 6406660 | tf_op jit(solution)/shard_map/acb,bji->acji/dot_general | solution.py:72
  75.3 5.0 %all-to-all-done.1 = f32[16,8,128]{2,1,0:T(8,128)S(1)} async-done(((f32[16,8,128]{2,1,0:T(8,128)}), f32[16,8,128]{2,1,0:T(8,128)S(1)}, u32[]{:S(2)}, u32[]{:S(2)}) %all-to-all-start.1) | async-done | bytes 65568 | tf_op jit(solution)/shard_map/all_to_all | solution.py:86
  80.7 1.9 %collective-permute-start.2 = (bf16[1,1,2,32,128]{3,4,2,1,0:T(8,128)(2,1)S(1)}, bf16[1,1,2,32,128]{3,4,2,1,0:T(8,128)(2,1)S(1)}, u32[]{:S(2)}, u32[]{:S(2)}) collective-permute-start(bf16[1,1,2,32,128]{3,4,2,1,0:T(8,128)(2,1)S(1)} %get-tuple-element.7), channel_id=1, source_target_pairs={{0,16},{16,32},{32,48},{48,64},{64,80},{80,96},{96,112},{112,128},... | collective-permute-start | bytes 49160 | tf_op jit(solution)/shard_map/ppermute | solution.py:17
  82.7 5.7 %collective-permute-start.3 = (bf16[1,1,2,32,128]{3,4,2,1,0:T(8,128)(2,1)S(1)}, bf16[1,1,2,32,128]{3,4,2,1,0:T(8,128)(2,1)S(1)}, u32[]{:S(2)}, u32[]{:S(2)}) collective-permute-start(bf16[1,1,2,32,128]{3,4,2,1,0:T(8,128)(2,1)S(1)} %get-tuple-element.8), channel_id=1, source_target_pairs={{16,0},{32,16},{48,32},{64,48},{80,64},{96,80},{112,96},{128,112},... | collective-permute-start | bytes 49160 | tf_op jit(solution)/shard_map/ppermute | solution.py:18
  88.4 1.1 collective-permute-done.3
  89.5 1.9 %convert_bitcast_fusion.2 = bf16[65,2,128,192]{2,3,0,1:T(8,128)(2,1)S(1)} fusion(pred[65,128,192]{1,0,2:T(8,128)(4,1)S(1)} %iota_compare_fusion, bf16[1,2,32,32]{2,3,1,0:T(8,128)(2,1)S(1)} %slice.117, bf16[1,2,32,128]{2,3,1,0:T(8,128)(2,1)S(1)} %get-tuple-element.12, bf16[1,2,32,32]{2,3,1,0:T(8,128)(2,1)S(1)} %slice.116, ...), kind=kOutput, calls=%fused_computation.12 | convolution fusion | flops 1231355904 | bytes 8134656 | tf_op jit(solution)/shard_map/apr,tcri->tacpi/dot_general | solution.py:110
  91.6 0.9 slice-done.1
  92.6 2.1 %fusion.8 = f32[128,128,1,1]{1,0,3,2:T(8,128)S(1)} fusion(bf16[65,2,128,192]{2,0,1,3:T(8,128)(2,1)S(1)} %bitcast.116, bf16[65,2,128,192]{2,3,0,1:T(8,128)(2,1)S(1)} %convert_bitcast_fusion.2), kind=kOutput, calls=%fused_computation.7 | convolution fusion | flops 817889280 | bytes 12845056 | tf_op jit(solution)/shard_map/tacpi,acqi->tpq/dot_general | solution.py:113
  94.7 15.5 %all_to_all.29 = f32[1,128,128]{2,0,1:T(1,128)S(1)} all-to-all(f32[1,128,128]{2,0,1:T(1,128)S(1)} %bitcast.126), channel_id=1, replica_groups=mesh['tile'=64,'kern'=16] {'kern'}, dimensions={1} | all-to-all | bytes 131072 | tf_op jit(solution)/shard_map/all_to_all | solution.py:79
  110.1 0.6 reduce_sum.32
  (47 shorter events, 1.4 us)
Async XLA Ops:
  1.3 34.7 %collective-permute-start = (bf16[1,1,32,128]{3,2,1,0:T(8,128)(2,1)S(1)}, bf16[1,1,32,128]{3,2,1,0:T(8,128)(2,1)S(1)}, u32[]{:S(2)}, u32[]{:S(2)}) collective-permute-start(bf16[1,1,32,128]{3,2,1,0:T(8,128)(2,1)S(1)} %get-tuple-element.14), channel_id=1, source_target_pairs={{0,16},{16,32},{32,48},{48,64},{64,80},{80,96},{96,112},{112,128},... | collective-permute-start | bytes 24584 | tf_op jit(solution)/shard_map/ppermute | solution.py:17
  5.3 31.0 %collective-permute-start.1 = (bf16[1,1,32,128]{3,2,1,0:T(8,128)(2,1)S(1)}, bf16[1,1,32,128]{3,2,1,0:T(8,128)(2,1)S(1)}, u32[]{:S(2)}, u32[]{:S(2)}) collective-permute-start(bf16[1,1,32,128]{3,2,1,0:T(8,128)(2,1)S(1)} %get-tuple-element.15), channel_id=1, source_target_pairs={{16,0},{32,16},{48,32},{64,48},{80,64},{96,80},{112,96},{128,112},... | collective-permute-start | bytes 24584 | tf_op jit(solution)/shard_map/ppermute | solution.py:18
  36.6 17.9 %copy-start = (bf16[2,1,65,65]{3,0,2,1:T(2,128)(2,1)S(1)}, bf16[2,1,65,65]{3,0,2,1:T(2,128)(2,1)}, u32[]{:S(2)}) copy-start(bf16[2,1,65,65]{3,0,2,1:T(2,128)(2,1)} %param.6) | copy-start | bytes 50704
  44.0 20.7 %all-to-all-start = ((f32[1,128,128]{2,0,1:T(1,128)}), f32[1,128,128]{2,0,1:T(1,128)S(1)}, u32[]{:S(2)}, u32[]{:S(2)}) async-start(f32[1,128,128]{2,0,1:T(1,128)} %copy.33), calls=%async_computation | async-start | bytes 131072 | tf_op jit(solution)/shard_map/all_to_all | solution.py:79
  66.6 13.7 %all-to-all-start.1 = ((f32[16,8,128]{2,1,0:T(8,128)}), f32[16,8,128]{2,1,0:T(8,128)S(1)}, u32[]{:S(2)}, u32[]{:S(2)}) async-start(f32[16,8,128]{2,1,0:T(8,128)} %broadcast_in_dim.95), calls=%async_computation.1 | async-start | bytes 131072 | tf_op jit(solution)/shard_map/all_to_all | solution.py:86
  80.7 7.6 %collective-permute-start.2 = (bf16[1,1,2,32,128]{3,4,2,1,0:T(8,128)(2,1)S(1)}, bf16[1,1,2,32,128]{3,4,2,1,0:T(8,128)(2,1)S(1)}, u32[]{:S(2)}, u32[]{:S(2)}) collective-permute-start(bf16[1,1,2,32,128]{3,4,2,1,0:T(8,128)(2,1)S(1)} %get-tuple-element.7), channel_id=1, source_target_pairs={{0,16},{16,32},{32,48},{48,64},{64,80},{80,96},{96,112},{112,128},... | collective-permute-start | bytes 49160 | tf_op jit(solution)/shard_map/ppermute | solution.py:17
  82.7 6.8 %collective-permute-start.3 = (bf16[1,1,2,32,128]{3,4,2,1,0:T(8,128)(2,1)S(1)}, bf16[1,1,2,32,128]{3,4,2,1,0:T(8,128)(2,1)S(1)}, u32[]{:S(2)}, u32[]{:S(2)}) collective-permute-start(bf16[1,1,2,32,128]{3,4,2,1,0:T(8,128)(2,1)S(1)} %get-tuple-element.8), channel_id=1, source_target_pairs={{16,0},{32,16},{48,32},{64,48},{80,64},{96,80},{112,96},{128,112},... | collective-permute-start | bytes 49160 | tf_op jit(solution)/shard_map/ppermute | solution.py:18
  89.5 2.2 %slice-start = ((s8[7077888]{0:T(1024)(128)(4,1)}), s8[4194304]{0:T(1024)(128)(4,1)S(1)}, s32[]{:S(2)}) async-start(s8[7077888]{0:T(1024)(128)(4,1)} %bitcast.115), calls=%async_computation.3 | async-start | bytes 8388608
  89.5 3.1 %slice-start.1 = ((s8[7077888]{0:T(1024)(128)(4,1)}), s8[2883584]{0:T(1024)(128)(4,1)S(1)}, s32[]{:S(2)}) async-start(s8[7077888]{0:T(1024)(128)(4,1)} %bitcast.115), calls=%async_computation.4 | async-start | bytes 5767168

commit v4 on v3

v4 whole, which is shorter than its diff:
```python
import jax
import jax.numpy as jnp
from jax import lax
from jax.sharding import PartitionSpec as P

steepness = 8.0
threshold = 0.5


def banded(taps, width_in, width_out):
    tap_count = taps.shape[2]
    shape = (tap_count, width_out, width_in)
    along = lax.broadcasted_iota(jnp.int32, shape, 0)
    row = lax.broadcasted_iota(jnp.int32, shape, 1)
    col = lax.broadcasted_iota(jnp.int32, shape, 2)
    select = (col - row == along).astype(taps.dtype)
    band = jnp.einsum(
        "acb,bji->acji", taps.transpose(1, 0, 2), select, preferred_element_type=jnp.float32
    )
    return band.astype(taps.dtype)


def scatter_sum(value, axis, dim):
    pieces = lax.all_to_all(value, axis, dim, 0, tiled=True)
    return jnp.sum(pieces, axis=0, keepdims=True)


def shifted_rows(images, tap_count, rows_out):
    rows_in = images.shape[-2]
    shape = (tap_count, rows_out, rows_in)
    along = lax.broadcasted_iota(jnp.int32, shape, 0)
    row = lax.broadcasted_iota(jnp.int32, shape, 1)
    source = lax.broadcasted_iota(jnp.int32, shape, 2)
    return (source - row == along).astype(images.dtype)


def correlate_forward(images, band, rows_out):
    select = shifted_rows(images, band.shape[0], rows_out)
    stacked = jnp.einsum(
        "apr,tri->tapi", select, images, preferred_element_type=jnp.float32
    ).astype(images.dtype)
    total = jnp.einsum("tapi,acqi->tcpq", stacked, band, preferred_element_type=jnp.float32)
    return total


def correlate_adjoint(images, band, rows_out):
    select = shifted_rows(images, band.shape[0], rows_out)
    stacked = jnp.einsum(
        "apr,tcri->tacpi", select, images, preferred_element_type=jnp.float32
    ).astype(images.dtype)
    return jnp.einsum("tacpi,acqi->tpq", stacked, band, preferred_element_type=jnp.float32)


def halo_rows(rows, direction):
    devices = lax.axis_size("tile")
    up = [(i, i + 1) for i in range(devices - 1)]
    pairs = up if direction == "up" else [(j, i) for i, j in up]
    return lax.ppermute(rows, "tile", pairs)


def by_block(own, halo, blocks):
    own_rows = own.shape[-2] // blocks
    halo_rows_each = halo.shape[-2] // blocks
    lead = own.shape[:-2]
    own_split = own.reshape(lead + (blocks, own_rows, own.shape[-1]))
    halo_split = halo.reshape(lead + (blocks, halo_rows_each, halo.shape[-1]))
    return jnp.concatenate([own_split, halo_split], axis=-2)


def shards(mask, kernels, weights, target, neighbours):
    tile_side = mask.shape[1]
    local_kernels = kernels.shape[1]
    tap_count = kernels.shape[2]
    half_width = (tap_count - 1) // 2
    reach = 2 * half_width
    kern_count = lax.axis_size("kern")
    kern_place = lax.axis_index("kern")
    share_rows = tile_side // kern_count
    width_in = tile_side + 2 * half_width
    rows_field = tile_side + 2 * half_width

    north_present = (neighbours[:, 1] >= 0).astype(jnp.float32)[:, None, None]
    south_present = (neighbours[:, 6] >= 0).astype(jnp.float32)[:, None, None]
    to_south = jnp.concatenate(
        [mask[:, tile_side - reach :], target[:, tile_side - half_width :]], axis=1
    )
    to_north = jnp.concatenate([mask[:, :reach], target[:, :half_width]], axis=1)
    north_pack = halo_rows(to_south, "up")
    south_pack = halo_rows(to_north, "down")
    north_mask, north_target = north_pack[:, :reach], north_pack[:, reach:]
    south_mask, south_target = south_pack[:, :reach], south_pack[:, reach:]
    north_mask = (north_mask.astype(jnp.float32) * north_present).astype(mask.dtype)
    south_mask = (south_mask.astype(jnp.float32) * south_present).astype(mask.dtype)
    image = jnp.concatenate([north_mask, mask, south_mask], axis=1)
    image = jnp.pad(image, ((0, 0), (0, 0), (half_width, half_width)))

    taps = kernels.reshape(2 * local_kernels, tap_count, tap_count)
    forward_band = banded(taps, width_in, tile_side)
    fields = correlate_forward(image, forward_band, rows_field)
    doubled = jnp.concatenate([weights, weights])
    partial_sum = jnp.sum(doubled[None, :, None, None] * fields * fields, axis=1)[0]

    def own_and_halo(values):
        own = values[..., half_width : half_width + tile_side, :]
        halo = jnp.concatenate(
            [values[..., :half_width, :], values[..., half_width + tile_side :, :]], axis=-2
        )
        return own, halo

    pieces = by_block(*own_and_halo(partial_sum), kern_count)
    intensity = jnp.sum(lax.all_to_all(pieces, "kern", 0, 0, tiled=True), axis=0)
    resist_block = jax.nn.sigmoid(steepness * (intensity - threshold))
    target_rows = jnp.concatenate(
        [north_target[0], target[0], south_target[0]], axis=0
    ).astype(jnp.float32)
    target_pieces = by_block(*own_and_halo(target_rows), kern_count)
    own_target = lax.dynamic_index_in_dim(target_pieces, kern_place, 0, keepdims=False)
    own_sensitivity = (
        2.0
        * (resist_block - own_target)
        * steepness
        * resist_block
        * (1.0 - resist_block)
    )
    copies = jnp.broadcast_to(own_sensitivity, (kern_count,) + own_sensitivity.shape)
    gathered = lax.all_to_all(copies, "kern", 0, 0, tiled=True)
    sens_own = gathered[:, :share_rows].reshape(tile_side, tile_side)
    sens_halo = gathered[:, share_rows:].reshape(2 * half_width, tile_side)
    sens_north = sens_halo[:half_width] * north_present[0]
    sens_south = sens_halo[half_width:] * south_present[0]
    sensitivity = jnp.concatenate([sens_north, sens_own, sens_south], axis=0)
    scaled = (2.0 * doubled)[None, :, None, None] * sensitivity[None, None] * fields
    adjoint_source = scaled.astype(jnp.bfloat16)
    source_ext = jnp.pad(adjoint_source, ((0, 0), (0, 0), (0, 0), (half_width, half_width)))
    adjoint_band = banded(taps[:, ::-1, ::-1], width_in, tile_side)
    gradient_term = correlate_adjoint(source_ext, adjoint_band, tile_side)
    gradient = scatter_sum(gradient_term, "kern", 1)
    resist = resist_block[None, :share_rows]
    return (gradient, resist)


def solution(mesh):
    in_specs = (
        P("tile", None, None),
        P(None, "kern", None, None),
        P("kern"),
        P("tile", None, None),
        P("tile", None),
    )
    out_specs = (P("tile", "kern", None), P("tile", "kern", None))
    return jax.shard_map(shards, mesh=mesh, in_specs=in_specs, out_specs=out_specs, check_vma=False)
```

time: 111 us -> 103 us (0.928)
  blocking collectives: 15.5 us -> 0 us
  waiting for transfers between devices: 16 us -> 29.9 us
  between operations: 6.62 us -> 2.8 us
  starting transfers between devices: 41.6 us -> 38.2 us
    all_to_all x1 -> x2, waiting for transfers between devices: 5.01 us -> 20.7 us  [the longest x1 11.4 us: shards(): lax.all_to_all(pieces, 'kern', 0, 0, tiled=True)]
    all_to_all x1 -> x0, blocking collectives: 15.5 us -> none  [scatter_sum(): pieces = lax.all_to_all(value, axis, dim, 0, tiled=True)]
    all_to_all x1 -> x2, starting transfers between devices: 3.8 us -> 14.5 us  [the longest x1 10.5 us: shards(): lax.all_to_all(pieces, 'kern', 0, 0, tiled=True)]
    ppermute x4 -> x2, starting transfers between devices: 27.3 us -> 19.8 us  [halo_rows(): return lax.ppermute(rows, 'tile', pairs)]
    all_to_all x1, starting transfers between devices: 10.5 us -> 4.02 us  [scatter_sum(): pieces = lax.all_to_all(value, axis, dim, 0, tiled=True)]
    broadcast_in_dim x1 -> x0, other arithmetic: 1.29 us -> none  [gather_blocks(): copies = jnp.broadcast_to(block, (devices,) + block.shape[1:])]
  transfers between devices with their start and end apart: 6 -> 5, of which waited for: 3 -> 3; matrix products, arithmetic and copies ran while one was open for 13% -> 14% of each run, Pallas kernels for 0% -> 0%
where the time goes in v4:
time: 103 us; the launch traced here: 102 us
  starting transfers between devices  38.2 us (37%)
  waiting for transfers between devices  29.9 us (29%)
  matrix products  22.3 us (22%)
  local copies, waits for them, and re-layouts  6.02 us (6%)
  other arithmetic  2.83 us (3%)
  between operations  2.8 us (3%)
    ppermute x2, starting transfers between devices, halo_rows(): return lax.ppermute(rows, 'tile', pairs)  19.8 us
    all_to_all x1, waiting for transfers between devices, shards(): lax.all_to_all(pieces, 'kern', 0, 0, tiled=True)  11.4 us
    dot_general x2, matrix products, banded(): jnp.einsum('acb,bji->acji', taps.transpose(1, 0, 2), select, preferred_el...  10.6 us
    all_to_all x1, starting transfers between devices, shards(): lax.all_to_all(pieces, 'kern', 0, 0, tiled=True)  10.5 us
    all_to_all x1, waiting for transfers between devices, shards(): gathered = lax.all_to_all(copies, 'kern', 0, 0, tiled=True)  9.25 us
    all_to_all x1, waiting for transfers between devices, scatter_sum(): pieces = lax.all_to_all(value, axis, dim, 0, tiled=True)  9.19 us
    dot_general x1, matrix products, correlate_forward(): jnp.einsum('tapi,acqi->tcpq', stacked, band, preferred_element_type=jnp.f...  7.01 us
    all_to_all x1, starting transfers between devices, scatter_sum(): pieces = lax.all_to_all(value, axis, dim, 0, tiled=True)  4.02 us
  transfers between devices with their start and end apart: 5, of which 3 were waited for; matrix products, arithmetic and copies ran while one was open for 14% of the time, Pallas kernels for 0%

profile of v4, /device:TPU:9, one launch (start us, length us, event | category | flops | bytes accessed | tf_op | source)
XLA Modules:
  0.0 102.1 jit_solution(6910815000839704453)
XLA Ops:
  0.6 0.9 copy.45
  1.6 0.7 fusion.72
  2.3 0.1 copy.71
  2.5 17.8 %collective-permute-start.1 = (bf16[1,96,128]{1,2,0:T(8,128)(2,1)S(1)}, bf16[1,96,128]{1,2,0:T(8,128)(2,1)S(1)}, u32[]{:S(2)}, u32[]{:S(2)}) collective-permute-start(bf16[1,96,128]{1,2,0:T(8,128)(2,1)S(1)} %pad_maximum_fusion.3), channel_id=1, source_target_pairs={{16,0},{32,16},{48,32},{64,48},{80,64},{96,80},{112,96},{128,112},... | collective-permute-start | bytes 73736 | tf_op jit(solution)/shard_map/ppermute | solution.py:58
  20.6 1.9 %collective-permute-start = (bf16[1,96,128]{1,2,0:T(8,128)(2,1)S(1)}, bf16[1,96,128]{1,2,0:T(8,128)(2,1)S(1)}, u32[]{:S(2)}, u32[]{:S(2)}) collective-permute-start(bf16[1,96,128]{1,2,0:T(8,128)(2,1)S(1)} %pad_maximum_fusion.2), channel_id=1, source_target_pairs={{0,16},{16,32},{32,48},{48,64},{64,80},{80,96},{96,112},{112,128},... | collective-permute-start | bytes 73736 | tf_op jit(solution)/shard_map/ppermute | solution.py:58
  22.5 1.3 %fusion.73 = (s32[1,1]{1,0:T(1,128)}, s32[1,1]{1,0:T(1,128)}) fusion(s32[1,8]{1,0:T(1,128)} %param.9), kind=kLoop, calls=%fused_computation.83 | loop fusion | bytes 16 | tf_op jit(solution)/shard_map/slice | solution.py:82
  24.5 5.7 %convert_bitcast_fusion.1 = bf16[65,2,128,192]{2,0,1,3:T(8,128)(2,1)} fusion(bf16[65,2,65]{2,1,0:T(2,128)(2,1)} %bitcast.115), kind=kOutput, calls=%fused_computation.3 | convolution fusion | flops 421724160 | bytes 6406660 | tf_op jit(solution)/shard_map/acb,bji->acji/dot_general | solution.py:17
  30.2 0.2 rev.3
  30.4 4.9 %convert_bitcast_fusion = bf16[65,2,128,192]{2,0,1,3:T(8,128)(2,1)} fusion(bf16[65,2,65]{2,1,0:T(2,128)(2,1)S(1)} %bitcast.117), kind=kOutput, calls=%fused_computation.2 | convolution fusion | flops 421724160 | bytes 6406660 | tf_op jit(solution)/shard_map/acb,bji->acji/dot_general | solution.py:17
  36.7 7.0 %fusion.26 = (f32[192,128]{1,0:T(8,128)S(1)}, f32[1,2,192,128]{3,2,1,0:T(8,128)S(1)}) fusion(f32[2]{0:T(128)S(1)} %pad_maximum_fusion.6, bf16[1,64,128]{1,2,0:T(8,128)(2,1)S(1)} %multiply_convert_fusion.1, bf16[1,128,128]{1,2,0:T(8,128)(2,1)S(1)} %copy.45, bf16[1,64,128]{1,2,0:T(8,128)(2,1)S(1)} %multiply_convert_fusion.2, ...), kind=kOutput, calls=%fused_computation.24 | convolution fusion | flops 2463166464 | bytes 6750216 | tf_op jit(solution)/shard_map/tapi,acqi->tcpq/dot_general | solution.py:42
  44.2 0.7 pad_maximum_fusion
  44.8 10.5 %all-to-all-start = ((f32[16,12,128]{2,1,0:T(8,128)}), f32[16,12,128]{2,1,0:T(8,128)S(1)}, u32[]{:S(2)}, u32[]{:S(2)}) async-start(f32[16,12,128]{2,1,0:T(8,128)} %pad_maximum_fusion), calls=%async_computation | async-start | bytes 262144 | tf_op jit(solution)/shard_map/all_to_all | solution.py:111
  55.4 11.4 %all-to-all-done = f32[16,12,128]{2,1,0:T(8,128)S(1)} async-done(((f32[16,12,128]{2,1,0:T(8,128)}), f32[16,12,128]{2,1,0:T(8,128)S(1)}, u32[]{:S(2)}, u32[]{:S(2)}) %all-to-all-start) | async-done | bytes 98336 | tf_op jit(solution)/shard_map/all_to_all | solution.py:111
  66.9 0.7 broadcast_in_dim.6
  67.5 4.0 %all-to-all-start.1 = ((f32[16,12,128]{2,1,0:T(8,128)}), f32[16,12,128]{2,1,0:T(8,128)S(1)}, u32[]{:S(2)}, u32[]{:S(2)}) async-start(f32[16,12,128]{2,1,0:T(8,128)} %broadcast_in_dim.6), calls=%async_computation.1 | async-start | bytes 262144 | tf_op jit(solution)/shard_map/all_to_all | solution.py:126
  71.5 1.0 iota_compare_fusion.2
  72.6 9.2 %all-to-all-done.1 = f32[16,12,128]{2,1,0:T(8,128)S(1)} async-done(((f32[16,12,128]{2,1,0:T(8,128)}), f32[16,12,128]{2,1,0:T(8,128)S(1)}, u32[]{:S(2)}, u32[]{:S(2)}) %all-to-all-start.1) | async-done | bytes 98336 | tf_op jit(solution)/shard_map/all_to_all | solution.py:126
  82.0 2.0 %convert_bitcast_fusion.2 = bf16[65,2,128,192]{2,3,0,1:T(8,128)(2,1)S(1)} fusion(pred[65,128,192]{1,0,2:T(8,128)(4,1)S(1)} %iota_compare_fusion.2, bf16[1,2,192,128]{3,2,1,0:T(8,128)(2,1)S(1)} %multiply_convert_fusion), kind=kOutput, calls=%fused_computation.16 | convolution fusion | flops 1230028800 | bytes 8085504 | tf_op jit(solution)/shard_map/apr,tcri->tacpi/dot_general | solution.py:48
  84.0 0.9 slice-done.1
  85.0 2.7 %fusion.12 = f32[128,128,1,1]{1,0,3,2:T(8,128)} fusion(bf16[65,2,128,192]{2,0,1,3:T(8,128)(2,1)S(1)} %bitcast.111, bf16[65,2,128,192]{2,3,0,1:T(8,128)(2,1)S(1)} %convert_bitcast_fusion.2), kind=kOutput, calls=%fused_computation.12 | convolution fusion | flops 817889280 | bytes 12845056 | tf_op jit(solution)/shard_map/tacpi,acqi->tpq/dot_general | solution.py:51
  87.7 4.0 %all-to-all-start.2 = ((f32[1,128,128]{2,0,1:T(1,128)}), f32[1,128,128]{2,0,1:T(1,128)S(1)}, u32[]{:S(2)}, u32[]{:S(2)}) async-start(f32[1,128,128]{2,0,1:T(1,128)} %bitcast.45), calls=%async_computation.2 | async-start | bytes 131072 | tf_op jit(solution)/shard_map/all_to_all | solution.py:24
  91.7 0.6 slice_bitcast_fusion.7
  92.3 9.2 %all-to-all-done.2 = f32[1,128,128]{2,0,1:T(1,128)S(1)} async-done(((f32[1,128,128]{2,0,1:T(1,128)}), f32[1,128,128]{2,0,1:T(1,128)S(1)}, u32[]{:S(2)}, u32[]{:S(2)}) %all-to-all-start.2) | async-done | bytes 65568 | tf_op jit(solution)/shard_map/all_to_all | solution.py:24
  101.5 0.6 reduce_sum.32
  (35 shorter events, 1.2 us)
Async XLA Ops:
  0.6 29.6 %copy-start.1 = (bf16[2,1,65,65]{3,0,2,1:T(2,128)(2,1)S(1)}, bf16[2,1,65,65]{3,0,2,1:T(2,128)(2,1)}, u32[]{:S(2)}) copy-start(bf16[2,1,65,65]{3,0,2,1:T(2,128)(2,1)} %param.6) | copy-start | bytes 50704
  2.5 34.1 %collective-permute-start.1 = (bf16[1,96,128]{1,2,0:T(8,128)(2,1)S(1)}, bf16[1,96,128]{1,2,0:T(8,128)(2,1)S(1)}, u32[]{:S(2)}, u32[]{:S(2)}) collective-permute-start(bf16[1,96,128]{1,2,0:T(8,128)(2,1)S(1)} %pad_maximum_fusion.3), channel_id=1, source_target_pairs={{16,0},{32,16},{48,32},{64,48},{80,64},{96,80},{112,96},{128,112},... | collective-permute-start | bytes 73736 | tf_op jit(solution)/shard_map/ppermute | solution.py:58
  20.6 16.1 %collective-permute-start = (bf16[1,96,128]{1,2,0:T(8,128)(2,1)S(1)}, bf16[1,96,128]{1,2,0:T(8,128)(2,1)S(1)}, u32[]{:S(2)}, u32[]{:S(2)}) collective-permute-start(bf16[1,96,128]{1,2,0:T(8,128)(2,1)S(1)} %pad_maximum_fusion.2), channel_id=1, source_target_pairs={{0,16},{16,32},{32,48},{48,64},{64,80},{80,96},{96,112},{112,128},... | collective-permute-start | bytes 73736 | tf_op jit(solution)/shard_map/ppermute | solution.py:58
  36.7 7.4 %copy-start = (bf16[1,128,128]{2,1,0:T(8,128)(2,1)S(1)}, bf16[1,128,128]{2,1,0:T(8,128)(2,1)}, u32[]{:S(2)}) copy-start(bf16[1,128,128]{2,1,0:T(8,128)(2,1)} %param.8) | copy-start | bytes 98308
  44.8 22.0 %all-to-all-start = ((f32[16,12,128]{2,1,0:T(8,128)}), f32[16,12,128]{2,1,0:T(8,128)S(1)}, u32[]{:S(2)}, u32[]{:S(2)}) async-start(f32[16,12,128]{2,1,0:T(8,128)} %pad_maximum_fusion), calls=%async_computation | async-start | bytes 262144 | tf_op jit(solution)/shard_map/all_to_all | solution.py:111
  67.5 14.3 %all-to-all-start.1 = ((f32[16,12,128]{2,1,0:T(8,128)}), f32[16,12,128]{2,1,0:T(8,128)S(1)}, u32[]{:S(2)}, u32[]{:S(2)}) async-start(f32[16,12,128]{2,1,0:T(8,128)} %broadcast_in_dim.6), calls=%async_computation.1 | async-start | bytes 262144 | tf_op jit(solution)/shard_map/all_to_all | solution.py:126
  81.8 2.2 %slice-start = ((s8[7077888]{0:T(1024)(128)(4,1)}), s8[4194304]{0:T(1024)(128)(4,1)S(1)}, s32[]{:S(2)}) async-start(s8[7077888]{0:T(1024)(128)(4,1)} %bitcast.110), calls=%async_computation.3 | async-start | bytes 8388608
  82.0 3.0 %slice-start.1 = ((s8[7077888]{0:T(1024)(128)(4,1)}), s8[2883584]{0:T(1024)(128)(4,1)S(1)}, s32[]{:S(2)}) async-start(s8[7077888]{0:T(1024)(128)(4,1)} %bitcast.110), calls=%async_computation.4 | async-start | bytes 5767168
  87.7 13.8 %all-to-all-start.2 = ((f32[1,128,128]{2,0,1:T(1,128)}), f32[1,128,128]{2,0,1:T(1,128)S(1)}, u32[]{:S(2)}, u32[]{:S(2)}) async-start(f32[1,128,128]{2,0,1:T(1,128)} %bitcast.45), calls=%async_computation.2 | async-start | bytes 131072 | tf_op jit(solution)/shard_map/all_to_all | solution.py:24

commit v5 on v4

--- a/solution.py
+++ b/solution.py
@@ -58,15 +58,6 @@
     return lax.ppermute(rows, "tile", pairs)
 
 
-def by_block(own, halo, blocks):
-    own_rows = own.shape[-2] // blocks
-    halo_rows_each = halo.shape[-2] // blocks
-    lead = own.shape[:-2]
-    own_split = own.reshape(lead + (blocks, own_rows, own.shape[-1]))
-    halo_split = halo.reshape(lead + (blocks, halo_rows_each, halo.shape[-1]))
-    return jnp.concatenate([own_split, halo_split], axis=-2)
-
-
 def shards(mask, kernels, weights, target, neighbours):
     tile_side = mask.shape[1]
     local_kernels = kernels.shape[1]
@@ -100,42 +91,31 @@
     doubled = jnp.concatenate([weights, weights])
     partial_sum = jnp.sum(doubled[None, :, None, None] * fields * fields, axis=1)[0]
 
-    def own_and_halo(values):
-        own = values[..., half_width : half_width + tile_side, :]
-        halo = jnp.concatenate(
-            [values[..., :half_width, :], values[..., half_width + tile_side :, :]], axis=-2
-        )
-        return own, halo
-
-    pieces = by_block(*own_and_halo(partial_sum), kern_count)
-    intensity = jnp.sum(lax.all_to_all(pieces, "kern", 0, 0, tiled=True), axis=0)
-    resist_block = jax.nn.sigmoid(steepness * (intensity - threshold))
+    copies = jnp.broadcast_to(partial_sum, (kern_count,) + partial_sum.shape)
+    intensity = jnp.sum(lax.all_to_all(copies, "kern", 0, 0, tiled=True), axis=0)
+    resist_rows = jax.nn.sigmoid(steepness * (intensity - threshold))
     target_rows = jnp.concatenate(
         [north_target[0], target[0], south_target[0]], axis=0
     ).astype(jnp.float32)
-    target_pieces = by_block(*own_and_halo(target_rows), kern_count)
-    own_target = lax.dynamic_index_in_dim(target_pieces, kern_place, 0, keepdims=False)
-    own_sensitivity = (
-        2.0
-        * (resist_block - own_target)
-        * steepness
-        * resist_block
-        * (1.0 - resist_block)
+    rows_sensitivity = (
+        2.0 * (resist_rows - target_rows) * steepness * resist_rows * (1.0 - resist_rows)
     )
-    copies = jnp.broadcast_to(own_sensitivity, (kern_count,) + own_sensitivity.shape)
-    gathered = lax.all_to_all(copies, "kern", 0, 0, tiled=True)
-    sens_own = gathered[:, :share_rows].reshape(tile_side, tile_side)
-    sens_halo = gathered[:, share_rows:].reshape(2 * half_width, tile_side)
-    sens_north = sens_halo[:half_width] * north_present[0]
-    sens_south = sens_halo[half_width:] * south_present[0]
-    sensitivity = jnp.concatenate([sens_north, sens_own, sens_south], axis=0)
+    row_index = lax.broadcasted_iota(jnp.int32, (rows_field, 1), 0)
+    present = jnp.where(
+        row_index < half_width,
+        north_present[0],
+        jnp.where(row_index >= half_width + tile_side, south_present[0], 1.0),
+    )
+    sensitivity = rows_sensitivity * present
     scaled = (2.0 * doubled)[None, :, None, None] * sensitivity[None, None] * fields
     adjoint_source = scaled.astype(jnp.bfloat16)
     source_ext = jnp.pad(adjoint_source, ((0, 0), (0, 0), (0, 0), (half_width, half_width)))
     adjoint_band = banded(taps[:, ::-1, ::-1], width_in, tile_side)
     gradient_term = correlate_adjoint(source_ext, adjoint_band, tile_side)
     gradient = scatter_sum(gradient_term, "kern", 1)
-    resist = resist_block[None, :share_rows]
+    resist = lax.dynamic_slice_in_dim(
+        resist_rows, half_width + kern_place * share_rows, share_rows, 0
+    )[None]
     return (gradient, resist)
 
 

time: 103 us -> 115 us (1.12)
  waiting for transfers between devices: 29.9 us -> 44.9 us
  starting transfers between devices: 38.2 us -> 34.5 us
    all_to_all x2 -> x1, waiting for transfers between devices: 20.7 us -> 35.7 us  [shards(): lax.all_to_all(copies, 'kern', 0, 0, tiled=True)]
    all_to_all x2 -> x1, starting transfers between devices: 14.5 us -> 10.7 us  [shards(): lax.all_to_all(copies, 'kern', 0, 0, tiled=True)]
  transfers between devices with their start and end apart: 5 -> 4, of which waited for: 3 -> 2; matrix products, arithmetic and copies ran while one was open for 14% -> 13% of each run, Pallas kernels for 0% -> 0%
where the time goes in v5:
time: 115 us; the launch traced here: 114 us
  waiting for transfers between devices  44.9 us (39%)
  starting transfers between devices  34.5 us (30%)
  matrix products  23.1 us (20%)
  local copies, waits for them, and re-layouts  5.92 us (5%)
  other arithmetic  3.33 us (3%)
  between operations  2.74 us (2%)
    all_to_all x1, waiting for transfers between devices, shards(): lax.all_to_all(copies, 'kern', 0, 0, tiled=True)  35.7 us
    ppermute x2, starting transfers between devices, halo_rows(): return lax.ppermute(rows, 'tile', pairs)  19.8 us
    all_to_all x1, starting transfers between devices, shards(): lax.all_to_all(copies, 'kern', 0, 0, tiled=True)  10.7 us
    dot_general x2, matrix products, banded(): jnp.einsum('acb,bji->acji', taps.transpose(1, 0, 2), select, preferred_el...  10.6 us
    all_to_all x1, waiting for transfers between devices, scatter_sum(): pieces = lax.all_to_all(value, axis, dim, 0, tiled=True)  9.19 us
    dot_general x1, matrix products, correlate_forward(): jnp.einsum('tapi,acqi->tcpq', stacked, band, preferred_element_type=jnp.f...  7.7 us
    all_to_all x1, starting transfers between devices, scatter_sum(): pieces = lax.all_to_all(value, axis, dim, 0, tiled=True)  4.11 us
    dot_general x1, matrix products, correlate_adjoint(): jnp.einsum('tacpi,acqi->tpq', stacked, band, preferred_element_type=jnp.f...  2.73 us
  transfers between devices with their start and end apart: 4, of which 2 were waited for; matrix products, arithmetic and copies ran while one was open for 13% of the time, Pallas kernels for 0%

profile of v5, /device:TPU:9, one launch (start us, length us, event | category | flops | bytes accessed | tf_op | source)
XLA Modules:
  0.0 114.4 jit_solution(6174800694020783413)
XLA Ops:
  0.6 0.9 copy.29
  1.6 0.7 fusion.68
  2.3 0.1 copy.53
  2.5 17.8 %collective-permute-start.1 = (bf16[1,96,128]{1,2,0:T(8,128)(2,1)S(1)}, bf16[1,96,128]{1,2,0:T(8,128)(2,1)S(1)}, u32[]{:S(2)}, u32[]{:S(2)}) collective-permute-start(bf16[1,96,128]{1,2,0:T(8,128)(2,1)S(1)} %pad_maximum_fusion.1), channel_id=1, source_target_pairs={{16,0},{32,16},{48,32},{64,48},{80,64},{96,80},{112,96},{128,112},... | collective-permute-start | bytes 73736 | tf_op jit(solution)/shard_map/ppermute | solution.py:58
  20.4 0.1 copy.52
  20.6 1.9 %collective-permute-start = (bf16[1,96,128]{1,2,0:T(8,128)(2,1)S(1)}, bf16[1,96,128]{1,2,0:T(8,128)(2,1)S(1)}, u32[]{:S(2)}, u32[]{:S(2)}) collective-permute-start(bf16[1,96,128]{1,2,0:T(8,128)(2,1)S(1)} %pad_maximum_fusion), channel_id=1, source_target_pairs={{0,16},{16,32},{32,48},{48,64},{64,80},{80,96},{96,112},{112,128},... | collective-permute-start | bytes 73736 | tf_op jit(solution)/shard_map/ppermute | solution.py:58
  22.5 1.3 %fusion.69 = (s32[1,1]{1,0:T(1,128)}, s32[1,1]{1,0:T(1,128)}) fusion(s32[1,8]{1,0:T(1,128)} %param.9), kind=kLoop, calls=%fused_computation.65 | loop fusion | bytes 16 | tf_op jit(solution)/shard_map/slice | solution.py:73
  24.5 5.7 %convert_bitcast_fusion.1 = bf16[65,2,128,192]{2,0,1,3:T(8,128)(2,1)} fusion(bf16[65,2,65]{2,1,0:T(2,128)(2,1)} %bitcast.90), kind=kOutput, calls=%fused_computation.3 | convolution fusion | flops 421724160 | bytes 6406660 | tf_op jit(solution)/shard_map/acb,bji->acji/dot_general | solution.py:17
  31.6 7.7 %fusion.26 = (f32[192,128]{1,0:T(8,128)S(1)}, f32[1,2,192,128]{3,2,1,0:T(8,128)}) fusion(f32[2]{0:T(128)S(1)} %pad_maximum_fusion.2, bf16[1,64,128]{1,2,0:T(8,128)(2,1)S(1)} %multiply_convert_fusion.1, bf16[1,128,128]{1,2,0:T(8,128)(2,1)S(1)} %copy.29, bf16[1,64,128]{1,2,0:T(8,128)(2,1)S(1)} %multiply_convert_fusion.2, ...), kind=kOutput, calls=%fused_computation.24 | convolution fusion | flops 2463166464 | bytes 6750216 | tf_op jit(solution)/shard_map/tapi,acqi->tcpq/dot_general | solution.py:42
  39.3 1.4 %broadcast_in_dim.34 = f32[16,192,128]{2,1,0:T(8,128)} broadcast(f32[192,128]{1,0:T(8,128)S(1)} %get-tuple-element.10), dimensions={1,2} | broadcast | bytes 1671168 | tf_op jit(solution)/shard_map/broadcast_in_dim | solution.py:94
  40.7 10.7 %all-to-all-start = ((f32[16,192,128]{2,1,0:T(8,128)}), f32[16,192,128]{2,1,0:T(8,128)S(1)}, u32[]{:S(2)}, u32[]{:S(2)}) async-start(f32[16,192,128]{2,1,0:T(8,128)} %broadcast_in_dim.34), calls=%async_computation | async-start | bytes 3145728 | tf_op jit(solution)/shard_map/all_to_all | solution.py:95
  51.4 0.2 rev.3
  51.6 1.0 iota_compare_fusion.2
  52.6 4.9 %convert_bitcast_fusion = bf16[65,2,128,192]{2,0,1,3:T(8,128)(2,1)} fusion(bf16[65,2,65]{2,1,0:T(2,128)(2,1)S(1)} %bitcast.92), kind=kOutput, calls=%fused_computation.2 | convolution fusion | flops 421724160 | bytes 6406660 | tf_op jit(solution)/shard_map/acb,bji->acji/dot_general | solution.py:17
  57.7 0.1 slice_bitcast_fusion
  57.9 35.7 %all-to-all-done = f32[16,192,128]{2,1,0:T(8,128)S(1)} async-done(((f32[16,192,128]{2,1,0:T(8,128)}), f32[16,192,128]{2,1,0:T(8,128)S(1)}, u32[]{:S(2)}, u32[]{:S(2)}) %all-to-all-start) | async-done | bytes 1572896 | tf_op jit(solution)/shard_map/all_to_all | solution.py:95
  93.8 1.2 %multiply_convert_fusion = bf16[1,2,192,128]{3,2,1,0:T(8,128)(2,1)S(1)} fusion(f32[1,2,192,128]{3,2,1,0:T(8,128)} %get-tuple-element.11, f32[192,128]{1,0:T(8,128)S(1)} %get-tuple-element.3, f32[2]{0:T(128)S(1)} %broadcast_multiply_fusion), kind=kLoop, calls=%fused_computation.27 | loop fusion | flops 147456 | bytes 393224 | tf_op jit(solution)/shard_map/convert_element_type | solution.py:111
  95.0 2.0 %convert_bitcast_fusion.2 = bf16[65,2,128,192]{2,3,0,1:T(8,128)(2,1)S(1)} fusion(pred[65,128,192]{1,0,2:T(8,128)(4,1)S(1)} %iota_compare_fusion.2, bf16[1,2,192,128]{3,2,1,0:T(8,128)(2,1)S(1)} %multiply_convert_fusion), kind=kOutput, calls=%fused_computation.16 | convolution fusion | flops 1230028800 | bytes 8085504 | tf_op jit(solution)/shard_map/apr,tcri->tacpi/dot_general | solution.py:48
  97.0 0.2 slice-done.1
  97.2 2.7 %fusion.12 = f32[128,128,1,1]{1,0,3,2:T(8,128)} fusion(bf16[65,2,128,192]{2,0,1,3:T(8,128)(2,1)S(1)} %bitcast.88, bf16[65,2,128,192]{2,3,0,1:T(8,128)(2,1)S(1)} %convert_bitcast_fusion.2), kind=kOutput, calls=%fused_computation.12 | convolution fusion | flops 817889280 | bytes 12845056 | tf_op jit(solution)/shard_map/tacpi,acqi->tpq/dot_general | solution.py:51
  99.9 4.1 %all-to-all-start.1 = ((f32[1,128,128]{2,0,1:T(1,128)}), f32[1,128,128]{2,0,1:T(1,128)S(1)}, u32[]{:S(2)}, u32[]{:S(2)}) async-start(f32[1,128,128]{2,0,1:T(1,128)} %bitcast.34), calls=%async_computation.1 | async-start | bytes 131072 | tf_op jit(solution)/shard_map/all_to_all | solution.py:24
  104.0 0.6 dynamic-slice_bitcast_fusion
  104.6 9.2 %all-to-all-done.1 = f32[1,128,128]{2,0,1:T(1,128)S(1)} async-done(((f32[1,128,128]{2,0,1:T(1,128)}), f32[1,128,128]{2,0,1:T(1,128)S(1)}, u32[]{:S(2)}, u32[]{:S(2)}) %all-to-all-start.1) | async-done | bytes 65568 | tf_op jit(solution)/shard_map/all_to_all | solution.py:24
  113.8 0.6 reduce_sum.29
  (23 shorter events, 0.9 us)
Async XLA Ops:
  2.5 29.0 %collective-permute-start.1 = (bf16[1,96,128]{1,2,0:T(8,128)(2,1)S(1)}, bf16[1,96,128]{1,2,0:T(8,128)(2,1)S(1)}, u32[]{:S(2)}, u32[]{:S(2)}) collective-permute-start(bf16[1,96,128]{1,2,0:T(8,128)(2,1)S(1)} %pad_maximum_fusion.1), channel_id=1, source_target_pairs={{16,0},{32,16},{48,32},{64,48},{80,64},{96,80},{112,96},{128,112},... | collective-permute-start | bytes 73736 | tf_op jit(solution)/shard_map/ppermute | solution.py:58
  20.6 11.0 %collective-permute-start = (bf16[1,96,128]{1,2,0:T(8,128)(2,1)S(1)}, bf16[1,96,128]{1,2,0:T(8,128)(2,1)S(1)}, u32[]{:S(2)}, u32[]{:S(2)}) collective-permute-start(bf16[1,96,128]{1,2,0:T(8,128)(2,1)S(1)} %pad_maximum_fusion), channel_id=1, source_target_pairs={{0,16},{16,32},{32,48},{48,64},{64,80},{80,96},{96,112},{112,128},... | collective-permute-start | bytes 73736 | tf_op jit(solution)/shard_map/ppermute | solution.py:58
  31.6 19.7 %copy-start = (bf16[2,1,65,65]{3,0,2,1:T(2,128)(2,1)S(1)}, bf16[2,1,65,65]{3,0,2,1:T(2,128)(2,1)}, u32[]{:S(2)}) copy-start(bf16[2,1,65,65]{3,0,2,1:T(2,128)(2,1)} %param.6) | copy-start | bytes 50704
  40.7 53.0 %copy-start.1 = (bf16[1,128,128]{2,1,0:T(8,128)(2,1)S(1)}, bf16[1,128,128]{2,1,0:T(8,128)(2,1)}, u32[]{:S(2)}) copy-start(bf16[1,128,128]{2,1,0:T(8,128)(2,1)} %param.8) | copy-start | bytes 98308
  40.7 52.9 %all-to-all-start = ((f32[16,192,128]{2,1,0:T(8,128)}), f32[16,192,128]{2,1,0:T(8,128)S(1)}, u32[]{:S(2)}, u32[]{:S(2)}) async-start(f32[16,192,128]{2,1,0:T(8,128)} %broadcast_in_dim.34), calls=%async_computation | async-start | bytes 3145728 | tf_op jit(solution)/shard_map/all_to_all | solution.py:95
  93.8 3.2 %slice-start = ((s8[7077888]{0:T(1024)(128)(4,1)}), s8[4194304]{0:T(1024)(128)(4,1)S(1)}, s32[]{:S(2)}) async-start(s8[7077888]{0:T(1024)(128)(4,1)} %bitcast.87), calls=%async_computation.2 | async-start | bytes 8388608
  95.0 2.2 %slice-start.1 = ((s8[7077888]{0:T(1024)(128)(4,1)}), s8[2883584]{0:T(1024)(128)(4,1)S(1)}, s32[]{:S(2)}) async-start(s8[7077888]{0:T(1024)(128)(4,1)} %bitcast.87), calls=%async_computation.3 | async-start | bytes 5767168
  99.9 13.9 %all-to-all-start.1 = ((f32[1,128,128]{2,0,1:T(1,128)}), f32[1,128,128]{2,0,1:T(1,128)S(1)}, u32[]{:S(2)}, u32[]{:S(2)}) async-start(f32[1,128,128]{2,0,1:T(1,128)} %bitcast.34), calls=%async_computation.1 | async-start | bytes 131072 | tf_op jit(solution)/shard_map/all_to_all | solution.py:24

commit v6 on v4

--- a/solution.py
+++ b/solution.py
@@ -91,14 +91,28 @@
     south_mask, south_target = south_pack[:, :reach], south_pack[:, reach:]
     north_mask = (north_mask.astype(jnp.float32) * north_present).astype(mask.dtype)
     south_mask = (south_mask.astype(jnp.float32) * south_present).astype(mask.dtype)
-    image = jnp.concatenate([north_mask, mask, south_mask], axis=1)
-    image = jnp.pad(image, ((0, 0), (0, 0), (half_width, half_width)))
+    columns = ((0, 0), (0, 0), (half_width, half_width))
+    inner = jnp.pad(mask, columns)
+    edges = jnp.pad(
+        jnp.concatenate(
+            [
+                jnp.concatenate([north_mask, mask[:, : tile_side - reach]], axis=1),
+                jnp.concatenate([mask[:, reach:], south_mask], axis=1),
+            ],
+            axis=0,
+        ),
+        columns,
+    )
 
     taps = kernels.reshape(2 * local_kernels, tap_count, tap_count)
     forward_band = banded(taps, width_in, tile_side)
-    fields = correlate_forward(image, forward_band, rows_field)
+    inner_rows = tile_side - reach
+    middle = correlate_forward(inner, forward_band, inner_rows)
+    outer = correlate_forward(edges, forward_band, reach)
+    fields = jnp.concatenate([outer[:1], middle, outer[1:]], axis=2)
     doubled = jnp.concatenate([weights, weights])
     partial_sum = jnp.sum(doubled[None, :, None, None] * fields * fields, axis=1)[0]
+    flipped, partial_sum = lax.optimization_barrier((taps[:, ::-1, ::-1], partial_sum))
 
     def own_and_halo(values):
         own = values[..., half_width : half_width + tile_side, :]
@@ -132,7 +146,7 @@
     scaled = (2.0 * doubled)[None, :, None, None] * sensitivity[None, None] * fields
     adjoint_source = scaled.astype(jnp.bfloat16)
     source_ext = jnp.pad(adjoint_source, ((0, 0), (0, 0), (0, 0), (half_width, half_width)))
-    adjoint_band = banded(taps[:, ::-1, ::-1], width_in, tile_side)
+    adjoint_band = banded(flipped, width_in, tile_side)
     gradient_term = correlate_adjoint(source_ext, adjoint_band, tile_side)
     gradient = scatter_sum(gradient_term, "kern", 1)
     resist = resist_block[None, :share_rows]

time: 103 us -> 102 us (level)
  waiting for transfers between devices: 29.9 us -> 26 us
  local copies, waits for them, and re-layouts: 6.02 us -> 8.9 us
    all_to_all x1, waiting for transfers between devices: 9.25 us -> 5.46 us  [shards(): gathered = lax.all_to_all(copies, 'kern', 0, 0, tiled=True)]
    dot_general x2, matrix products: 10.6 us -> 7.63 us  [banded(): jnp.einsum('acb,bji->acji', taps.transpose(1, 0, 2), select, preferred_el...]
    unnamed x11 -> x13, local copies, waits for them, and re-layouts: 2.11 us -> 4.98 us
    dot_general x1 -> x2, matrix products: 7.01 us -> 8.62 us  [correlate_forward(): jnp.einsum('tapi,acqi->tcpq', stacked, band, preferred_element_type=jnp.f...]
  transfers between devices with their start and end apart: 5 -> 5, of which waited for: 3 -> 3; matrix products, arithmetic and copies ran while one was open for 14% -> 15% of each run, Pallas kernels for 0% -> 0%
where the time goes in v6:
time: 102 us; the launch traced here: 101 us
  starting transfers between devices  38.5 us (38%)
  waiting for transfers between devices  26 us (25%)
  matrix products  21.5 us (21%)
  local copies, waits for them, and re-layouts  8.9 us (9%)
  other arithmetic  3.28 us (3%)
  between operations  2.85 us (3%)
    ppermute x2, starting transfers between devices, halo_rows(): return lax.ppermute(rows, 'tile', pairs)  19.8 us
    all_to_all x1, waiting for transfers between devices, shards(): lax.all_to_all(pieces, 'kern', 0, 0, tiled=True)  11.4 us
    all_to_all x1, starting transfers between devices, shards(): lax.all_to_all(pieces, 'kern', 0, 0, tiled=True)  10.5 us
    all_to_all x1, waiting for transfers between devices, scatter_sum(): pieces = lax.all_to_all(value, axis, dim, 0, tiled=True)  9.14 us
    dot_general x2, matrix products, correlate_forward(): jnp.einsum('tapi,acqi->tcpq', stacked, band, preferred_element_type=jnp.f...  8.62 us
    dot_general x2, matrix products, banded(): jnp.einsum('acb,bji->acji', taps.transpose(1, 0, 2), select, preferred_el...  7.63 us
    all_to_all x1, waiting for transfers between devices, shards(): gathered = lax.all_to_all(copies, 'kern', 0, 0, tiled=True)  5.46 us
    unnamed x13, local copies, waits for them, and re-layouts  4.98 us
  transfers between devices with their start and end apart: 5, of which 3 were waited for; matrix products, arithmetic and copies ran while one was open for 15% of the time, Pallas kernels for 0%

profile of v6, /device:TPU:9, one launch (start us, length us, event | category | flops | bytes accessed | tf_op | source)
XLA Modules:
  0.0 101.1 jit_solution(9493387236114242416)
XLA Ops:
  0.6 0.7 fusion.98
  1.3 0.9 copy.43
  2.5 17.8 %collective-permute-start.1 = (bf16[1,96,128]{1,2,0:T(8,128)(2,1)S(1)}, bf16[1,96,128]{1,2,0:T(8,128)(2,1)S(1)}, u32[]{:S(2)}, u32[]{:S(2)}) collective-permute-start(bf16[1,96,128]{1,2,0:T(8,128)(2,1)S(1)} %pad_maximum_fusion.4), channel_id=1, source_target_pairs={{16,0},{32,16},{48,32},{64,48},{80,64},{96,80},{112,96},{128,112},... | collective-permute-start | bytes 73736 | tf_op jit(solution)/shard_map/ppermute | solution.py:58
  20.6 1.9 %collective-permute-start = (bf16[1,96,128]{1,2,0:T(8,128)(2,1)S(1)}, bf16[1,96,128]{1,2,0:T(8,128)(2,1)S(1)}, u32[]{:S(2)}, u32[]{:S(2)}) collective-permute-start(bf16[1,96,128]{1,2,0:T(8,128)(2,1)S(1)} %pad_maximum_fusion.3), channel_id=1, source_target_pairs={{0,16},{16,32},{32,48},{48,64},{64,80},{80,96},{96,112},{112,128},... | collective-permute-start | bytes 73736 | tf_op jit(solution)/shard_map/ppermute | solution.py:58
  22.9 1.0 iota_compare_fusion
  23.9 0.8 convert_bitcast_fusion.1
  25.4 1.3 %fusion.100 = (s32[1,1]{1,0:T(1,128)}, s32[1,1]{1,0:T(1,128)}) fusion(s32[1,8]{1,0:T(1,128)} %param.9), kind=kLoop, calls=%fused_computation.96 | loop fusion | bytes 16 | tf_op jit(solution)/shard_map/slice | solution.py:82
  26.7 2.8 %fusion.4 = bf16[128,192,65,2]{0,2,3,1:T(8,128)(2,1)S(1)} fusion(bf16[65,2,65]{2,1,0:T(2,128)(2,1)} %bitcast.129), kind=kOutput, calls=%fused_computation.5 | convolution fusion | flops 421724160 | bytes 6406660 | tf_op jit(solution)/shard_map/acb,bji->acji/dot_general | solution.py:17
  29.5 2.9 %copy-done = bf16[128,192,65,2]{0,2,3,1:T(8,128)(2,1)} copy-done((bf16[128,192,65,2]{0,2,3,1:T(8,128)(2,1)}, bf16[128,192,65,2]{0,2,3,1:T(8,128)(2,1)S(1)}, u32[]{:S(2)}) %copy-start) | copy-done | bytes 6389784
  32.4 2.5 %fusion.39 = f32[1,2,64,128]{3,2,0,1:T(8,128)S(1)} fusion(bf16[65,2,128,192]{2,0,1,3:T(8,128)(2,1)S(1)} %bitcast.122, bf16[65,64,192]{2,0,1:T(8,128)(2,1)S(1)} %convert_bitcast_fusion.1), kind=kOutput, calls=%fused_computation.28 | convolution fusion | flops 408944640 | bytes 8052736 | tf_op jit(solution)/shard_map/tapi,acqi->tcpq/dot_general | solution.py:42
  36.9 6.2 %fusion.32 = f32[2,2,64,128]{3,2,0,1:T(8,128)S(1)} fusion(pred[65,64,128]{2,0,1:T(8,128)(4,1)S(1)} %iota_compare_fusion.3, bf16[65,2,128,192,1]{2,0,1,3,4:T(8,128)(2,1)} %bitcast.123, bf16[1,64,128]{1,2,0:T(8,128)(2,1)S(1)} %multiply_convert_fusion.1, bf16[1,64,128]{1,2,0:T(8,128)(2,1)S(1)} %get-tuple-element.16, ...), kind=kOutput, calls=%fused_computation.27 | convolution fusion | flops 1229168640 | bytes 7118848 | tf_op jit(solution)/shard_map/tapi,acqi->tcpq/dot_general | solution.py:42
  43.2 0.7 pad_maximum_fusion.1
  43.8 10.5 %all-to-all-start = ((f32[16,12,128]{2,1,0:T(8,128)}), f32[16,12,128]{2,1,0:T(8,128)S(1)}, u32[]{:S(2)}, u32[]{:S(2)}) async-start(f32[16,12,128]{2,1,0:T(8,128)} %pad_maximum_fusion.1), calls=%async_computation | async-start | bytes 262144 | tf_op jit(solution)/shard_map/all_to_all | solution.py:125
  54.4 11.4 %all-to-all-done = f32[16,12,128]{2,1,0:T(8,128)S(1)} async-done(((f32[16,12,128]{2,1,0:T(8,128)}), f32[16,12,128]{2,1,0:T(8,128)S(1)}, u32[]{:S(2)}, u32[]{:S(2)}) %all-to-all-start) | async-done | bytes 98336 | tf_op jit(solution)/shard_map/all_to_all | solution.py:125
  65.9 0.7 broadcast_in_dim.6
  66.5 4.0 %all-to-all-start.1 = ((f32[16,12,128]{2,1,0:T(8,128)}), f32[16,12,128]{2,1,0:T(8,128)S(1)}, u32[]{:S(2)}, u32[]{:S(2)}) async-start(f32[16,12,128]{2,1,0:T(8,128)} %broadcast_in_dim.6), calls=%async_computation.1 | async-start | bytes 262144 | tf_op jit(solution)/shard_map/all_to_all | solution.py:140
  70.5 4.9 %fusion.17 = bf16[65,2,128,192]{2,0,3,1:T(8,128)(2,1)} fusion(bf16[65,2,65,1]{2,1,0,3:T(2,128)(2,1)S(1)} %bitcast.131), kind=kOutput, calls=%fused_computation.17 | convolution fusion | flops 421724160 | bytes 6406660 | tf_op jit(solution)/shard_map/acb,bji->acji/dot_general | solution.py:17
  75.4 5.5 %all-to-all-done.1 = f32[16,12,128]{2,1,0:T(8,128)S(1)} async-done(((f32[16,12,128]{2,1,0:T(8,128)}), f32[16,12,128]{2,1,0:T(8,128)S(1)}, u32[]{:S(2)}, u32[]{:S(2)}) %all-to-all-start.1) | async-done | bytes 98336 | tf_op jit(solution)/shard_map/all_to_all | solution.py:140
  81.0 2.0 %convert_bitcast_fusion = bf16[65,2,128,192]{2,3,0,1:T(8,128)(2,1)S(1)} fusion(pred[65,128,192]{1,0,2:T(8,128)(4,1)S(1)} %iota_compare_fusion, bf16[1,2,192,128]{3,2,0,1:T(8,128)(2,1)S(1)} %multiply_convert_fusion), kind=kOutput, calls=%fused_computation.13 | convolution fusion | flops 1230028800 | bytes 8085504 | tf_op jit(solution)/shard_map/apr,tcri->tacpi/dot_general | solution.py:48
  83.1 0.9 slice-done.1
  84.0 2.5 %fusion.9 = f32[128,128,1,1]{1,0,3,2:T(8,128)} fusion(bf16[65,2,128,192]{2,0,3,1:T(8,128)(2,1)S(1)} %bitcast.125, bf16[65,2,128,192]{2,3,0,1:T(8,128)(2,1)S(1)} %convert_bitcast_fusion), kind=kOutput, calls=%fused_computation.8 | convolution fusion | flops 817889280 | bytes 12845056 | tf_op jit(solution)/shard_map/tacpi,acqi->tpq/dot_general | solution.py:51
  86.5 4.2 %all-to-all-start.2 = ((f32[1,128,128]{2,0,1:T(1,128)}), f32[1,128,128]{2,0,1:T(1,128)S(1)}, u32[]{:S(2)}, u32[]{:S(2)}) async-start(f32[1,128,128]{2,0,1:T(1,128)} %bitcast.50), calls=%async_computation.2 | async-start | bytes 131072 | tf_op jit(solution)/shard_map/all_to_all | solution.py:24
  91.3 9.1 %all-to-all-done.2 = f32[1,128,128]{2,0,1:T(1,128)S(1)} async-done(((f32[1,128,128]{2,0,1:T(1,128)}), f32[1,128,128]{2,0,1:T(1,128)S(1)}, u32[]{:S(2)}, u32[]{:S(2)}) %all-to-all-start.2) | async-done | bytes 65568 | tf_op jit(solution)/shard_map/all_to_all | solution.py:24
  100.4 0.6 reduce_sum.29
  (42 shorter events, 2.5 us)
Async XLA Ops:
  2.5 33.9 %collective-permute-start.1 = (bf16[1,96,128]{1,2,0:T(8,128)(2,1)S(1)}, bf16[1,96,128]{1,2,0:T(8,128)(2,1)S(1)}, u32[]{:S(2)}, u32[]{:S(2)}) collective-permute-start(bf16[1,96,128]{1,2,0:T(8,128)(2,1)S(1)} %pad_maximum_fusion.4), channel_id=1, source_target_pairs={{16,0},{32,16},{48,32},{64,48},{80,64},{96,80},{112,96},{128,112},... | collective-permute-start | bytes 73736 | tf_op jit(solution)/shard_map/ppermute | solution.py:58
  20.6 16.0 %collective-permute-start = (bf16[1,96,128]{1,2,0:T(8,128)(2,1)S(1)}, bf16[1,96,128]{1,2,0:T(8,128)(2,1)S(1)}, u32[]{:S(2)}, u32[]{:S(2)}) collective-permute-start(bf16[1,96,128]{1,2,0:T(8,128)(2,1)S(1)} %pad_maximum_fusion.3), channel_id=1, source_target_pairs={{0,16},{16,32},{32,48},{48,64},{64,80},{80,96},{96,112},{112,128},... | collective-permute-start | bytes 73736 | tf_op jit(solution)/shard_map/ppermute | solution.py:58
  29.5 2.9 %copy-start = (bf16[128,192,65,2]{0,2,3,1:T(8,128)(2,1)}, bf16[128,192,65,2]{0,2,3,1:T(8,128)(2,1)S(1)}, u32[]{:S(2)}) copy-start(bf16[128,192,65,2]{0,2,3,1:T(8,128)(2,1)S(1)} %fusion.4) | copy-start | bytes 19169284
  29.5 6.7 %copy-start.2 = (bf16[2,1,65,65]{3,0,2,1:T(2,128)(2,1)S(1)}, bf16[2,1,65,65]{3,0,2,1:T(2,128)(2,1)}, u32[]{:S(2)}) copy-start(bf16[2,1,65,65]{3,0,2,1:T(2,128)(2,1)} %param.6) | copy-start | bytes 50704
  29.5 7.3 %copy-start.1 = (bf16[1,128,128]{2,1,0:T(8,128)(2,1)S(1)}, bf16[1,128,128]{2,1,0:T(8,128)(2,1)}, u32[]{:S(2)}) copy-start(bf16[1,128,128]{2,1,0:T(8,128)(2,1)} %param.8) | copy-start | bytes 98308
  43.8 22.0 %all-to-all-start = ((f32[16,12,128]{2,1,0:T(8,128)}), f32[16,12,128]{2,1,0:T(8,128)S(1)}, u32[]{:S(2)}, u32[]{:S(2)}) async-start(f32[16,12,128]{2,1,0:T(8,128)} %pad_maximum_fusion.1), calls=%async_computation | async-start | bytes 262144 | tf_op jit(solution)/shard_map/all_to_all | solution.py:125
  66.5 14.3 %all-to-all-start.1 = ((f32[16,12,128]{2,1,0:T(8,128)}), f32[16,12,128]{2,1,0:T(8,128)S(1)}, u32[]{:S(2)}, u32[]{:S(2)}) async-start(f32[16,12,128]{2,1,0:T(8,128)} %broadcast_in_dim.6), calls=%async_computation.1 | async-start | bytes 262144 | tf_op jit(solution)/shard_map/all_to_all | solution.py:140
  80.9 2.2 %slice-start = ((s8[7077888]{0:T(1024)(128)(4,1)}), s8[4194304]{0:T(1024)(128)(4,1)S(1)}, s32[]{:S(2)}) async-start(s8[7077888]{0:T(1024)(128)(4,1)} %bitcast.124), calls=%async_computation.3 | async-start | bytes 8388608
  81.0 3.0 %slice-start.1 = ((s8[7077888]{0:T(1024)(128)(4,1)}), s8[2883584]{0:T(1024)(128)(4,1)S(1)}, s32[]{:S(2)}) async-start(s8[7077888]{0:T(1024)(128)(4,1)} %bitcast.124), calls=%async_computation.4 | async-start | bytes 5767168
  86.5 14.0 %all-to-all-start.2 = ((f32[1,128,128]{2,0,1:T(1,128)}), f32[1,128,128]{2,0,1:T(1,128)S(1)}, u32[]{:S(2)}, u32[]{:S(2)}) async-start(f32[1,128,128]{2,0,1:T(1,128)} %bitcast.50), calls=%async_computation.2 | async-start | bytes 131072 | tf_op jit(solution)/shard_map/all_to_all | solution.py:24

commit v7 on v6

--- a/solution.py
+++ b/solution.py
@@ -34,13 +34,16 @@
     return (source - row == along).astype(images.dtype)
 
 
-def correlate_forward(images, band, rows_out):
-    select = shifted_rows(images, band.shape[0], rows_out)
+def correlate_forward(images, bands, rows_out):
+    select = shifted_rows(images, bands[0].shape[0], rows_out)
     stacked = jnp.einsum(
         "apr,tri->tapi", select, images, preferred_element_type=jnp.float32
     ).astype(images.dtype)
-    total = jnp.einsum("tapi,acqi->tcpq", stacked, band, preferred_element_type=jnp.float32)
-    return total
+    per_channel = [
+        jnp.einsum("tapi,aqi->tpq", stacked, band, preferred_element_type=jnp.float32)
+        for band in bands
+    ]
+    return jnp.stack(per_channel, axis=1)
 
 
 def correlate_adjoint(images, band, rows_out):
@@ -105,7 +108,9 @@
     )
 
     taps = kernels.reshape(2 * local_kernels, tap_count, tap_count)
-    forward_band = banded(taps, width_in, tile_side)
+    forward_band = [
+        banded(taps[c : c + 1], width_in, tile_side)[:, 0] for c in range(taps.shape[0])
+    ]
     inner_rows = tile_side - reach
     middle = correlate_forward(inner, forward_band, inner_rows)
     outer = correlate_forward(edges, forward_band, reach)

time: 102 us -> 97.8 us (0.959)
  local copies, waits for them, and re-layouts: 8.9 us -> 6.11 us
    dot_general x2 -> x4, matrix products: 8.62 us -> 5.98 us  [correlate_forward(): jnp.einsum('tapi,aqi->tpq', stacked, band, preferred_element_type=jnp.flo...]
    unnamed x13 -> x21, local copies, waits for them, and re-layouts: 4.98 us -> 2.88 us
    dot_general x1 -> x2, matrix products: 0.78 us -> 2.24 us  [correlate_forward(): jnp.einsum('apr,tri->tapi', select, images, preferred_element_type=jnp.fl...]
    dot_general x2 -> x3, matrix products: 7.63 us -> 8.06 us  [banded(): jnp.einsum('acb,bji->acji', taps.transpose(1, 0, 2), select, preferred_el...]
  transfers between devices with their start and end apart: 5 -> 5, of which waited for: 3 -> 3; matrix products, arithmetic and copies ran while one was open for 15% -> 14% of each run, Pallas kernels for 0% -> 0%
where the time goes in v7:
time: 97.8 us; the launch traced here: 97.2 us
  starting transfers between devices  38.4 us (39%)
  waiting for transfers between devices  26.1 us (27%)
  matrix products  20.8 us (21%)
  local copies, waits for them, and re-layouts  6.11 us (6%)
  other arithmetic  2.95 us (3%)
  between operations  2.9 us (3%)
    ppermute x2, starting transfers between devices, halo_rows(): return lax.ppermute(rows, 'tile', pairs)  19.8 us
    all_to_all x1, waiting for transfers between devices, shards(): lax.all_to_all(pieces, 'kern', 0, 0, tiled=True)  11.4 us
    all_to_all x1, starting transfers between devices, shards(): lax.all_to_all(pieces, 'kern', 0, 0, tiled=True)  10.5 us
    all_to_all x1, waiting for transfers between devices, scatter_sum(): pieces = lax.all_to_all(value, axis, dim, 0, tiled=True)  9.14 us
    dot_general x3, matrix products, banded(): jnp.einsum('acb,bji->acji', taps.transpose(1, 0, 2), select, preferred_el...  8.06 us
    dot_general x4, matrix products, correlate_forward(): jnp.einsum('tapi,aqi->tpq', stacked, band, preferred_element_type=jnp.flo...  5.98 us
    all_to_all x1, waiting for transfers between devices, shards(): gathered = lax.all_to_all(copies, 'kern', 0, 0, tiled=True)  5.48 us
    all_to_all x1, starting transfers between devices, scatter_sum(): pieces = lax.all_to_all(value, axis, dim, 0, tiled=True)  4.22 us
  transfers between devices with their start and end apart: 5, of which 3 were waited for; matrix products, arithmetic and copies ran while one was open for 14% of the time, Pallas kernels for 0%

profile of v7, /device:TPU:9, one launch (start us, length us, event | category | flops | bytes accessed | tf_op | source)
XLA Modules:
  0.0 97.2 jit_solution(232030304364661714)
XLA Ops:
  0.6 0.9 copy.73
  1.6 0.7 fusion.90
  2.6 17.8 %collective-permute-start.1 = (bf16[1,96,128]{1,2,0:T(8,128)(2,1)S(1)}, bf16[1,96,128]{1,2,0:T(8,128)(2,1)S(1)}, u32[]{:S(2)}, u32[]{:S(2)}) collective-permute-start(bf16[1,96,128]{1,2,0:T(8,128)(2,1)S(1)} %pad_maximum_fusion.4), channel_id=1, source_target_pairs={{16,0},{32,16},{48,32},{64,48},{80,64},{96,80},{112,96},{128,112},... | collective-permute-start | bytes 73736 | tf_op jit(solution)/shard_map/ppermute | solution.py:61
  20.6 1.9 %collective-permute-start = (bf16[1,96,128]{1,2,0:T(8,128)(2,1)S(1)}, bf16[1,96,128]{1,2,0:T(8,128)(2,1)S(1)}, u32[]{:S(2)}, u32[]{:S(2)}) collective-permute-start(bf16[1,96,128]{1,2,0:T(8,128)(2,1)S(1)} %pad_maximum_fusion.3), channel_id=1, source_target_pairs={{0,16},{16,32},{32,48},{48,64},{64,80},{80,96},{96,112},{112,128},... | collective-permute-start | bytes 73736 | tf_op jit(solution)/shard_map/ppermute | solution.py:61
  22.5 0.8 convert_bitcast_fusion.4
  23.3 1.0 %iota_compare_fusion = pred[65,128,192]{1,0,2:T(8,128)(4,1)S(1)} fusion(), kind=kLoop, calls=%fused_computation | loop fusion | flops 3194880 | bytes 1597440 | tf_op jit(solution)/shard_map/eq | solution.py:16
  25.0 1.6 %convert_bitcast_fusion.3 = bf16[65,128,192]{1,0,2:T(8,128)(2,1)S(1)} fusion(bf16[1,1,65,65]{3,0,2,1:T(2,128)(2,1)S(1)} %get-tuple-element.12), kind=kOutput, calls=%fused_computation.15 | convolution fusion | flops 212459520 | bytes 3203330 | tf_op jit(solution)/shard_map/acb,bji->acji/dot_general | solution.py:17
  26.6 1.6 %convert_bitcast_fusion.2 = bf16[65,128,192]{1,0,2:T(8,128)(2,1)S(1)} fusion(bf16[1,1,65,65]{3,0,2,1:T(2,128)(2,1)S(1)} %get-tuple-element.13), kind=kOutput, calls=%fused_computation.14 | convolution fusion | flops 212459520 | bytes 3203330 | tf_op jit(solution)/shard_map/acb,bji->acji/dot_general | solution.py:17
  28.2 1.1 %fusion.42 = f32[1,1,64,128]{3,2,0,1:T(8,128)S(1)} fusion(bf16[65,128,192]{1,0,2:T(8,128)(2,1)S(1)} %convert_bitcast_fusion.3, bf16[65,64,192]{2,0,1:T(8,128)(2,1)S(1)} %convert_bitcast_fusion.4), kind=kOutput, calls=%fused_computation.36 | convolution fusion | flops 204472320 | bytes 4825088 | tf_op jit(solution)/shard_map/tapi,aqi->tpq/dot_general | solution.py:43
  29.4 1.1 %fusion.47 = f32[1,1,64,128]{3,2,0,1:T(8,128)S(1)} fusion(bf16[65,128,192]{1,0,2:T(8,128)(2,1)S(1)} %convert_bitcast_fusion.2, bf16[65,64,192]{2,0,1:T(8,128)(2,1)S(1)} %convert_bitcast_fusion.4), kind=kOutput, calls=%fused_computation.37 | convolution fusion | flops 204472320 | bytes 4825088 | tf_op jit(solution)/shard_map/tapi,aqi->tpq/dot_general | solution.py:43
  32.9 1.5 %convert_bitcast_fusion.1 = bf16[2,65,64,192]{3,1,2,0:T(8,128)(2,1)S(1)} fusion(bf16[1,64,128]{1,2,0:T(8,128)(2,1)S(1)} %multiply_convert_fusion.1, bf16[1,64,128]{1,2,0:T(8,128)(2,1)S(1)} %get-tuple-element.16, bf16[1,64,128]{1,2,0:T(8,128)(2,1)S(1)} %get-tuple-element.17, bf16[1,64,128]{1,2,0:T(8,128)(2,1)S(1)} %multiply_convert_fusion.2), kind=kOutput, calls=%fused_computation.13 | convolution fusion | flops 412344320 | bytes 3260416 | tf_op jit(solution)/shard_map/apr,tri->tapi/dot_general | solution.py:39
  34.9 1.8 %fusion.32 = f32[2,1,64,128]{3,2,0,1:T(8,128)S(1)} fusion(bf16[65,128,192]{1,0,2:T(8,128)(2,1)S(1)} %copy-done.4, bf16[2,65,64,192]{3,1,2,0:T(8,128)(2,1)S(1)} %convert_bitcast_fusion.1), kind=kOutput, calls=%fused_computation.34 | convolution fusion | flops 408944640 | bytes 6455296 | tf_op jit(solution)/shard_map/tapi,aqi->tpq/dot_general | solution.py:43
  36.9 2.0 %fusion.37 = f32[2,1,64,128]{3,2,0,1:T(8,128)S(1)} fusion(bf16[65,128,192]{1,0,2:T(8,128)(2,1)S(1)} %copy-done.6, bf16[2,65,64,192]{3,1,2,0:T(8,128)(2,1)S(1)} %convert_bitcast_fusion.1), kind=kOutput, calls=%fused_computation.35 | convolution fusion | flops 408944640 | bytes 6455296 | tf_op jit(solution)/shard_map/tapi,aqi->tpq/dot_general | solution.py:43
  39.3 0.7 pad_maximum_fusion.1
  40.0 10.5 %all-to-all-start = ((f32[16,12,128]{2,1,0:T(8,128)}), f32[16,12,128]{2,1,0:T(8,128)S(1)}, u32[]{:S(2)}, u32[]{:S(2)}) async-start(f32[16,12,128]{2,1,0:T(8,128)} %pad_maximum_fusion.1), calls=%async_computation | async-start | bytes 262144 | tf_op jit(solution)/shard_map/all_to_all | solution.py:130
  50.6 11.4 %all-to-all-done = f32[16,12,128]{2,1,0:T(8,128)S(1)} async-done(((f32[16,12,128]{2,1,0:T(8,128)}), f32[16,12,128]{2,1,0:T(8,128)S(1)}, u32[]{:S(2)}, u32[]{:S(2)}) %all-to-all-start) | async-done | bytes 98336 | tf_op jit(solution)/shard_map/all_to_all | solution.py:130
  62.7 4.0 %all-to-all-start.1 = ((f32[16,12,128]{2,1,0:T(8,128)}), f32[16,12,128]{2,1,0:T(8,128)S(1)}, u32[]{:S(2)}, u32[]{:S(2)}) async-start(f32[16,12,128]{2,1,0:T(8,128)} %broadcast_in_dim.6), calls=%async_computation.1 | async-start | bytes 262144 | tf_op jit(solution)/shard_map/all_to_all | solution.py:145
  66.7 4.9 %fusion.10 = bf16[65,2,128,192]{2,0,3,1:T(8,128)(2,1)} fusion(bf16[65,2,65,1]{2,1,0,3:T(2,128)(2,1)S(1)} %bitcast.129), kind=kOutput, calls=%fused_computation.12 | convolution fusion | flops 421724160 | bytes 6406660 | tf_op jit(solution)/shard_map/acb,bji->acji/dot_general | solution.py:17
  71.5 5.5 %all-to-all-done.1 = f32[16,12,128]{2,1,0:T(8,128)S(1)} async-done(((f32[16,12,128]{2,1,0:T(8,128)}), f32[16,12,128]{2,1,0:T(8,128)S(1)}, u32[]{:S(2)}, u32[]{:S(2)}) %all-to-all-start.1) | async-done | bytes 98336 | tf_op jit(solution)/shard_map/all_to_all | solution.py:145
  77.2 2.0 %convert_bitcast_fusion = bf16[65,2,128,192]{2,3,0,1:T(8,128)(2,1)S(1)} fusion(pred[65,128,192]{1,0,2:T(8,128)(4,1)S(1)} %iota_compare_fusion, bf16[1,2,192,128]{3,2,0,1:T(8,128)(2,1)S(1)} %multiply_convert_fusion), kind=kOutput, calls=%fused_computation.6 | convolution fusion | flops 1230028800 | bytes 8085504 | tf_op jit(solution)/shard_map/apr,tcri->tacpi/dot_general | solution.py:51
  79.2 0.9 slice-done.1
  80.2 2.5 %fusion.2 = f32[128,128,1,1]{1,0,3,2:T(8,128)} fusion(bf16[65,2,128,192]{2,0,3,1:T(8,128)(2,1)S(1)} %bitcast.124, bf16[65,2,128,192]{2,3,0,1:T(8,128)(2,1)S(1)} %convert_bitcast_fusion), kind=kOutput, calls=%fused_computation.3 | convolution fusion | flops 817889280 | bytes 12845056 | tf_op jit(solution)/shard_map/tacpi,acqi->tpq/dot_general | solution.py:54
  82.7 4.2 %all-to-all-start.2 = ((f32[1,128,128]{2,0,1:T(1,128)}), f32[1,128,128]{2,0,1:T(1,128)S(1)}, u32[]{:S(2)}, u32[]{:S(2)}) async-start(f32[1,128,128]{2,0,1:T(1,128)} %bitcast.55), calls=%async_computation.2 | async-start | bytes 131072 | tf_op jit(solution)/shard_map/all_to_all | solution.py:24
  87.5 9.1 %all-to-all-done.2 = f32[1,128,128]{2,0,1:T(1,128)S(1)} async-done(((f32[1,128,128]{2,0,1:T(1,128)}), f32[1,128,128]{2,0,1:T(1,128)S(1)}, u32[]{:S(2)}, u32[]{:S(2)}) %all-to-all-start.2) | async-done | bytes 65568 | tf_op jit(solution)/shard_map/all_to_all | solution.py:24
  (54 shorter events, 4.8 us)
Async XLA Ops:
  0.6 23.7 %copy-start.2 = (s32[1,8]{1,0:T(1,128)S(1)}, s32[1,8]{1,0:T(1,128)}, u32[]{:S(2)}) copy-start(s32[1,8]{1,0:T(1,128)} %param.9) | copy-start | bytes 100
  0.6 24.3 %copy-start = (bf16[2,1,65,65]{3,0,2,1:T(2,128)(2,1)S(1)}, bf16[2,1,65,65]{3,0,2,1:T(2,128)(2,1)}, u32[]{:S(2)}) copy-start(bf16[2,1,65,65]{3,0,2,1:T(2,128)(2,1)} %param.6) | copy-start | bytes 50704
  2.6 30.2 %collective-permute-start.1 = (bf16[1,96,128]{1,2,0:T(8,128)(2,1)S(1)}, bf16[1,96,128]{1,2,0:T(8,128)(2,1)S(1)}, u32[]{:S(2)}, u32[]{:S(2)}) collective-permute-start(bf16[1,96,128]{1,2,0:T(8,128)(2,1)S(1)} %pad_maximum_fusion.4), channel_id=1, source_target_pairs={{16,0},{32,16},{48,32},{64,48},{80,64},{96,80},{112,96},{128,112},... | collective-permute-start | bytes 73736 | tf_op jit(solution)/shard_map/ppermute | solution.py:61
  20.6 12.2 %collective-permute-start = (bf16[1,96,128]{1,2,0:T(8,128)(2,1)S(1)}, bf16[1,96,128]{1,2,0:T(8,128)(2,1)S(1)}, u32[]{:S(2)}, u32[]{:S(2)}) collective-permute-start(bf16[1,96,128]{1,2,0:T(8,128)(2,1)S(1)} %pad_maximum_fusion.3), channel_id=1, source_target_pairs={{0,16},{16,32},{32,48},{48,64},{64,80},{80,96},{96,112},{112,128},... | collective-permute-start | bytes 73736 | tf_op jit(solution)/shard_map/ppermute | solution.py:61
  26.6 2.8 %copy-start.3 = (bf16[65,128,192]{1,0,2:T(8,128)(2,1)}, bf16[65,128,192]{1,0,2:T(8,128)(2,1)S(1)}, u32[]{:S(2)}) copy-start(bf16[65,128,192]{1,0,2:T(8,128)(2,1)S(1)} %convert_bitcast_fusion.3) | copy-start | bytes 9584644
  28.2 2.3 %copy-start.5 = (bf16[65,128,192]{1,0,2:T(8,128)(2,1)}, bf16[65,128,192]{1,0,2:T(8,128)(2,1)S(1)}, u32[]{:S(2)}) copy-start(bf16[65,128,192]{1,0,2:T(8,128)(2,1)S(1)} %convert_bitcast_fusion.2) | copy-start | bytes 9584644
  32.9 2.0 %copy-start.4 = (bf16[65,128,192]{1,0,2:T(8,128)(2,1)S(1)}, bf16[65,128,192]{1,0,2:T(8,128)(2,1)}, u32[]{:S(2)}) copy-start(bf16[65,128,192]{1,0,2:T(8,128)(2,1)} %copy-done.3) | copy-start | bytes 9584644
  34.9 2.0 %copy-start.6 = (bf16[65,128,192]{1,0,2:T(8,128)(2,1)S(1)}, bf16[65,128,192]{1,0,2:T(8,128)(2,1)}, u32[]{:S(2)}) copy-start(bf16[65,128,192]{1,0,2:T(8,128)(2,1)} %copy-done.5) | copy-start | bytes 9584644
  36.9 2.4 %copy-start.1 = (bf16[1,128,128]{2,1,0:T(8,128)(2,1)S(1)}, bf16[1,128,128]{2,1,0:T(8,128)(2,1)}, u32[]{:S(2)}) copy-start(bf16[1,128,128]{2,1,0:T(8,128)(2,1)} %param.8) | copy-start | bytes 98308
  40.0 22.0 %all-to-all-start = ((f32[16,12,128]{2,1,0:T(8,128)}), f32[16,12,128]{2,1,0:T(8,128)S(1)}, u32[]{:S(2)}, u32[]{:S(2)}) async-start(f32[16,12,128]{2,1,0:T(8,128)} %pad_maximum_fusion.1), calls=%async_computation | async-start | bytes 262144 | tf_op jit(solution)/shard_map/all_to_all | solution.py:130
  62.7 14.3 %all-to-all-start.1 = ((f32[16,12,128]{2,1,0:T(8,128)}), f32[16,12,128]{2,1,0:T(8,128)S(1)}, u32[]{:S(2)}, u32[]{:S(2)}) async-start(f32[16,12,128]{2,1,0:T(8,128)} %broadcast_in_dim.6), calls=%async_computation.1 | async-start | bytes 262144 | tf_op jit(solution)/shard_map/all_to_all | solution.py:145
  77.1 2.2 %slice-start = ((s8[7077888]{0:T(1024)(128)(4,1)}), s8[4194304]{0:T(1024)(128)(4,1)S(1)}, s32[]{:S(2)}) async-start(s8[7077888]{0:T(1024)(128)(4,1)} %bitcast.123), calls=%async_computation.3 | async-start | bytes 8388608
  77.2 3.0 %slice-start.1 = ((s8[7077888]{0:T(1024)(128)(4,1)}), s8[2883584]{0:T(1024)(128)(4,1)S(1)}, s32[]{:S(2)}) async-start(s8[7077888]{0:T(1024)(128)(4,1)} %bitcast.123), calls=%async_computation.4 | async-start | bytes 5767168
  82.7 13.9 %all-to-all-start.2 = ((f32[1,128,128]{2,0,1:T(1,128)}), f32[1,128,128]{2,0,1:T(1,128)S(1)}, u32[]{:S(2)}, u32[]{:S(2)}) async-start(f32[1,128,128]{2,0,1:T(1,128)} %bitcast.55), calls=%async_computation.2 | async-start | bytes 131072 | tf_op jit(solution)/shard_map/all_to_all | solution.py:24

commit v8 on v7

--- a/solution.py
+++ b/solution.py
@@ -46,12 +46,16 @@
     return jnp.stack(per_channel, axis=1)
 
 
-def correlate_adjoint(images, band, rows_out):
-    select = shifted_rows(images, band.shape[0], rows_out)
-    stacked = jnp.einsum(
-        "apr,tcri->tacpi", select, images, preferred_element_type=jnp.float32
-    ).astype(images.dtype)
-    return jnp.einsum("tacpi,acqi->tpq", stacked, band, preferred_element_type=jnp.float32)
+def correlate_adjoint(images, bands, rows_out):
+    select = shifted_rows(images, bands[0].shape[0], rows_out)
+    total = None
+    for channel, band in enumerate(bands):
+        stacked = jnp.einsum(
+            "apr,tri->tapi", select, images[:, channel], preferred_element_type=jnp.float32
+        ).astype(images.dtype)
+        term = jnp.einsum("tapi,aqi->tpq", stacked, band, preferred_element_type=jnp.float32)
+        total = term if total is None else total + term
+    return total
 
 
 def halo_rows(rows, direction):
@@ -151,7 +155,9 @@
     scaled = (2.0 * doubled)[None, :, None, None] * sensitivity[None, None] * fields
     adjoint_source = scaled.astype(jnp.bfloat16)
     source_ext = jnp.pad(adjoint_source, ((0, 0), (0, 0), (0, 0), (half_width, half_width)))
-    adjoint_band = banded(flipped, width_in, tile_side)
+    adjoint_band = [
+        banded(flipped[c : c + 1], width_in, tile_side)[:, 0] for c in range(flipped.shape[0])
+    ]
     gradient_term = correlate_adjoint(source_ext, adjoint_band, tile_side)
     gradient = scatter_sum(gradient_term, "kern", 1)
     resist = resist_block[None, :share_rows]

time: 97.8 us -> 101 us (1.033)
  matrix products: 20.8 us -> 26.2 us
  waiting for transfers between devices: 26.1 us -> 24.5 us
    dot_general x2, matrix products: 4.49 us -> 8.55 us  [correlate_adjoint(): jnp.einsum('tapi,aqi->tpq', stacked, band, preferred_element_type=jnp.flo...]
    all_to_all x1, waiting for transfers between devices: 11.4 us -> 8.24 us  [shards(): lax.all_to_all(pieces, 'kern', 0, 0, tiled=True)]
    all_to_all x1, waiting for transfers between devices: 5.48 us -> 7.08 us  [shards(): gathered = lax.all_to_all(copies, 'kern', 0, 0, tiled=True)]
    dot_general x3 -> x4, matrix products: 8.06 us -> 9.65 us  [banded(): jnp.einsum('acb,bji->acji', taps.transpose(1, 0, 2), select, preferred_el...]
    unnamed x21 -> x18, local copies, waits for them, and re-layouts: 2.88 us -> 1.88 us
  transfers between devices with their start and end apart: 5 -> 5, of which waited for: 3 -> 3; matrix products, arithmetic and copies ran while one was open for 14% -> 16% of each run, Pallas kernels for 0% -> 0%
where the time goes in v8:
time: 101 us; the launch traced here: 100 us
  starting transfers between devices  38.3 us (38%)
  matrix products  26.2 us (26%)
  waiting for transfers between devices  24.5 us (24%)
  local copies, waits for them, and re-layouts  5.36 us (5%)
  other arithmetic  2.92 us (3%)
  between operations  2.88 us (3%)
    ppermute x2, starting transfers between devices, halo_rows(): return lax.ppermute(rows, 'tile', pairs)  19.8 us
    all_to_all x1, starting transfers between devices, shards(): lax.all_to_all(pieces, 'kern', 0, 0, tiled=True)  10.5 us
    dot_general x4, matrix products, banded(): jnp.einsum('acb,bji->acji', taps.transpose(1, 0, 2), select, preferred_el...  9.65 us
    all_to_all x1, waiting for transfers between devices, scatter_sum(): pieces = lax.all_to_all(value, axis, dim, 0, tiled=True)  9.19 us
    dot_general x2, matrix products, correlate_adjoint(): jnp.einsum('tapi,aqi->tpq', stacked, band, preferred_element_type=jnp.flo...  8.55 us
    all_to_all x1, waiting for transfers between devices, shards(): lax.all_to_all(pieces, 'kern', 0, 0, tiled=True)  8.24 us
    all_to_all x1, waiting for transfers between devices, shards(): gathered = lax.all_to_all(copies, 'kern', 0, 0, tiled=True)  7.08 us
    dot_general x4, matrix products, correlate_forward(): jnp.einsum('tapi,aqi->tpq', stacked, band, preferred_element_type=jnp.flo...  5.79 us
  transfers between devices with their start and end apart: 5, of which 3 were waited for; matrix products, arithmetic and copies ran while one was open for 16% of the time, Pallas kernels for 0%

profile of v8, /device:TPU:9, one launch (start us, length us, event | category | flops | bytes accessed | tf_op | source)
XLA Modules:
  0.0 100.2 jit_solution(16407304132232428306)
XLA Ops:
  0.6 0.9 copy.101
  1.6 0.7 fusion.132
  2.6 17.8 %collective-permute-start.1 = (bf16[1,96,128]{1,2,0:T(8,128)(2,1)S(1)}, bf16[1,96,128]{1,2,0:T(8,128)(2,1)S(1)}, u32[]{:S(2)}, u32[]{:S(2)}) collective-permute-start(bf16[1,96,128]{1,2,0:T(8,128)(2,1)S(1)} %pad_maximum_fusion.4), channel_id=1, source_target_pairs={{16,0},{32,16},{48,32},{64,48},{80,64},{96,80},{112,96},{128,112},... | collective-permute-start | bytes 73736 | tf_op jit(solution)/shard_map/ppermute | solution.py:65
  20.6 1.9 %collective-permute-start = (bf16[1,96,128]{1,2,0:T(8,128)(2,1)S(1)}, bf16[1,96,128]{1,2,0:T(8,128)(2,1)S(1)}, u32[]{:S(2)}, u32[]{:S(2)}) collective-permute-start(bf16[1,96,128]{1,2,0:T(8,128)(2,1)S(1)} %pad_maximum_fusion.3), channel_id=1, source_target_pairs={{0,16},{16,32},{32,48},{48,64},{64,80},{80,96},{96,112},{112,128},... | collective-permute-start | bytes 73736 | tf_op jit(solution)/shard_map/ppermute | solution.py:65
  22.5 0.8 convert_bitcast_fusion.3
  23.3 1.0 %iota_compare_fusion = pred[65,128,192]{1,0,2:T(8,128)(4,1)S(1)} fusion(), kind=kLoop, calls=%fused_computation | loop fusion | flops 3194880 | bytes 1597440 | tf_op jit(solution)/shard_map/eq | solution.py:16
  25.0 1.6 %convert_bitcast_fusion.2 = bf16[65,128,192]{1,0,2:T(8,128)(2,1)S(1)} fusion(bf16[1,1,65,65]{3,0,2,1:T(2,128)(2,1)S(1)} %get-tuple-element.12), kind=kOutput, calls=%fused_computation.11 | convolution fusion | flops 212459520 | bytes 3203330 | tf_op jit(solution)/shard_map/acb,bji->acji/dot_general | solution.py:17
  26.6 1.6 %convert_bitcast_fusion.1 = bf16[65,128,192]{1,0,2:T(8,128)(2,1)S(1)} fusion(bf16[1,1,65,65]{3,0,2,1:T(2,128)(2,1)S(1)} %get-tuple-element.13), kind=kOutput, calls=%fused_computation.10 | convolution fusion | flops 212459520 | bytes 3203330 | tf_op jit(solution)/shard_map/acb,bji->acji/dot_general | solution.py:17
  28.2 1.1 %fusion.74 = f32[1,1,64,128]{3,2,0,1:T(8,128)S(1)} fusion(bf16[65,128,192]{1,0,2:T(8,128)(2,1)S(1)} %convert_bitcast_fusion.2, bf16[65,64,192]{2,0,1:T(8,128)(2,1)S(1)} %convert_bitcast_fusion.3), kind=kOutput, calls=%fused_computation.45 | convolution fusion | flops 204472320 | bytes 4825088 | tf_op jit(solution)/shard_map/tapi,aqi->tpq/dot_general | solution.py:43
  29.4 1.1 %fusion.79 = f32[1,1,64,128]{3,2,0,1:T(8,128)S(1)} fusion(bf16[65,128,192]{1,0,2:T(8,128)(2,1)S(1)} %convert_bitcast_fusion.1, bf16[65,64,192]{2,0,1:T(8,128)(2,1)S(1)} %convert_bitcast_fusion.3), kind=kOutput, calls=%fused_computation.46 | convolution fusion | flops 204472320 | bytes 4825088 | tf_op jit(solution)/shard_map/tapi,aqi->tpq/dot_general | solution.py:43
  33.1 1.5 %convert_bitcast_fusion = bf16[2,65,64,192]{3,1,2,0:T(8,128)(2,1)S(1)} fusion(bf16[1,64,128]{1,2,0:T(8,128)(2,1)S(1)} %multiply_convert_fusion.1, bf16[1,64,128]{1,2,0:T(8,128)(2,1)S(1)} %get-tuple-element.16, bf16[1,64,128]{1,2,0:T(8,128)(2,1)S(1)} %get-tuple-element.17, bf16[1,64,128]{1,2,0:T(8,128)(2,1)S(1)} %multiply_convert_fusion.2), kind=kOutput, calls=%fused_computation.5 | convolution fusion | flops 412344320 | bytes 3260416 | tf_op jit(solution)/shard_map/apr,tri->tapi/dot_general | solution.py:39
  35.1 1.8 %fusion.57 = f32[2,1,64,128]{3,2,0,1:T(8,128)S(1)} fusion(bf16[65,128,192]{1,0,2:T(8,128)(2,1)S(1)} %copy-done.4, bf16[2,65,64,192]{3,1,2,0:T(8,128)(2,1)S(1)} %convert_bitcast_fusion), kind=kOutput, calls=%fused_computation.42 | convolution fusion | flops 408944640 | bytes 6455296 | tf_op jit(solution)/shard_map/tapi,aqi->tpq/dot_general | solution.py:43
  37.1 1.8 %fusion.62 = f32[2,1,64,128]{3,2,0,1:T(8,128)S(1)} fusion(bf16[65,128,192]{1,0,2:T(8,128)(2,1)S(1)} %copy-done.6, bf16[2,65,64,192]{3,1,2,0:T(8,128)(2,1)S(1)} %convert_bitcast_fusion), kind=kOutput, calls=%fused_computation.43 | convolution fusion | flops 408944640 | bytes 6455296 | tf_op jit(solution)/shard_map/tapi,aqi->tpq/dot_general | solution.py:43
  40.1 10.5 %all-to-all-start = ((f32[16,12,128]{2,1,0:T(8,128)}), f32[16,12,128]{2,1,0:T(8,128)S(1)}, u32[]{:S(2)}, u32[]{:S(2)}) async-start(f32[16,12,128]{2,1,0:T(8,128)} %pad_maximum_fusion.1), calls=%async_computation | async-start | bytes 262144 | tf_op jit(solution)/shard_map/all_to_all | solution.py:134
  50.6 3.2 %fusion.28 = bf16[65,128,192]{1,0,2:T(8,128)(2,1)} fusion(bf16[2,65,65]{2,1,0:T(8,128)(2,1)S(1)} %rev.3), kind=kOutput, calls=%fused_computation.32 | convolution fusion | flops 212459520 | bytes 3213312 | tf_op jit(solution)/shard_map/acb,bji->acji/dot_general | solution.py:17
  53.8 8.2 %all-to-all-done = f32[16,12,128]{2,1,0:T(8,128)S(1)} async-done(((f32[16,12,128]{2,1,0:T(8,128)}), f32[16,12,128]{2,1,0:T(8,128)S(1)}, u32[]{:S(2)}, u32[]{:S(2)}) %all-to-all-start) | async-done | bytes 98336 | tf_op jit(solution)/shard_map/all_to_all | solution.py:134
  62.1 0.7 broadcast_in_dim.6
  62.8 4.0 %all-to-all-start.1 = ((f32[16,12,128]{2,1,0:T(8,128)}), f32[16,12,128]{2,1,0:T(8,128)S(1)}, u32[]{:S(2)}, u32[]{:S(2)}) async-start(f32[16,12,128]{2,1,0:T(8,128)} %broadcast_in_dim.6), calls=%async_computation.1 | async-start | bytes 262144 | tf_op jit(solution)/shard_map/all_to_all | solution.py:149
  66.8 3.3 %fusion.29 = bf16[65,128,192]{1,0,2:T(8,128)(2,1)} fusion(bf16[2,65,65]{2,1,0:T(8,128)(2,1)S(1)} %rev.3), kind=kOutput, calls=%fused_computation.33 | convolution fusion | flops 212459520 | bytes 3213312 | tf_op jit(solution)/shard_map/acb,bji->acji/dot_general | solution.py:17
  70.0 7.1 %all-to-all-done.1 = f32[16,12,128]{2,1,0:T(8,128)S(1)} async-done(((f32[16,12,128]{2,1,0:T(8,128)}), f32[16,12,128]{2,1,0:T(8,128)S(1)}, u32[]{:S(2)}, u32[]{:S(2)}) %all-to-all-start.1) | async-done | bytes 98336 | tf_op jit(solution)/shard_map/all_to_all | solution.py:149
  77.2 4.0 %fusion.43 = f32[128,128]{1,0:T(8,128)S(1)} fusion(bf16[65,128,192]{1,0,2:T(8,128)(2,1)} %fusion.28, pred[65,128,192]{1,0,2:T(8,128)(4,1)S(1)} %iota_compare_fusion, bf16[1,2,192,128]{3,2,0,1:T(8,128)(2,1)S(1)} %multiply_convert_fusion), kind=kOutput, calls=%fused_computation.40 | convolution fusion | flops 1023959040 | bytes 4956160 | tf_op jit(solution)/shard_map/tapi,aqi->tpq/dot_general | solution.py:56
  81.2 4.6 %fusion.67 = f32[128,128]{1,0:T(8,128)} fusion(f32[128,128]{1,0:T(8,128)S(1)} %fusion.43, bf16[65,128,192]{1,0,2:T(8,128)(2,1)} %fusion.29, pred[65,128,192]{1,0,2:T(8,128)(4,1)S(1)} %iota_compare_fusion, bf16[1,2,192,128]{3,2,0,1:T(8,128)(2,1)S(1)} %multiply_convert_fusion), kind=kOutput, calls=%fused_computation.44 | convolution fusion | flops 1023975424 | bytes 5021696 | tf_op jit(solution)/shard_map/tapi,aqi->tpq/dot_general | solution.py:56
  85.8 4.0 %all-to-all-start.2 = ((f32[1,128,128]{2,0,1:T(1,128)}), f32[1,128,128]{2,0,1:T(1,128)S(1)}, u32[]{:S(2)}, u32[]{:S(2)}) async-start(f32[1,128,128]{2,0,1:T(1,128)} %bitcast.60), calls=%async_computation.2 | async-start | bytes 131072 | tf_op jit(solution)/shard_map/all_to_all | solution.py:24
  90.4 9.2 %all-to-all-done.2 = f32[1,128,128]{2,0,1:T(1,128)S(1)} async-done(((f32[1,128,128]{2,0,1:T(1,128)}), f32[1,128,128]{2,0,1:T(1,128)S(1)}, u32[]{:S(2)}, u32[]{:S(2)}) %all-to-all-start.2) | async-done | bytes 65568 | tf_op jit(solution)/shard_map/all_to_all | solution.py:24
  (51 shorter events, 5.0 us)
Async XLA Ops:
  0.6 23.7 %copy-start.2 = (s32[1,8]{1,0:T(1,128)S(1)}, s32[1,8]{1,0:T(1,128)}, u32[]{:S(2)}) copy-start(s32[1,8]{1,0:T(1,128)} %param.9) | copy-start | bytes 100
  0.6 24.3 %copy-start = (bf16[2,1,65,65]{3,0,2,1:T(2,128)(2,1)S(1)}, bf16[2,1,65,65]{3,0,2,1:T(2,128)(2,1)}, u32[]{:S(2)}) copy-start(bf16[2,1,65,65]{3,0,2,1:T(2,128)(2,1)} %param.6) | copy-start | bytes 50704
  2.6 30.5 %collective-permute-start.1 = (bf16[1,96,128]{1,2,0:T(8,128)(2,1)S(1)}, bf16[1,96,128]{1,2,0:T(8,128)(2,1)S(1)}, u32[]{:S(2)}, u32[]{:S(2)}) collective-permute-start(bf16[1,96,128]{1,2,0:T(8,128)(2,1)S(1)} %pad_maximum_fusion.4), channel_id=1, source_target_pairs={{16,0},{32,16},{48,32},{64,48},{80,64},{96,80},{112,96},{128,112},... | collective-permute-start | bytes 73736 | tf_op jit(solution)/shard_map/ppermute | solution.py:65
  20.6 12.5 %collective-permute-start = (bf16[1,96,128]{1,2,0:T(8,128)(2,1)S(1)}, bf16[1,96,128]{1,2,0:T(8,128)(2,1)S(1)}, u32[]{:S(2)}, u32[]{:S(2)}) collective-permute-start(bf16[1,96,128]{1,2,0:T(8,128)(2,1)S(1)} %pad_maximum_fusion.3), channel_id=1, source_target_pairs={{0,16},{16,32},{32,48},{48,64},{64,80},{80,96},{96,112},{112,128},... | collective-permute-start | bytes 73736 | tf_op jit(solution)/shard_map/ppermute | solution.py:65
  26.6 2.8 %copy-start.3 = (bf16[65,128,192]{1,0,2:T(8,128)(2,1)}, bf16[65,128,192]{1,0,2:T(8,128)(2,1)S(1)}, u32[]{:S(2)}) copy-start(bf16[65,128,192]{1,0,2:T(8,128)(2,1)S(1)} %convert_bitcast_fusion.2) | copy-start | bytes 9584644
  28.2 2.3 %copy-start.5 = (bf16[65,128,192]{1,0,2:T(8,128)(2,1)}, bf16[65,128,192]{1,0,2:T(8,128)(2,1)S(1)}, u32[]{:S(2)}) copy-start(bf16[65,128,192]{1,0,2:T(8,128)(2,1)S(1)} %convert_bitcast_fusion.1) | copy-start | bytes 9584644
  33.1 2.0 %copy-start.4 = (bf16[65,128,192]{1,0,2:T(8,128)(2,1)S(1)}, bf16[65,128,192]{1,0,2:T(8,128)(2,1)}, u32[]{:S(2)}) copy-start(bf16[65,128,192]{1,0,2:T(8,128)(2,1)} %copy-done.3) | copy-start | bytes 9584644
  35.1 2.0 %copy-start.6 = (bf16[65,128,192]{1,0,2:T(8,128)(2,1)S(1)}, bf16[65,128,192]{1,0,2:T(8,128)(2,1)}, u32[]{:S(2)}) copy-start(bf16[65,128,192]{1,0,2:T(8,128)(2,1)} %copy-done.5) | copy-start | bytes 9584644
  37.1 2.2 %copy-start.1 = (bf16[1,128,128]{2,1,0:T(8,128)(2,1)S(1)}, bf16[1,128,128]{2,1,0:T(8,128)(2,1)}, u32[]{:S(2)}) copy-start(bf16[1,128,128]{2,1,0:T(8,128)(2,1)} %param.8) | copy-start | bytes 98308
  40.1 22.0 %all-to-all-start = ((f32[16,12,128]{2,1,0:T(8,128)}), f32[16,12,128]{2,1,0:T(8,128)S(1)}, u32[]{:S(2)}, u32[]{:S(2)}) async-start(f32[16,12,128]{2,1,0:T(8,128)} %pad_maximum_fusion.1), calls=%async_computation | async-start | bytes 262144 | tf_op jit(solution)/shard_map/all_to_all | solution.py:134
  62.8 14.3 %all-to-all-start.1 = ((f32[16,12,128]{2,1,0:T(8,128)}), f32[16,12,128]{2,1,0:T(8,128)S(1)}, u32[]{:S(2)}, u32[]{:S(2)}) async-start(f32[16,12,128]{2,1,0:T(8,128)} %broadcast_in_dim.6), calls=%async_computation.1 | async-start | bytes 262144 | tf_op jit(solution)/shard_map/all_to_all | solution.py:149
  85.8 13.8 %all-to-all-start.2 = ((f32[1,128,128]{2,0,1:T(1,128)}), f32[1,128,128]{2,0,1:T(1,128)S(1)}, u32[]{:S(2)}, u32[]{:S(2)}) async-start(f32[1,128,128]{2,0,1:T(1,128)} %bitcast.60), calls=%async_computation.2 | async-start | bytes 131072 | tf_op jit(solution)/shard_map/all_to_all | solution.py:24

commit v9 on v7

--- a/solution.py
+++ b/solution.py
@@ -141,6 +141,8 @@
         * resist_block
         * (1.0 - resist_block)
     )
+    adjoint_band = banded(flipped, width_in, tile_side)
+    adjoint_band, own_sensitivity = lax.optimization_barrier((adjoint_band, own_sensitivity))
     copies = jnp.broadcast_to(own_sensitivity, (kern_count,) + own_sensitivity.shape)
     gathered = lax.all_to_all(copies, "kern", 0, 0, tiled=True)
     sens_own = gathered[:, :share_rows].reshape(tile_side, tile_side)
@@ -151,7 +153,6 @@
     scaled = (2.0 * doubled)[None, :, None, None] * sensitivity[None, None] * fields
     adjoint_source = scaled.astype(jnp.bfloat16)
     source_ext = jnp.pad(adjoint_source, ((0, 0), (0, 0), (0, 0), (half_width, half_width)))
-    adjoint_band = banded(flipped, width_in, tile_side)
     gradient_term = correlate_adjoint(source_ext, adjoint_band, tile_side)
     gradient = scatter_sum(gradient_term, "kern", 1)
     resist = resist_block[None, :share_rows]

time: 97.8 us -> 99 us (1.012)
  matrix products: 20.8 us -> 22.8 us
    all_to_all x1, waiting for transfers between devices: 5.48 us -> 11.3 us  [shards(): gathered = lax.all_to_all(copies, 'kern', 0, 0, tiled=True)]
    all_to_all x1, waiting for transfers between devices: 11.4 us -> 6.13 us  [shards(): lax.all_to_all(pieces, 'kern', 0, 0, tiled=True)]
    dot_general x3, matrix products: 8.06 us -> 10.1 us  [banded(): jnp.einsum('acb,bji->acji', taps.transpose(1, 0, 2), select, preferred_el...]
  transfers between devices with their start and end apart: 5 -> 5, of which waited for: 3 -> 3; matrix products, arithmetic and copies ran while one was open for 14% -> 16% of each run, Pallas kernels for 0% -> 0%
where the time goes in v9:
time: 99 us; the launch traced here: 98.4 us
  starting transfers between devices  38.1 us (38%)
  waiting for transfers between devices  26.7 us (27%)
  matrix products  22.8 us (23%)
  local copies, waits for them, and re-layouts  5.27 us (5%)
  between operations  2.9 us (3%)
  other arithmetic  2.62 us (3%)
    ppermute x2, starting transfers between devices, halo_rows(): return lax.ppermute(rows, 'tile', pairs)  19.8 us
    all_to_all x1, waiting for transfers between devices, shards(): gathered = lax.all_to_all(copies, 'kern', 0, 0, tiled=True)  11.3 us
    all_to_all x1, starting transfers between devices, shards(): lax.all_to_all(pieces, 'kern', 0, 0, tiled=True)  10.5 us
    dot_general x3, matrix products, banded(): jnp.einsum('acb,bji->acji', taps.transpose(1, 0, 2), select, preferred_el...  10.1 us
    all_to_all x1, waiting for transfers between devices, scatter_sum(): pieces = lax.all_to_all(value, axis, dim, 0, tiled=True)  9.19 us
    all_to_all x1, waiting for transfers between devices, shards(): lax.all_to_all(pieces, 'kern', 0, 0, tiled=True)  6.13 us
    dot_general x4, matrix products, correlate_forward(): jnp.einsum('tapi,aqi->tpq', stacked, band, preferred_element_type=jnp.flo...  5.97 us
    all_to_all x1, starting transfers between devices, shards(): gathered = lax.all_to_all(copies, 'kern', 0, 0, tiled=True)  4.09 us
  transfers between devices with their start and end apart: 5, of which 3 were waited for; matrix products, arithmetic and copies ran while one was open for 16% of the time, Pallas kernels for 0%

profile of v9, /device:TPU:9, one launch (start us, length us, event | category | flops | bytes accessed | tf_op | source)
XLA Modules:
  0.0 98.4 jit_solution(11052857111864938058)
XLA Ops:
  0.6 0.9 copy.81
  1.6 0.7 fusion.96
  2.6 17.8 %collective-permute-start.1 = (bf16[1,96,128]{1,2,0:T(8,128)(2,1)S(1)}, bf16[1,96,128]{1,2,0:T(8,128)(2,1)S(1)}, u32[]{:S(2)}, u32[]{:S(2)}) collective-permute-start(bf16[1,96,128]{1,2,0:T(8,128)(2,1)S(1)} %pad_maximum_fusion.4), channel_id=1, source_target_pairs={{16,0},{32,16},{48,32},{64,48},{80,64},{96,80},{112,96},{128,112},... | collective-permute-start | bytes 73736 | tf_op jit(solution)/shard_map/ppermute | solution.py:61
  20.6 1.9 %collective-permute-start = (bf16[1,96,128]{1,2,0:T(8,128)(2,1)S(1)}, bf16[1,96,128]{1,2,0:T(8,128)(2,1)S(1)}, u32[]{:S(2)}, u32[]{:S(2)}) collective-permute-start(bf16[1,96,128]{1,2,0:T(8,128)(2,1)S(1)} %pad_maximum_fusion.3), channel_id=1, source_target_pairs={{0,16},{16,32},{32,48},{48,64},{64,80},{80,96},{96,112},{112,128},... | collective-permute-start | bytes 73736 | tf_op jit(solution)/shard_map/ppermute | solution.py:61
  22.5 0.7 iota_compare_fusion
  23.2 0.8 convert_bitcast_fusion.4
  24.7 2.4 %convert_bitcast_fusion.3 = bf16[65,128,192]{1,0,2:T(8,128)(2,1)S(1)} fusion(pred[65,128,192]{1,2,0:T(32,128)(4,1)S(1)} %iota_compare_fusion, bf16[1,1,65,65]{3,0,2,1:T(2,128)(2,1)S(1)} %get-tuple-element.16), kind=kOutput, calls=%fused_computation.17 | convolution fusion | flops 209264640 | bytes 4800770 | tf_op jit(solution)/shard_map/acb,bji->acji/dot_general | solution.py:17
  27.1 2.4 %convert_bitcast_fusion.2 = bf16[65,128,192]{1,0,2:T(8,128)(2,1)S(1)} fusion(pred[65,128,192]{1,2,0:T(32,128)(4,1)S(1)} %iota_compare_fusion, bf16[1,1,65,65]{3,0,2,1:T(2,128)(2,1)S(1)} %get-tuple-element.17), kind=kOutput, calls=%fused_computation.16 | convolution fusion | flops 209264640 | bytes 4800770 | tf_op jit(solution)/shard_map/acb,bji->acji/dot_general | solution.py:17
  29.5 1.1 %fusion.48 = f32[1,1,64,128]{3,2,0,1:T(8,128)S(1)} fusion(bf16[65,128,192]{1,0,2:T(8,128)(2,1)S(1)} %convert_bitcast_fusion.3, bf16[65,64,192]{2,0,1:T(8,128)(2,1)S(1)} %convert_bitcast_fusion.4), kind=kOutput, calls=%fused_computation.38 | convolution fusion | flops 204472320 | bytes 4825088 | tf_op jit(solution)/shard_map/tapi,aqi->tpq/dot_general | solution.py:43
  30.7 1.1 %fusion.53 = f32[1,1,64,128]{3,2,0,1:T(8,128)S(1)} fusion(bf16[65,128,192]{1,0,2:T(8,128)(2,1)S(1)} %convert_bitcast_fusion.2, bf16[65,64,192]{2,0,1:T(8,128)(2,1)S(1)} %convert_bitcast_fusion.4), kind=kOutput, calls=%fused_computation.39 | convolution fusion | flops 204472320 | bytes 4825088 | tf_op jit(solution)/shard_map/tapi,aqi->tpq/dot_general | solution.py:43
  34.1 1.5 %convert_bitcast_fusion.1 = bf16[2,65,64,192]{3,1,2,0:T(8,128)(2,1)S(1)} fusion(bf16[1,64,128]{1,2,0:T(8,128)(2,1)S(1)} %multiply_convert_fusion.1, bf16[1,64,128]{1,2,0:T(8,128)(2,1)S(1)} %get-tuple-element.20, bf16[1,64,128]{1,2,0:T(8,128)(2,1)S(1)} %get-tuple-element.21, bf16[1,64,128]{1,2,0:T(8,128)(2,1)S(1)} %multiply_convert_fusion.2), kind=kOutput, calls=%fused_computation.10 | convolution fusion | flops 412344320 | bytes 3260416 | tf_op jit(solution)/shard_map/apr,tri->tapi/dot_general | solution.py:39
  36.1 1.8 %fusion.38 = f32[2,1,64,128]{3,2,0,1:T(8,128)S(1)} fusion(bf16[65,128,192]{1,0,2:T(8,128)(2,1)S(1)} %copy-done.4, bf16[2,65,64,192]{3,1,2,0:T(8,128)(2,1)S(1)} %convert_bitcast_fusion.1), kind=kOutput, calls=%fused_computation.36 | convolution fusion | flops 408944640 | bytes 6455296 | tf_op jit(solution)/shard_map/tapi,aqi->tpq/dot_general | solution.py:43
  38.1 2.0 %fusion.43 = f32[2,1,64,128]{3,2,0,1:T(8,128)S(1)} fusion(bf16[65,128,192]{1,0,2:T(8,128)(2,1)S(1)} %copy-done.6, bf16[2,65,64,192]{3,1,2,0:T(8,128)(2,1)S(1)} %convert_bitcast_fusion.1), kind=kOutput, calls=%fused_computation.37 | convolution fusion | flops 408944640 | bytes 6455296 | tf_op jit(solution)/shard_map/tapi,aqi->tpq/dot_general | solution.py:43
  40.6 0.7 pad_maximum_fusion.1
  41.2 10.5 %all-to-all-start = ((f32[16,12,128]{2,1,0:T(8,128)}), f32[16,12,128]{2,1,0:T(8,128)S(1)}, u32[]{:S(2)}, u32[]{:S(2)}) async-start(f32[16,12,128]{2,1,0:T(8,128)} %pad_maximum_fusion.1), calls=%async_computation | async-start | bytes 262144 | tf_op jit(solution)/shard_map/all_to_all | solution.py:130
  51.7 5.3 %fusion.7 = bf16[65,2,128,192]{2,0,3,1:T(8,128)(2,1)} fusion(pred[65,128,192]{1,2,0:T(32,128)(4,1)S(1)} %iota_compare_fusion, bf16[65,2,65,1]{2,1,0,3:T(2,128)(2,1)S(1)} %bitcast.129), kind=kOutput, calls=%fused_computation.9 | convolution fusion | flops 418529280 | bytes 8004100 | tf_op jit(solution)/shard_map/acb,bji->acji/dot_general | solution.py:17
  57.1 6.1 %all-to-all-done = f32[16,12,128]{2,1,0:T(8,128)S(1)} async-done(((f32[16,12,128]{2,1,0:T(8,128)}), f32[16,12,128]{2,1,0:T(8,128)S(1)}, u32[]{:S(2)}, u32[]{:S(2)}) %all-to-all-start) | async-done | bytes 98336 | tf_op jit(solution)/shard_map/all_to_all | solution.py:130
  63.2 0.7 broadcast_in_dim.6
  63.9 4.1 %all-to-all-start.1 = ((f32[16,12,128]{2,1,0:T(8,128)}), f32[16,12,128]{2,1,0:T(8,128)S(1)}, u32[]{:S(2)}, u32[]{:S(2)}) async-start(f32[16,12,128]{2,1,0:T(8,128)} %broadcast_in_dim.6), calls=%async_computation.1 | async-start | bytes 262144 | tf_op jit(solution)/shard_map/all_to_all | solution.py:147
  68.1 11.3 %all-to-all-done.1 = f32[16,12,128]{2,1,0:T(8,128)S(1)} async-done(((f32[16,12,128]{2,1,0:T(8,128)}), f32[16,12,128]{2,1,0:T(8,128)S(1)}, u32[]{:S(2)}, u32[]{:S(2)}) %all-to-all-start.1) | async-done | bytes 98336 | tf_op jit(solution)/shard_map/all_to_all | solution.py:147
  79.5 2.0 %convert_bitcast_fusion = bf16[65,2,128,192]{2,3,0,1:T(8,128)(2,1)S(1)} fusion(bf16[1,2,192,128]{3,2,0,1:T(8,128)(2,1)S(1)} %multiply_convert_fusion), kind=kOutput, calls=%fused_computation.5 | convolution fusion | flops 1233223680 | bytes 6488064 | tf_op jit(solution)/shard_map/apr,tcri->tacpi/dot_general | solution.py:51
  81.7 2.5 %fusion.2 = f32[128,128,1,1]{1,0,3,2:T(8,128)} fusion(bf16[65,2,128,192]{2,0,3,1:T(8,128)(2,1)S(1)} %bitcast.124, bf16[65,2,128,192]{2,3,0,1:T(8,128)(2,1)S(1)} %convert_bitcast_fusion), kind=kOutput, calls=%fused_computation.2 | convolution fusion | flops 817889280 | bytes 12845056 | tf_op jit(solution)/shard_map/tacpi,acqi->tpq/dot_general | solution.py:54
  84.2 3.7 %all-to-all-start.2 = ((f32[1,128,128]{2,0,1:T(1,128)}), f32[1,128,128]{2,0,1:T(1,128)S(1)}, u32[]{:S(2)}, u32[]{:S(2)}) async-start(f32[1,128,128]{2,0,1:T(1,128)} %bitcast.55), calls=%async_computation.2 | async-start | bytes 131072 | tf_op jit(solution)/shard_map/all_to_all | solution.py:24
  88.5 9.2 %all-to-all-done.2 = f32[1,128,128]{2,0,1:T(1,128)S(1)} async-done(((f32[1,128,128]{2,0,1:T(1,128)}), f32[1,128,128]{2,0,1:T(1,128)S(1)}, u32[]{:S(2)}, u32[]{:S(2)}) %all-to-all-start.2) | async-done | bytes 65568 | tf_op jit(solution)/shard_map/all_to_all | solution.py:24
  (54 shorter events, 4.3 us)
Async XLA Ops:
  0.6 23.4 %copy-start.2 = (s32[1,8]{1,0:T(1,128)S(1)}, s32[1,8]{1,0:T(1,128)}, u32[]{:S(2)}) copy-start(s32[1,8]{1,0:T(1,128)} %param.9) | copy-start | bytes 100
  0.6 24.0 %copy-start = (bf16[2,1,65,65]{3,0,2,1:T(2,128)(2,1)S(1)}, bf16[2,1,65,65]{3,0,2,1:T(2,128)(2,1)}, u32[]{:S(2)}) copy-start(bf16[2,1,65,65]{3,0,2,1:T(2,128)(2,1)} %param.6) | copy-start | bytes 50704
  2.6 31.4 %collective-permute-start.1 = (bf16[1,96,128]{1,2,0:T(8,128)(2,1)S(1)}, bf16[1,96,128]{1,2,0:T(8,128)(2,1)S(1)}, u32[]{:S(2)}, u32[]{:S(2)}) collective-permute-start(bf16[1,96,128]{1,2,0:T(8,128)(2,1)S(1)} %pad_maximum_fusion.4), channel_id=1, source_target_pairs={{16,0},{32,16},{48,32},{64,48},{80,64},{96,80},{112,96},{128,112},... | collective-permute-start | bytes 73736 | tf_op jit(solution)/shard_map/ppermute | solution.py:61
  20.6 13.4 %collective-permute-start = (bf16[1,96,128]{1,2,0:T(8,128)(2,1)S(1)}, bf16[1,96,128]{1,2,0:T(8,128)(2,1)S(1)}, u32[]{:S(2)}, u32[]{:S(2)}) collective-permute-start(bf16[1,96,128]{1,2,0:T(8,128)(2,1)S(1)} %pad_maximum_fusion.3), channel_id=1, source_target_pairs={{0,16},{16,32},{32,48},{48,64},{64,80},{80,96},{96,112},{112,128},... | collective-permute-start | bytes 73736 | tf_op jit(solution)/shard_map/ppermute | solution.py:61
  27.1 3.5 %copy-start.3 = (bf16[65,128,192]{1,0,2:T(8,128)(2,1)}, bf16[65,128,192]{1,0,2:T(8,128)(2,1)S(1)}, u32[]{:S(2)}) copy-start(bf16[65,128,192]{1,0,2:T(8,128)(2,1)S(1)} %convert_bitcast_fusion.3) | copy-start | bytes 9584644
  29.5 2.3 %copy-start.5 = (bf16[65,128,192]{1,0,2:T(8,128)(2,1)}, bf16[65,128,192]{1,0,2:T(8,128)(2,1)S(1)}, u32[]{:S(2)}) copy-start(bf16[65,128,192]{1,0,2:T(8,128)(2,1)S(1)} %convert_bitcast_fusion.2) | copy-start | bytes 9584644
  34.1 2.0 %copy-start.4 = (bf16[65,128,192]{1,0,2:T(8,128)(2,1)S(1)}, bf16[65,128,192]{1,0,2:T(8,128)(2,1)}, u32[]{:S(2)}) copy-start(bf16[65,128,192]{1,0,2:T(8,128)(2,1)} %copy-done.3) | copy-start | bytes 9584644
  36.1 2.0 %copy-start.6 = (bf16[65,128,192]{1,0,2:T(8,128)(2,1)S(1)}, bf16[65,128,192]{1,0,2:T(8,128)(2,1)}, u32[]{:S(2)}) copy-start(bf16[65,128,192]{1,0,2:T(8,128)(2,1)} %copy-done.5) | copy-start | bytes 9584644
  38.1 2.4 %copy-start.1 = (bf16[1,128,128]{2,1,0:T(8,128)(2,1)S(1)}, bf16[1,128,128]{2,1,0:T(8,128)(2,1)}, u32[]{:S(2)}) copy-start(bf16[1,128,128]{2,1,0:T(8,128)(2,1)} %param.8) | copy-start | bytes 98308
  41.2 22.0 %all-to-all-start = ((f32[16,12,128]{2,1,0:T(8,128)}), f32[16,12,128]{2,1,0:T(8,128)S(1)}, u32[]{:S(2)}, u32[]{:S(2)}) async-start(f32[16,12,128]{2,1,0:T(8,128)} %pad_maximum_fusion.1), calls=%async_computation | async-start | bytes 262144 | tf_op jit(solution)/shard_map/all_to_all | solution.py:130
  63.2 18.3 %slice-start = ((s8[7077888]{0:T(1024)(128)(4,1)}), s8[2883584]{0:T(1024)(128)(4,1)S(1)}, s32[]{:S(2)}) async-start(s8[7077888]{0:T(1024)(128)(4,1)} %bitcast.123), calls=%async_computation.3 | async-start | bytes 5767168
  63.9 15.5 %all-to-all-start.1 = ((f32[16,12,128]{2,1,0:T(8,128)}), f32[16,12,128]{2,1,0:T(8,128)S(1)}, u32[]{:S(2)}, u32[]{:S(2)}) async-start(f32[16,12,128]{2,1,0:T(8,128)} %broadcast_in_dim.6), calls=%async_computation.1 | async-start | bytes 262144 | tf_op jit(solution)/shard_map/all_to_all | solution.py:147
  79.5 2.2 %slice-start.1 = ((s8[7077888]{0:T(1024)(128)(4,1)}), s8[4194304]{0:T(1024)(128)(4,1)S(1)}, s32[]{:S(2)}) async-start(s8[7077888]{0:T(1024)(128)(4,1)} %bitcast.123), calls=%async_computation.4 | async-start | bytes 8388608
  84.2 13.5 %all-to-all-start.2 = ((f32[1,128,128]{2,0,1:T(1,128)}), f32[1,128,128]{2,0,1:T(1,128)S(1)}, u32[]{:S(2)}, u32[]{:S(2)}) async-start(f32[1,128,128]{2,0,1:T(1,128)} %bitcast.55), calls=%async_computation.2 | async-start | bytes 131072 | tf_op jit(solution)/shard_map/all_to_all | solution.py:24
